TPU v7x, 128 devices: a whole 4x4x4 slice. The times are simulated.
128 devices in a mesh: blk: 32 (over z, x_hi, y), rep: 4 (over x_lo, core).
Axes of the slice: x: 4 (x_hi: 2, x_lo: 2; x = x_hi * 2 + x_lo), y: 4, z: 4, core: 2. Of those that a mesh axis runs over, the one named last changes fastest.
Arguments:
- node_features: bfloat16 [49152, 512], P('blk', 'rep'), may hold values from -6 to 6
- weight: bfloat16 [512, 512], replicated, may hold values from -0.25 to 0.25
- cotangent: bfloat16 [49152, 512], P(('blk', 'rep')), may hold values from -6 to 6
- adjacency_tiles: bfloat16 [384, 56, 128, 128], P('blk'), as said below
- block_cols: int32 [384, 56], P('blk'), may hold values from 0 to 383, as said below
- block_perm: int32 [384], replicated, may hold values from 0 to 383, as said below
Outputs:
- activated: bfloat16 [49152, 512], P(('blk', 'rep'))
- feature_grad: bfloat16 [49152, 512], P('blk', 'rep')
- weight_grad: float32 [512, 512], P('rep')
Inputs may be any that keep to these rules, and one draw needn't show every extreme that they name: Each row of block_cols names 56 different initial node blocks; if the row at position p (initial block q, block_perm[q] = p) names block c, then the row at position block_perm[c] names q. `block_perm`: each initial node block appears exactly once. `adjacency_tiles`: A is symmetric: the tile at row block p for column block c is the transpose of the tile at row block c for column block p.
All inputs are finite; a program needn't handle non-finite values.
Results may differ from a plain program's by a relative error of at most 0.0065.
Values may be sent and summed in bfloat16 or wider, within the bound.
No kernel may reach another device: no remote copies, remote signals or barrier semaphores. Data moves between devices by JAX's collectives and lax.ppermute only.
A program may use at most 128 MiB of HBM per device.

v0:
```python
import math

import jax
import jax.numpy as jnp
from jax import lax
from jax.sharding import PartitionSpec as P


def column_positions(block_cols, block_perm):
    numbers = jnp.arange(block_perm.shape[0], dtype=jnp.int32)
    matches = block_cols[:, :, None] == numbers[None, None, :]
    return jnp.sum(jnp.where(matches, block_perm[None, None, :], 0), axis=-1)


def block_product(adjacency_tiles, positions, gathered):
    block_rows = adjacency_tiles.shape[2]
    blocks = gathered.reshape(-1, block_rows, gathered.shape[1])
    picked = blocks[positions]
    result = jnp.einsum(
        "pkab,pkbf->paf", adjacency_tiles, picked, preferred_element_type=jnp.float32
    )
    return result.reshape(-1, gathered.shape[1])


def local(node_features, weight, cotangent, adjacency_tiles, block_cols, block_perm):
    feat_dev = node_features.shape[1]
    column_start = lax.axis_index("rep") * feat_dev
    weight_slice = lax.dynamic_slice_in_dim(weight, column_start, feat_dev, 0)
    positions = column_positions(block_cols, block_perm)
    gathered = lax.all_gather(node_features, "blk", axis=0, tiled=True)
    aggregate = block_product(adjacency_tiles, positions, gathered).astype(jnp.bfloat16)
    preact = lax.psum_scatter(
        jnp.dot(aggregate, weight_slice, preferred_element_type=jnp.float32),
        "rep",
        scatter_dimension=0,
        tiled=True,
    )
    gating = jax.nn.sigmoid(preact)
    activated = (preact * gating).astype(jnp.bfloat16)
    slopes = gating * (1.0 + preact * (1.0 - gating))
    grad_pre = (cotangent.astype(jnp.float32) * slopes).astype(jnp.bfloat16)
    group_grad = lax.all_gather(grad_pre, "rep", axis=0, tiled=True)
    grad_agg = lax.dot_general(
        group_grad, weight_slice, (((1,), (1,)), ((), ())), preferred_element_type=jnp.float32
    ).astype(jnp.bfloat16)
    weight_part = lax.dot_general(
        aggregate, group_grad, (((0,), (0,)), ((), ())), preferred_element_type=jnp.float32
    )
    node_total = node_features.shape[0] * lax.axis_size("blk")
    weight_grad = lax.psum(weight_part, "blk") * (1.0 / math.sqrt(node_total))
    gathered_grad = lax.all_gather(grad_agg, "blk", axis=0, tiled=True)
    feature_grad = block_product(adjacency_tiles, positions, gathered_grad).astype(jnp.bfloat16)
    return (activated, feature_grad, weight_grad)


def solution(mesh):
    return jax.shard_map(
        local,
        mesh=mesh,
        in_specs=(
            P("blk", "rep"),
            P(),
            P(("blk", "rep"), None),
            P("blk", None, None, None),
            P("blk", None),
            P(),
        ),
        out_specs=(P(("blk", "rep"), None), P("blk", "rep"), P("rep", None)),
        check_vma=False,
    )
```

profile of v0, /device:TPU:1, one launch (start us, length us, event | category | flops | bytes accessed | tf_op | source)
XLA Modules:
  0.0 784.5 jit_solution(18412645651205708438)
XLA Ops:
  7.2 0.0 copy-start
  7.2 0.0 all-gather.4.cloned.1.call-start
  7.2 0.7 all-gather.4.cloned.1.call-update
  7.9 0.0 reduce-scatter.2.cloned.1.call-start
  8.0 1.1 select_reduce_fusion
  9.1 0.1 reshape.35
  9.2 134.0 %all-gather.4.cloned.1.call-done = bf16[49152,128]{1,0:T(8,128)(2,1)} async-done(((bf16[1536,128]{1,0:T(8,128)(2,1)}), bf16[49152,128]{1,0:T(8,128)(2,1)}) %all-gather.4.cloned.1.call-update) | async-done | bytes 12582928 | tf_op jit(solution)/shard_map/all_gather | solution.py:30
  143.2 22.9 %gather_fusion = bf16[672,128,128]{2,1,0:T(8,128)(2,1)} fusion(bf16[384,128,128]{2,1,0:T(8,128)(2,1)} %bitcast.34, s32[1024]{0:T(1024)S(1)} %pad_clamp_fusion), kind=kCustom, calls=%fused_computation | custom fusion | bytes 44042880 | tf_op jit(solution)/shard_map/gather | solution.py:18
  166.1 0.0 copy-start.1
  166.1 16.7 %fusion = bf16[12,128,128]{1,2,0:T(8,128)(2,1)S(1)} fusion(bf16[12,56,128,128]{3,2,1,0:T(8,128)(2,1)} %param.9, bf16[12,56,128,128]{3,2,1,0:T(8,128)(2,1)} %bitcast.33), kind=kOutput, calls=%fused_computation.5 | convolution fusion | flops 2818768896 | bytes 44433408 | tf_op jit(solution)/shard_map/pkab,pkbf->paf/dot_general | solution.py:19
  182.7 0.0 copy-done
  182.7 2.2 fusion.3
  184.9 0.0 reduce-scatter.2.cloned.1.call-update
  185.0 0.0 all-gather.6.cloned.1.call-start
  185.0 35.7 %reduce-scatter.2.cloned.1.call-done = f32[384,512]{1,0:T(8,128)} async-done(((f32[1536,512]{1,0:T(8,128)}), f32[384,512]{1,0:T(8,128)}) %reduce-scatter.2.cloned.1.call-update) | async-done | bytes 786448 | tf_op jit(solution)/shard_map/reduce_scatter | solution.py:32
  220.7 0.0 copy-done.1
  220.7 2.4 multiply_convert_fusion
  223.1 0.0 all-gather.6.cloned.1.call-update
  223.1 0.0 all-reduce.2.cloned.1.call-start
  223.2 25.9 %all-gather.6.cloned.1.call-done = bf16[1536,512]{1,0:T(8,128)(2,1)} async-done(((bf16[384,512]{1,0:T(8,128)(2,1)}), bf16[1536,512]{1,0:T(8,128)(2,1)}) %all-gather.6.cloned.1.call-update) | async-done | bytes 1572880 | tf_op jit(solution)/shard_map/all_gather | solution.py:42
  249.1 2.5 fusion.7
  251.6 0.0 all-reduce.2.cloned.1.call-update
  251.7 0.2 all-gather.8.cloned.1.call-start
  251.9 2.7 convolution_convert_fusion
  254.6 0.0 all-gather.8.cloned.1.call-update
  254.7 329.5 %all-reduce.2.cloned.1.call-done = f32[128,512]{1,0:T(8,128)} async-done(((f32[128,512]{1,0:T(8,128)}), f32[128,512]{1,0:T(8,128)}) %all-reduce.2.cloned.1.call-update) | async-done | bytes 262160 | tf_op jit(solution)/shard_map/psum | solution.py:50
  584.2 1.7 broadcast_multiply_fusion
  585.9 151.9 %all-gather.8.cloned.1.call-done = bf16[49152,128]{1,0:T(8,128)(2,1)} async-done(((bf16[1536,128]{1,0:T(8,128)(2,1)}), bf16[49152,128]{1,0:T(8,128)(2,1)}) %all-gather.8.cloned.1.call-update) | async-done | bytes 12582928 | tf_op jit(solution)/shard_map/all_gather | solution.py:51
  737.8 22.9 %gather_fusion.1 = bf16[672,128,128]{2,1,0:T(8,128)(2,1)} fusion(bf16[384,128,128]{2,1,0:T(8,128)(2,1)} %bitcast.35, s32[1024]{0:T(1024)S(1)} %pad_clamp_fusion), kind=kCustom, calls=%fused_computation.1 | custom fusion | bytes 44042880 | tf_op jit(solution)/shard_map/gather | solution.py:18
  760.7 17.3 %fusion.1 = bf16[12,128,128]{1,2,0:T(8,128)(2,1)} fusion(bf16[12,56,128,128]{3,2,1,0:T(8,128)(2,1)} %param.9, bf16[12,56,128,128]{3,2,1,0:T(8,128)(2,1)} %bitcast.32), kind=kOutput, calls=%fused_computation.6 | convolution fusion | flops 2818768896 | bytes 44433408 | tf_op jit(solution)/shard_map/pkab,pkbf->paf/dot_general | solution.py:19
  (2 shorter events, 0.0 us)
Async XLA Ops:
  7.2 175.6 %copy-start = (bf16[512,512]{1,0:T(8,128)(2,1)S(1)}, bf16[512,512]{1,0:T(8,128)(2,1)}, u32[]{:S(2)}) copy-start(bf16[512,512]{1,0:T(8,128)(2,1)} %param.7) | copy-start | bytes 1572868
  7.2 136.0 %all-gather.4.cloned.1.call-start = ((), (), s32[]{:S(2)}) async-start(), calls=%async_computation.1 | async-start | bytes 12976128 | tf_op jit(solution)/shard_map/all_gather | solution.py:30
  7.9 212.8 %reduce-scatter.2.cloned.1.call-start = ((), (), s32[]{:S(2)}) async-start(), calls=%async_computation.2 | async-start | bytes 3932160 | tf_op jit(solution)/shard_map/reduce_scatter | solution.py:32
  166.1 54.7 %copy-start.1 = (bf16[384,512]{1,0:T(8,128)(2,1)S(1)}, bf16[384,512]{1,0:T(8,128)(2,1)}, u32[]{:S(2)}) copy-start(bf16[384,512]{1,0:T(8,128)(2,1)} %param.8) | copy-start | bytes 1179652
  185.0 64.1 %all-gather.6.cloned.1.call-start = ((), (), s32[]{:S(2)}) async-start(), calls=%async_computation.3 | async-start | bytes 1966080 | tf_op jit(solution)/shard_map/all_gather | solution.py:42
  223.1 361.1 %all-reduce.2.cloned.1.call-start = ((), (), s32[]{:S(2)}) async-start(), calls=%async_computation.5 | async-start | bytes 524288 | tf_op jit(solution)/shard_map/psum | solution.py:50
  251.7 486.2 %all-gather.8.cloned.1.call-start = ((), (), s32[]{:S(2)}) async-start(), calls=%async_computation.4 | async-start | bytes 12976128 | tf_op jit(solution)/shard_map/all_gather | solution.py:51
Sparse Core Ops, SparseCore 0:
  11.0 132.1 all-gather.3
  185.1 35.6 reduce-scatter.1
  223.3 25.8 all-gather.5
  252.0 332.1 all-reduce.1
  587.6 150.1 all-gather.7
where the time goes:
time: 785 us
  waiting for transfers between devices  678 us (86%)
  local copies, waits for them, and re-layouts  45.8 us (6%)
  matrix products  41.5 us (5%)
  between operations  13.8 us (2%)
    psum x1, waiting for transfers between devices, local(): weight_grad = lax.psum(weight_part, 'blk') * (1.0 / math.sqrt(node_total))  330 us
    all_gather x1, waiting for transfers between devices, local(): gathered_grad = lax.all_gather(grad_agg, 'blk', axis=0, tiled=True)  152 us
    all_gather x1, waiting for transfers between devices, local(): gathered = lax.all_gather(node_features, 'blk', axis=0, tiled=True)  134 us
    gather x2, local copies, waits for them, and re-layouts, block_product(): picked = blocks[positions]  45.7 us
    reduce_scatter x1, waiting for transfers between devices, local(): lax.psum_scatter(jnp.dot(aggregate, weight_slice, preferred_element_type=...  35.7 us
    dot_general x2, matrix products, block_product(): jnp.einsum('pkab,pkbf->paf', adjacency_tiles, picked, preferred_element_t...  34 us
    all_gather x1, waiting for transfers between devices, local(): group_grad = lax.all_gather(grad_pre, 'rep', axis=0, tiled=True)  25.9 us
  transfers between devices with their start and end apart: 5, of which 5 were waited for; matrix products, arithmetic and copies ran while one was open for 1% of the time, Pallas kernels for 0%

commit v1 on v0

--- a/solution.py
+++ b/solution.py
@@ -22,34 +22,59 @@
     return result.reshape(-1, gathered.shape[1])
 
 
+def xor_pairs(size, bit):
+    return [(i, i ^ bit) for i in range(size)]
+
+
+def butterfly_sum(x, axis):
+    size = lax.axis_size(axis)
+    bit = 1
+    while bit < size:
+        x = x + lax.ppermute(x, axis, xor_pairs(size, bit))
+        bit *= 2
+    return x
+
+
+def halving_scatter(parts, axis):
+    size = lax.axis_size(axis)
+    me = lax.axis_index(axis)
+    bit = size // 2
+    while bit >= 1:
+        half = parts.shape[0] // 2
+        lo, hi = parts[:half], parts[half:]
+        mine_hi = (me & bit) != 0
+        keep = jnp.where(mine_hi, hi, lo)
+        send = jnp.where(mine_hi, lo, hi)
+        parts = keep + lax.ppermute(send, axis, xor_pairs(size, bit))
+        bit //= 2
+    return parts[0]
+
+
 def local(node_features, weight, cotangent, adjacency_tiles, block_cols, block_perm):
     feat_dev = node_features.shape[1]
-    column_start = lax.axis_index("rep") * feat_dev
-    weight_slice = lax.dynamic_slice_in_dim(weight, column_start, feat_dev, 0)
+    n_rep = lax.axis_size("rep")
+    f_all = weight.shape[0]
+    w_split = weight.reshape(n_rep, feat_dev, f_all)
     positions = column_positions(block_cols, block_perm)
     gathered = lax.all_gather(node_features, "blk", axis=0, tiled=True)
     aggregate = block_product(adjacency_tiles, positions, gathered).astype(jnp.bfloat16)
-    preact = lax.psum_scatter(
-        jnp.dot(aggregate, weight_slice, preferred_element_type=jnp.float32),
-        "rep",
-        scatter_dimension=0,
-        tiled=True,
-    )
+    rows = aggregate.shape[0] // n_rep
+    agg_rows = lax.all_to_all(aggregate, "rep", 0, 0, tiled=True).reshape(n_rep, rows, feat_dev)
+    preact = jnp.einsum("irf,ifo->ro", agg_rows, w_split, preferred_element_type=jnp.float32)
     gating = jax.nn.sigmoid(preact)
     activated = (preact * gating).astype(jnp.bfloat16)
     slopes = gating * (1.0 + preact * (1.0 - gating))
     grad_pre = (cotangent.astype(jnp.float32) * slopes).astype(jnp.bfloat16)
-    group_grad = lax.all_gather(grad_pre, "rep", axis=0, tiled=True)
-    grad_agg = lax.dot_general(
-        group_grad, weight_slice, (((1,), (1,)), ((), ())), preferred_element_type=jnp.float32
+    grad_split = jnp.einsum(
+        "rf,jof->jro", grad_pre, w_split, preferred_element_type=jnp.float32
     ).astype(jnp.bfloat16)
-    weight_part = lax.dot_general(
-        aggregate, group_grad, (((0,), (0,)), ((), ())), preferred_element_type=jnp.float32
-    )
-    node_total = node_features.shape[0] * lax.axis_size("blk")
-    weight_grad = lax.psum(weight_part, "blk") * (1.0 / math.sqrt(node_total))
+    grad_agg = lax.all_to_all(grad_split.reshape(n_rep * rows, feat_dev), "rep", 0, 0, tiled=True)
     gathered_grad = lax.all_gather(grad_agg, "blk", axis=0, tiled=True)
     feature_grad = block_product(adjacency_tiles, positions, gathered_grad).astype(jnp.bfloat16)
+    weight_part = jnp.einsum("irf,ro->ifo", agg_rows, grad_pre, preferred_element_type=jnp.float32)
+    weight_rows = halving_scatter(weight_part, "rep")
+    node_total = node_features.shape[0] * lax.axis_size("blk")
+    weight_grad = butterfly_sum(weight_rows, "blk") * (1.0 / math.sqrt(node_total))
     return (activated, feature_grad, weight_grad)
 
 

time: 785 us -> 391 us (0.50)
  waiting for transfers between devices: 678 us -> 261 us
  blocking collectives: 0 us -> 20.6 us
  starting transfers between devices: 0.38 us -> 10.6 us
    psum x1 -> x0, waiting for transfers between devices: 330 us -> none  [local(): weight_grad = lax.psum(weight_part, 'blk') * (1.0 / math.sqrt(node_total))]
    all_gather x1, waiting for transfers between devices: 152 us -> 66.9 us  [local(): gathered_grad = lax.all_gather(grad_agg, 'blk', axis=0, tiled=True)]
    ppermute x0 -> x7, waiting for transfers between devices: none -> 59.7 us  [the longest x5 45.5 us: butterfly_sum(): x = x + lax.ppermute(x, axis, xor_pairs(size, bit))]
    reduce_scatter x1 -> x0, waiting for transfers between devices: 35.7 us -> none  [local(): lax.psum_scatter(jnp.dot(aggregate, weight_slice, preferred_element_type=...]
    all_gather x1 -> x0, waiting for transfers between devices: 25.9 us -> none  [local(): group_grad = lax.all_gather(grad_pre, 'rep', axis=0, tiled=True)]
    all_to_all x0 -> x2, blocking collectives: none -> 20.6 us  [the longest x1 10.5 us: local(): lax.all_to_all(grad_split.reshape(n_rep * rows, feat_dev), 'rep', 0, 0, t...]
    ppermute x0 -> x7, starting transfers between devices: none -> 10.6 us  [the longest x5 6.26 us: butterfly_sum(): x = x + lax.ppermute(x, axis, xor_pairs(size, bit))]
  transfers between devices with their start and end apart: 5 -> 9, of which waited for: 5 -> 9; matrix products, arithmetic and copies ran while one was open for 1% -> 1% of each run, Pallas kernels for 0% -> 0%
where the time goes in v1:
time: 391 us
  waiting for transfers between devices  261 us (67%)
  local copies, waits for them, and re-layouts  45.8 us (12%)
  matrix products  36.2 us (9%)
  blocking collectives  20.6 us (5%)
  between operations  14.2 us (4%)
  starting transfers between devices  10.6 us (3%)
    all_gather x1, waiting for transfers between devices, local(): gathered = lax.all_gather(node_features, 'blk', axis=0, tiled=True)  134 us
    all_gather x1, waiting for transfers between devices, local(): gathered_grad = lax.all_gather(grad_agg, 'blk', axis=0, tiled=True)  66.9 us
    gather x2, local copies, waits for them, and re-layouts, block_product(): picked = blocks[positions]  45.7 us
    ppermute x5, waiting for transfers between devices, butterfly_sum(): x = x + lax.ppermute(x, axis, xor_pairs(size, bit))  45.5 us
    dot_general x2, matrix products, block_product(): jnp.einsum('pkab,pkbf->paf', adjacency_tiles, picked, preferred_element_t...  34 us
    ppermute x2, waiting for transfers between devices, halving_scatter(): parts = keep + lax.ppermute(send, axis, xor_pairs(size, bit))  14.2 us
    all_to_all x1, blocking collectives, local(): lax.all_to_all(grad_split.reshape(n_rep * rows, feat_dev), 'rep', 0, 0, t...  10.5 us
    all_to_all x1, blocking collectives, local(): lax.all_to_all(aggregate, 'rep', 0, 0, tiled=True)  10.2 us
  transfers between devices with their start and end apart: 9, of which 9 were waited for; matrix products, arithmetic and copies ran while one was open for 1% of the time, Pallas kernels for 0%

profile of v1, /device:TPU:1, one launch (start us, length us, event | category | flops | bytes accessed | tf_op | source)
XLA Modules:
  0.0 391.1 jit_solution(861940744964411366)
XLA Ops:
  7.2 0.0 copy-start
  7.2 0.0 all-gather.3.cloned.1.call-start
  7.2 0.7 all-gather.3.cloned.1.call-update
  7.9 0.0 all-gather.5.cloned.1.call-start
  8.0 1.1 select_reduce_fusion
  9.1 0.1 reshape.48
  9.2 134.0 %all-gather.3.cloned.1.call-done = bf16[49152,128]{1,0:T(8,128)(2,1)} async-done(((bf16[1536,128]{1,0:T(8,128)(2,1)}), bf16[49152,128]{1,0:T(8,128)(2,1)}) %all-gather.3.cloned.1.call-update) | async-done | bytes 12582928 | tf_op jit(solution)/shard_map/all_gather | solution.py:59
  143.2 22.9 %gather_fusion = bf16[672,128,128]{2,1,0:T(8,128)(2,1)} fusion(bf16[384,128,128]{2,1,0:T(8,128)(2,1)} %bitcast.50, s32[1024]{0:T(1024)S(1)} %pad_clamp_fusion), kind=kCustom, calls=%fused_computation | custom fusion | bytes 44042880 | tf_op jit(solution)/shard_map/gather | solution.py:18
  166.1 0.0 copy-start.1
  166.1 16.7 %fusion = bf16[12,128,128]{1,2,0:T(8,128)(2,1)S(1)} fusion(bf16[12,56,128,128]{3,2,1,0:T(8,128)(2,1)} %param.9, bf16[12,56,128,128]{3,2,1,0:T(8,128)(2,1)} %bitcast.48), kind=kOutput, calls=%fused_computation.6 | convolution fusion | flops 2818768896 | bytes 44433408 | tf_op jit(solution)/shard_map/pkab,pkbf->paf/dot_general | solution.py:19
  182.7 10.2 %all_to_all.15 = bf16[4,384,128]{2,1,0:T(8,128)(2,1)S(1)} all-to-all(bf16[4,384,128]{2,1,0:T(8,128)(2,1)S(1)} %bitcast.51), channel_id=1, replica_groups=mesh['blk'=32,'rep'=4] {'rep'}, dimensions={0} | all-to-all | bytes 786432 | tf_op jit(solution)/shard_map/all_to_all | solution.py:62
  192.9 0.0 copy-done
  192.9 0.0 copy-done.1
  192.9 1.4 multiply_convert_fusion
  194.3 0.4 fusion.2
  194.7 10.5 %all_to_all.16 = bf16[4,384,128]{2,1,0:T(8,128)(2,1)} all-to-all(bf16[4,384,128]{2,1,0:T(8,128)(2,1)S(1)} %fusion.2), channel_id=1, replica_groups=mesh['blk'=32,'rep'=4] {'rep'}, dimensions={0} | all-to-all | bytes 786432 | tf_op jit(solution)/shard_map/all_to_all | solution.py:71
  205.2 0.0 all-gather.5.cloned.1.call-update
  205.2 0.5 fusion.3
  205.7 0.1 slice_select_fusion
  205.7 0.6 collective-permute-start
  206.4 13.0 %collective-permute-done = f32[2,128,512]{2,1,0:T(8,128)S(1)} collective-permute-done((f32[2,128,512]{2,1,0:T(8,128)S(1)}, f32[2,128,512]{2,1,0:T(8,128)S(1)}, u32[]{:S(2)}, u32[]{:S(2)}) %collective-permute-start) | collective-permute-done | bytes 524320 | tf_op jit(solution)/shard_map/ppermute | solution.py:48
  219.4 0.1 select_add_fusion
  219.6 3.7 collective-permute-start.1
  223.2 1.2 collective-permute-done.1
  224.4 0.1 add_bitcast_fusion
  224.5 0.1 collective-permute-start.2
  224.6 8.4 %collective-permute-done.2 = f32[128,512]{1,0:T(8,128)S(1)} collective-permute-done((f32[128,512]{1,0:T(8,128)S(1)}, f32[128,512]{1,0:T(8,128)S(1)}, u32[]{:S(2)}, u32[]{:S(2)}) %collective-permute-start.2) | collective-permute-done | bytes 262176 | tf_op jit(solution)/shard_map/ppermute | solution.py:33
  233.0 0.9 collective-permute-start.3
  233.9 8.1 %collective-permute-done.3 = f32[128,512]{1,0:T(8,128)S(1)} collective-permute-done((f32[128,512]{1,0:T(8,128)S(1)}, f32[128,512]{1,0:T(8,128)S(1)}, u32[]{:S(2)}, u32[]{:S(2)}) %collective-permute-start.3) | collective-permute-done | bytes 262176 | tf_op jit(solution)/shard_map/ppermute | solution.py:33
  242.0 0.3 collective-permute-start.4
  242.3 13.8 %collective-permute-done.4 = f32[128,512]{1,0:T(8,128)S(1)} collective-permute-done((f32[128,512]{1,0:T(8,128)S(1)}, f32[128,512]{1,0:T(8,128)S(1)}, u32[]{:S(2)}, u32[]{:S(2)}) %collective-permute-start.4) | collective-permute-done | bytes 262176 | tf_op jit(solution)/shard_map/ppermute | solution.py:33
  256.1 1.7 collective-permute-start.5
  257.8 10.4 %collective-permute-done.5 = f32[128,512]{1,0:T(8,128)S(1)} collective-permute-done((f32[128,512]{1,0:T(8,128)S(1)}, f32[128,512]{1,0:T(8,128)S(1)}, u32[]{:S(2)}, u32[]{:S(2)}) %collective-permute-start.5) | collective-permute-done | bytes 262176 | tf_op jit(solution)/shard_map/ppermute | solution.py:33
  268.3 3.3 collective-permute-start.6
  271.5 4.9 %collective-permute-done.6 = f32[128,512]{1,0:T(8,128)S(1)} collective-permute-done((f32[128,512]{1,0:T(8,128)S(1)}, f32[128,512]{1,0:T(8,128)S(1)}, u32[]{:S(2)}, u32[]{:S(2)}) %collective-permute-start.6) | collective-permute-done | bytes 262176 | tf_op jit(solution)/shard_map/ppermute | solution.py:33
  276.4 0.7 add_multiply_fusion
  277.2 66.9 %all-gather.5.cloned.1.call-done = bf16[49152,128]{1,0:T(8,128)(2,1)} async-done(((bf16[1536,128]{1,0:T(8,128)(2,1)}), bf16[49152,128]{1,0:T(8,128)(2,1)}) %all-gather.5.cloned.1.call-update) | async-done | bytes 12582928 | tf_op jit(solution)/shard_map/all_gather | solution.py:72
  344.1 22.9 %gather_fusion.1 = bf16[672,128,128]{2,1,0:T(8,128)(2,1)} fusion(bf16[384,128,128]{2,1,0:T(8,128)(2,1)} %bitcast.49, s32[1024]{0:T(1024)S(1)} %pad_clamp_fusion), kind=kCustom, calls=%fused_computation.1 | custom fusion | bytes 44042880 | tf_op jit(solution)/shard_map/gather | solution.py:18
  367.0 17.3 %fusion.1 = bf16[12,128,128]{1,2,0:T(8,128)(2,1)} fusion(bf16[12,56,128,128]{3,2,1,0:T(8,128)(2,1)} %param.9, bf16[12,56,128,128]{3,2,1,0:T(8,128)(2,1)} %bitcast.47), kind=kOutput, calls=%fused_computation.7 | convolution fusion | flops 2818768896 | bytes 44433408 | tf_op jit(solution)/shard_map/pkab,pkbf->paf/dot_general | solution.py:19
  (7 shorter events, 0.2 us)
Async XLA Ops:
  7.2 185.7 %copy-start = (bf16[512,512]{1,0:T(8,128)(2,1)S(1)}, bf16[512,512]{1,0:T(8,128)(2,1)}, u32[]{:S(2)}) copy-start(bf16[512,512]{1,0:T(8,128)(2,1)} %param.7) | copy-start | bytes 1572868
  7.2 136.0 %all-gather.3.cloned.1.call-start = ((), (), s32[]{:S(2)}) async-start(), calls=%async_computation.2 | async-start | bytes 12976128 | tf_op jit(solution)/shard_map/all_gather | solution.py:59
  7.9 336.2 %all-gather.5.cloned.1.call-start = ((), (), s32[]{:S(2)}) async-start(), calls=%async_computation.3 | async-start | bytes 12976128 | tf_op jit(solution)/shard_map/all_gather | solution.py:72
  166.1 26.8 %copy-start.1 = (bf16[384,512]{1,0:T(8,128)(2,1)S(1)}, bf16[384,512]{1,0:T(8,128)(2,1)}, u32[]{:S(2)}) copy-start(bf16[384,512]{1,0:T(8,128)(2,1)} %param.8) | copy-start | bytes 1179652
  205.7 13.6 %collective-permute-start = (f32[2,128,512]{2,1,0:T(8,128)S(1)}, f32[2,128,512]{2,1,0:T(8,128)S(1)}, u32[]{:S(2)}, u32[]{:S(2)}) collective-permute-start(f32[2,128,512]{2,1,0:T(8,128)S(1)} %slice_select_fusion), channel_id=1, source_target_pairs={{0,2},{1,3},{2,0},{3,1},{4,6},{5,7},{6,4},{7,5},{8,10},{9,11},{10,... | collective-permute-start | bytes 1572872 | tf_op jit(solution)/shard_map/ppermute | solution.py:48
  219.6 4.8 %collective-permute-start.1 = (f32[1,128,512]{2,1,0:T(8,128)S(1)}, f32[1,128,512]{2,1,0:T(8,128)S(1)}, u32[]{:S(2)}, u32[]{:S(2)}) collective-permute-start(f32[1,128,512]{2,1,0:T(8,128)S(1)} %slice_select_fusion.1), channel_id=1, source_target_pairs={{0,1},{1,0},{2,3},{3,2},{4,5},{5,4},{6,7},{7,6},{8,9},{9,8},{10,11... | collective-permute-start | bytes 786440 | tf_op jit(solution)/shard_map/ppermute | solution.py:48
  224.5 8.5 %collective-permute-start.2 = (f32[128,512]{1,0:T(8,128)S(1)}, f32[128,512]{1,0:T(8,128)S(1)}, u32[]{:S(2)}, u32[]{:S(2)}) collective-permute-start(f32[128,512]{1,0:T(8,128)S(1)} %add_bitcast_fusion), channel_id=1, source_target_pairs={{0,4},{4,0},{8,12},{12,8},{16,20},{20,16},{24,28},{28,24},{32,36},... | collective-permute-start | bytes 786440 | tf_op jit(solution)/shard_map/ppermute | solution.py:33
  233.0 9.0 %collective-permute-start.3 = (f32[128,512]{1,0:T(8,128)S(1)}, f32[128,512]{1,0:T(8,128)S(1)}, u32[]{:S(2)}, u32[]{:S(2)}) collective-permute-start(f32[128,512]{1,0:T(8,128)S(1)} %add.43), channel_id=1, source_target_pairs={{0,8},{4,12},{8,0},{12,4},{16,24},{20,28},{24,16},{28,20},{32,40},... | collective-permute-start | bytes 786440 | tf_op jit(solution)/shard_map/ppermute | solution.py:33
  242.0 14.0 %collective-permute-start.4 = (f32[128,512]{1,0:T(8,128)S(1)}, f32[128,512]{1,0:T(8,128)S(1)}, u32[]{:S(2)}, u32[]{:S(2)}) collective-permute-start(f32[128,512]{1,0:T(8,128)S(1)} %add.44), channel_id=1, source_target_pairs={{0,16},{4,20},{8,24},{12,28},{16,0},{20,4},{24,8},{28,12},{32,48},... | collective-permute-start | bytes 786440 | tf_op jit(solution)/shard_map/ppermute | solution.py:33
  256.1 12.1 %collective-permute-start.5 = (f32[128,512]{1,0:T(8,128)S(1)}, f32[128,512]{1,0:T(8,128)S(1)}, u32[]{:S(2)}, u32[]{:S(2)}) collective-permute-start(f32[128,512]{1,0:T(8,128)S(1)} %add.45), channel_id=1, source_target_pairs={{0,32},{4,36},{8,40},{12,44},{16,48},{20,52},{24,56},{28,60},{32,0... | collective-permute-start | bytes 786440 | tf_op jit(solution)/shard_map/ppermute | solution.py:33
  268.3 8.2 %collective-permute-start.6 = (f32[128,512]{1,0:T(8,128)S(1)}, f32[128,512]{1,0:T(8,128)S(1)}, u32[]{:S(2)}, u32[]{:S(2)}) collective-permute-start(f32[128,512]{1,0:T(8,128)S(1)} %add.46), channel_id=1, source_target_pairs={{0,64},{4,68},{8,72},{12,76},{16,80},{20,84},{24,88},{28,92},{32,9... | collective-permute-start | bytes 786440 | tf_op jit(solution)/shard_map/ppermute | solution.py:33
Sparse Core Ops, SparseCore 0:
  11.0 132.1 all-gather.2
  205.3 138.7 all-gather.4

commit v2 on v1

--- a/solution.py
+++ b/solution.py
@@ -3,6 +3,8 @@
 import jax
 import jax.numpy as jnp
 from jax import lax
+from jax.experimental import pallas as pl
+from jax.experimental.pallas import tpu as pltpu
 from jax.sharding import PartitionSpec as P
 
 
@@ -12,14 +14,41 @@
     return jnp.sum(jnp.where(matches, block_perm[None, None, :], 0), axis=-1)
 
 
+def _product_kernel(pos_ref, a_ref, *refs):
+    x_refs, o_ref = refs[:-1], refs[-1]
+    acc = jnp.zeros(o_ref.shape[1:], jnp.float32)
+    for k, x_ref in enumerate(x_refs):
+        acc = acc + jnp.dot(a_ref[0, k], x_ref[0], preferred_element_type=jnp.float32)
+    o_ref[0] = acc.astype(o_ref.dtype)
+
+
 def block_product(adjacency_tiles, positions, gathered):
-    block_rows = adjacency_tiles.shape[2]
-    blocks = gathered.reshape(-1, block_rows, gathered.shape[1])
-    picked = blocks[positions]
-    result = jnp.einsum(
-        "pkab,pkbf->paf", adjacency_tiles, picked, preferred_element_type=jnp.float32
+    rows, tiles, bs, _ = adjacency_tiles.shape
+    width = gathered.shape[1]
+    blocks = gathered.reshape(-1, bs, width)
+    in_specs = [pl.BlockSpec((1, tiles, bs, bs), lambda p, pos: (p, 0, 0, 0))]
+    for k in range(tiles):
+        in_specs.append(
+            pl.BlockSpec((1, bs, width), lambda p, pos, k=k: (pos[p * tiles + k], 0, 0))
+        )
+    cost = pl.CostEstimate(
+        flops=2 * rows * tiles * bs * bs * width,
+        bytes_accessed=2 * rows * tiles * bs * (bs + width) + 2 * rows * bs * width,
+        transcendentals=0,
     )
-    return result.reshape(-1, gathered.shape[1])
+    out = pl.pallas_call(
+        _product_kernel,
+        grid_spec=pltpu.PrefetchScalarGridSpec(
+            num_scalar_prefetch=1,
+            grid=(rows,),
+            in_specs=in_specs,
+            out_specs=pl.BlockSpec((1, bs, width), lambda p, pos: (p, 0, 0)),
+        ),
+        out_shape=jax.ShapeDtypeStruct((rows, bs, width), jnp.bfloat16),
+        compiler_params=pltpu.CompilerParams(dimension_semantics=("arbitrary",)),
+        cost_estimate=cost,
+    )(positions.reshape(-1), adjacency_tiles, *([blocks] * tiles))
+    return out.reshape(rows * bs, width)
 
 
 def xor_pairs(size, bit):
@@ -57,7 +86,7 @@
     w_split = weight.reshape(n_rep, feat_dev, f_all)
     positions = column_positions(block_cols, block_perm)
     gathered = lax.all_gather(node_features, "blk", axis=0, tiled=True)
-    aggregate = block_product(adjacency_tiles, positions, gathered).astype(jnp.bfloat16)
+    aggregate = block_product(adjacency_tiles, positions, gathered)
     rows = aggregate.shape[0] // n_rep
     agg_rows = lax.all_to_all(aggregate, "rep", 0, 0, tiled=True).reshape(n_rep, rows, feat_dev)
     preact = jnp.einsum("irf,ifo->ro", agg_rows, w_split, preferred_element_type=jnp.float32)
@@ -70,7 +99,7 @@
     ).astype(jnp.bfloat16)
     grad_agg = lax.all_to_all(grad_split.reshape(n_rep * rows, feat_dev), "rep", 0, 0, tiled=True)
     gathered_grad = lax.all_gather(grad_agg, "blk", axis=0, tiled=True)
-    feature_grad = block_product(adjacency_tiles, positions, gathered_grad).astype(jnp.bfloat16)
+    feature_grad = block_product(adjacency_tiles, positions, gathered_grad)
     weight_part = jnp.einsum("irf,ro->ifo", agg_rows, grad_pre, preferred_element_type=jnp.float32)
     weight_rows = halving_scatter(weight_part, "rep")
     node_total = node_features.shape[0] * lax.axis_size("blk")

time: 391 us -> 361 us (0.923)
  Pallas kernels: 0 us -> 48.1 us
  local copies, waits for them, and re-layouts: 45.8 us -> 0.68 us
  matrix products: 36.2 us -> 2.23 us
    pallas_call x0 -> x2, Pallas kernels: none -> 48.1 us  [block_product(): pl.pallas_call(_product_kernel, grid_spec=pltpu.PrefetchScalarGridSpec(nu...]
    gather x2 -> x0, local copies, waits for them, and re-layouts: 45.7 us -> none  [block_product(): picked = blocks[positions]]
    dot_general x2 -> x0, matrix products: 34 us -> none  [block_product(): jnp.einsum('pkab,pkbf->paf', adjacency_tiles, picked, preferred_element_t...]
where the time goes in v2:
time: 361 us; the launch traced here: 360 us
  waiting for transfers between devices  261 us (72%)
  Pallas kernels  48.1 us (13%)
  blocking collectives  21.7 us (6%)
  between operations  14.1 us (4%)
  starting transfers between devices  10.1 us (3%)
    all_gather x1, waiting for transfers between devices, local(): gathered = lax.all_gather(node_features, 'blk', axis=0, tiled=True)  133 us
    all_gather x1, waiting for transfers between devices, local(): gathered_grad = lax.all_gather(grad_agg, 'blk', axis=0, tiled=True)  66.7 us
    pallas_call x2, Pallas kernels, block_product(): pl.pallas_call(_product_kernel, grid_spec=pltpu.PrefetchScalarGridSpec(nu...  48.1 us
    ppermute x5, waiting for transfers between devices, butterfly_sum(): x = x + lax.ppermute(x, axis, xor_pairs(size, bit))  45.4 us
    ppermute x2, waiting for transfers between devices, halving_scatter(): parts = keep + lax.ppermute(send, axis, xor_pairs(size, bit))  14.7 us
    all_to_all x1, blocking collectives, local(): lax.all_to_all(aggregate, 'rep', 0, 0, tiled=True)  11.2 us
    all_to_all x1, blocking collectives, local(): lax.all_to_all(grad_split.reshape(n_rep * rows, feat_dev), 'rep', 0, 0, t...  10.5 us
  transfers between devices with their start and end apart: 9, of which 9 were waited for; matrix products, arithmetic and copies ran while one was open for 1% of the time, Pallas kernels for 0%

profile of v2, /device:TPU:1, one launch (start us, length us, event | category | flops | bytes accessed | tf_op | source)
XLA Modules:
  0.0 360.4 jit_solution(10551996134601474429)
XLA Ops:
  7.2 0.0 copy-start
  7.2 0.0 all-gather.3.cloned.1.call-start
  7.2 0.7 all-gather.3.cloned.1.call-update
  7.9 0.0 all-gather.5.cloned.1.call-start
  8.0 1.1 select_reduce_fusion
  9.1 0.7 reshape.34.pos_ref
  9.8 133.4 %all-gather.3.cloned.1.call-done = bf16[49152,128]{1,0:T(8,128)(2,1)} async-done(((bf16[1536,128]{1,0:T(8,128)(2,1)}), bf16[49152,128]{1,0:T(8,128)(2,1)}) %all-gather.3.cloned.1.call-update) | async-done | bytes 12582928 | tf_op jit(solution)/shard_map/all_gather | solution.py:88
  143.2 0.0 copy-start.1
  143.2 24.1 %shard_map.85 = bf16[12,128,128]{2,1,0:T(8,128)(2,1)} custom-call(s32[672]{0:T(1024)} %reshape.34.pos_ref, bf16[12,56,128,128]{3,2,1,0:T(8,128)(2,1)} %a_ref.3, bf16[384,128,128]{2,1,0:T(8,128)(2,1)} %bitcast.106, bf16[384,128,128]{2,1,0:T(8,128)(2,1)} %bitcast.134, bf16[384,128,128]{2,1,0:T(8,128)(2,1)} %bitcast.81, bf16[384,128,128]{2,1,0:T(8,128)(2,1)} %bitcast.82, ...), custom_call_target="tpu_custom_call" | custom-call | flops 2818572288 | bytes 44433408 | tf_op jit(solution)/shard_map/pallas_call | solution.py:39
  167.3 11.2 %all_to_all.18 = bf16[4,384,128]{2,1,0:T(8,128)(2,1)S(1)} all-to-all(bf16[4,384,128]{2,1,0:T(8,128)(2,1)} %bitcast.136), channel_id=1, replica_groups=mesh['blk'=32,'rep'=4] {'rep'}, dimensions={0} | all-to-all | bytes 786432 | tf_op jit(solution)/shard_map/all_to_all | solution.py:91
  178.5 0.0 copy-done
  178.5 0.0 copy-done.1
  178.6 1.4 multiply_convert_fusion
  179.9 0.4 fusion
  180.3 10.5 %all_to_all.19 = bf16[4,384,128]{2,1,0:T(8,128)(2,1)} all-to-all(bf16[4,384,128]{2,1,0:T(8,128)(2,1)S(1)} %fusion), channel_id=1, replica_groups=mesh['blk'=32,'rep'=4] {'rep'}, dimensions={0} | all-to-all | bytes 786432 | tf_op jit(solution)/shard_map/all_to_all | solution.py:100
  190.8 0.0 all-gather.5.cloned.1.call-update
  190.9 0.5 fusion.1
  191.3 0.1 slice_select_fusion
  191.4 0.6 collective-permute-start
  192.0 13.5 %collective-permute-done = f32[2,128,512]{2,1,0:T(8,128)S(1)} collective-permute-done((f32[2,128,512]{2,1,0:T(8,128)S(1)}, f32[2,128,512]{2,1,0:T(8,128)S(1)}, u32[]{:S(2)}, u32[]{:S(2)}) %collective-permute-start) | collective-permute-done | bytes 524320 | tf_op jit(solution)/shard_map/ppermute | solution.py:77
  205.6 0.1 select_add_fusion
  205.8 3.2 collective-permute-start.1
  208.9 1.2 collective-permute-done.1
  210.1 0.1 add_bitcast_fusion
  210.1 0.2 collective-permute-start.2
  210.4 8.4 %collective-permute-done.2 = f32[128,512]{1,0:T(8,128)S(1)} collective-permute-done((f32[128,512]{1,0:T(8,128)S(1)}, f32[128,512]{1,0:T(8,128)S(1)}, u32[]{:S(2)}, u32[]{:S(2)}) %collective-permute-start.2) | collective-permute-done | bytes 262176 | tf_op jit(solution)/shard_map/ppermute | solution.py:62
  218.8 1.4 collective-permute-start.3
  220.2 8.0 %collective-permute-done.3 = f32[128,512]{1,0:T(8,128)S(1)} collective-permute-done((f32[128,512]{1,0:T(8,128)S(1)}, f32[128,512]{1,0:T(8,128)S(1)}, u32[]{:S(2)}, u32[]{:S(2)}) %collective-permute-start.3) | collective-permute-done | bytes 262176 | tf_op jit(solution)/shard_map/ppermute | solution.py:62
  228.3 0.1 collective-permute-start.4
  228.4 13.6 %collective-permute-done.4 = f32[128,512]{1,0:T(8,128)S(1)} collective-permute-done((f32[128,512]{1,0:T(8,128)S(1)}, f32[128,512]{1,0:T(8,128)S(1)}, u32[]{:S(2)}, u32[]{:S(2)}) %collective-permute-start.4) | collective-permute-done | bytes 262176 | tf_op jit(solution)/shard_map/ppermute | solution.py:62
  242.0 1.5 collective-permute-start.5
  243.5 10.5 %collective-permute-done.5 = f32[128,512]{1,0:T(8,128)S(1)} collective-permute-done((f32[128,512]{1,0:T(8,128)S(1)}, f32[128,512]{1,0:T(8,128)S(1)}, u32[]{:S(2)}, u32[]{:S(2)}) %collective-permute-start.5) | collective-permute-done | bytes 262176 | tf_op jit(solution)/shard_map/ppermute | solution.py:62
  254.0 3.1 collective-permute-start.6
  257.1 4.9 %collective-permute-done.6 = f32[128,512]{1,0:T(8,128)S(1)} collective-permute-done((f32[128,512]{1,0:T(8,128)S(1)}, f32[128,512]{1,0:T(8,128)S(1)}, u32[]{:S(2)}, u32[]{:S(2)}) %collective-permute-start.6) | collective-permute-done | bytes 262176 | tf_op jit(solution)/shard_map/ppermute | solution.py:62
  262.0 0.7 add_multiply_fusion
  262.8 66.7 %all-gather.5.cloned.1.call-done = bf16[49152,128]{1,0:T(8,128)(2,1)} async-done(((bf16[1536,128]{1,0:T(8,128)(2,1)}), bf16[49152,128]{1,0:T(8,128)(2,1)}) %all-gather.5.cloned.1.call-update) | async-done | bytes 12582928 | tf_op jit(solution)/shard_map/all_gather | solution.py:101
  329.5 24.0 %shard_map.86 = bf16[12,128,128]{2,1,0:T(8,128)(2,1)} custom-call(s32[672]{0:T(1024)} %reshape.34.pos_ref, bf16[12,56,128,128]{3,2,1,0:T(8,128)(2,1)} %a_ref.3, bf16[384,128,128]{2,1,0:T(8,128)(2,1)} %bitcast.50, bf16[384,128,128]{2,1,0:T(8,128)(2,1)} %bitcast.78, bf16[384,128,128]{2,1,0:T(8,128)(2,1)} %bitcast.25, bf16[384,128,128]{2,1,0:T(8,128)(2,1)} %bitcast.26, ...), custom_call_target="tpu_custom_call" | custom-call | flops 2818572288 | bytes 44433408 | tf_op jit(solution)/shard_map/pallas_call | solution.py:39
  (5 shorter events, 0.2 us)
Async XLA Ops:
  7.2 171.4 %copy-start = (bf16[512,512]{1,0:T(8,128)(2,1)S(1)}, bf16[512,512]{1,0:T(8,128)(2,1)}, u32[]{:S(2)}) copy-start(bf16[512,512]{1,0:T(8,128)(2,1)} %param.7) | copy-start | bytes 1572868
  7.2 136.0 %all-gather.3.cloned.1.call-start = ((), (), s32[]{:S(2)}) async-start(), calls=%async_computation.2 | async-start | bytes 12976128 | tf_op jit(solution)/shard_map/all_gather | solution.py:88
  7.9 321.6 %all-gather.5.cloned.1.call-start = ((), (), s32[]{:S(2)}) async-start(), calls=%async_computation.3 | async-start | bytes 12976128 | tf_op jit(solution)/shard_map/all_gather | solution.py:101
  143.2 35.4 %copy-start.1 = (bf16[384,512]{1,0:T(8,128)(2,1)S(1)}, bf16[384,512]{1,0:T(8,128)(2,1)}, u32[]{:S(2)}) copy-start(bf16[384,512]{1,0:T(8,128)(2,1)} %param.8) | copy-start | bytes 1179652
  191.4 14.1 %collective-permute-start = (f32[2,128,512]{2,1,0:T(8,128)S(1)}, f32[2,128,512]{2,1,0:T(8,128)S(1)}, u32[]{:S(2)}, u32[]{:S(2)}) collective-permute-start(f32[2,128,512]{2,1,0:T(8,128)S(1)} %slice_select_fusion), channel_id=1, source_target_pairs={{0,2},{1,3},{2,0},{3,1},{4,6},{5,7},{6,4},{7,5},{8,10},{9,11},{10,... | collective-permute-start | bytes 1572872 | tf_op jit(solution)/shard_map/ppermute | solution.py:77
  205.8 4.3 %collective-permute-start.1 = (f32[1,128,512]{2,1,0:T(8,128)S(1)}, f32[1,128,512]{2,1,0:T(8,128)S(1)}, u32[]{:S(2)}, u32[]{:S(2)}) collective-permute-start(f32[1,128,512]{2,1,0:T(8,128)S(1)} %slice_select_fusion.1), channel_id=1, source_target_pairs={{0,1},{1,0},{2,3},{3,2},{4,5},{5,4},{6,7},{7,6},{8,9},{9,8},{10,11... | collective-permute-start | bytes 786440 | tf_op jit(solution)/shard_map/ppermute | solution.py:77
  210.1 8.6 %collective-permute-start.2 = (f32[128,512]{1,0:T(8,128)S(1)}, f32[128,512]{1,0:T(8,128)S(1)}, u32[]{:S(2)}, u32[]{:S(2)}) collective-permute-start(f32[128,512]{1,0:T(8,128)S(1)} %add_bitcast_fusion), channel_id=1, source_target_pairs={{0,4},{4,0},{8,12},{12,8},{16,20},{20,16},{24,28},{28,24},{32,36},... | collective-permute-start | bytes 786440 | tf_op jit(solution)/shard_map/ppermute | solution.py:62
  218.8 9.4 %collective-permute-start.3 = (f32[128,512]{1,0:T(8,128)S(1)}, f32[128,512]{1,0:T(8,128)S(1)}, u32[]{:S(2)}, u32[]{:S(2)}) collective-permute-start(f32[128,512]{1,0:T(8,128)S(1)} %add.31), channel_id=1, source_target_pairs={{0,8},{4,12},{8,0},{12,4},{16,24},{20,28},{24,16},{28,20},{32,40},... | collective-permute-start | bytes 786440 | tf_op jit(solution)/shard_map/ppermute | solution.py:62
  228.3 13.7 %collective-permute-start.4 = (f32[128,512]{1,0:T(8,128)S(1)}, f32[128,512]{1,0:T(8,128)S(1)}, u32[]{:S(2)}, u32[]{:S(2)}) collective-permute-start(f32[128,512]{1,0:T(8,128)S(1)} %add.32), channel_id=1, source_target_pairs={{0,16},{4,20},{8,24},{12,28},{16,0},{20,4},{24,8},{28,12},{32,48},... | collective-permute-start | bytes 786440 | tf_op jit(solution)/shard_map/ppermute | solution.py:62
  242.0 12.0 %collective-permute-start.5 = (f32[128,512]{1,0:T(8,128)S(1)}, f32[128,512]{1,0:T(8,128)S(1)}, u32[]{:S(2)}, u32[]{:S(2)}) collective-permute-start(f32[128,512]{1,0:T(8,128)S(1)} %add.33), channel_id=1, source_target_pairs={{0,32},{4,36},{8,40},{12,44},{16,48},{20,52},{24,56},{28,60},{32,0... | collective-permute-start | bytes 786440 | tf_op jit(solution)/shard_map/ppermute | solution.py:62
  254.0 8.0 %collective-permute-start.6 = (f32[128,512]{1,0:T(8,128)S(1)}, f32[128,512]{1,0:T(8,128)S(1)}, u32[]{:S(2)}, u32[]{:S(2)}) collective-permute-start(f32[128,512]{1,0:T(8,128)S(1)} %add.34), channel_id=1, source_target_pairs={{0,64},{4,68},{8,72},{12,76},{16,80},{20,84},{24,88},{28,92},{32,9... | collective-permute-start | bytes 786440 | tf_op jit(solution)/shard_map/ppermute | solution.py:62
Sparse Core Ops, SparseCore 0:
  11.0 132.1 all-gather.2
  191.0 138.4 all-gather.4

commit v3 on v2

--- a/solution.py
+++ b/solution.py
@@ -1,3 +1,4 @@
+import functools
 import math
 
 import jax
@@ -5,7 +6,7 @@
 from jax import lax
 from jax.experimental import pallas as pl
 from jax.experimental.pallas import tpu as pltpu
-from jax.sharding import PartitionSpec as P
+from jax.sharding import Mesh, PartitionSpec as P
 
 
 def column_positions(block_cols, block_perm):
@@ -55,8 +56,7 @@
     return [(i, i ^ bit) for i in range(size)]
 
 
-def butterfly_sum(x, axis):
-    size = lax.axis_size(axis)
+def butterfly_sum(x, axis, size):
     bit = 1
     while bit < size:
         x = x + lax.ppermute(x, axis, xor_pairs(size, bit))
@@ -64,8 +64,7 @@
     return x
 
 
-def halving_scatter(parts, axis):
-    size = lax.axis_size(axis)
+def halving_scatter(parts, axis, size):
     me = lax.axis_index(axis)
     bit = size // 2
     while bit >= 1:
@@ -79,16 +78,34 @@
     return parts[0]
 
 
-def local(node_features, weight, cotangent, adjacency_tiles, block_cols, block_perm):
+BLK = ("z", "xh", "y")
+REP = ("xl", "c")
+
+
+def hier_gather(x):
+    pair = lax.all_gather(x, "xh", axis=0, tiled=True)
+    return lax.all_gather(pair, ("z", "y"), axis=0, tiled=True)
+
+
+def hier_positions(positions, local_blocks, n_xh, n_y):
+    owner, block = positions // local_blocks, positions % local_blocks
+    z, xh, y = owner // (n_xh * n_y), (owner // n_y) % n_xh, owner % n_y
+    return ((z * n_y + y) * n_xh + xh) * local_blocks + block
+
+
+def local(sizes, node_features, weight, cotangent, adjacency_tiles, block_cols, block_perm):
+    n_z, n_xh, n_y, n_xl, n_c = sizes
+    n_blk, n_rep = n_z * n_xh * n_y, n_xl * n_c
     feat_dev = node_features.shape[1]
-    n_rep = lax.axis_size("rep")
     f_all = weight.shape[0]
+    bs = adjacency_tiles.shape[2]
     w_split = weight.reshape(n_rep, feat_dev, f_all)
     positions = column_positions(block_cols, block_perm)
-    gathered = lax.all_gather(node_features, "blk", axis=0, tiled=True)
+    positions = hier_positions(positions, node_features.shape[0] // bs, n_xh, n_y)
+    gathered = hier_gather(node_features)
     aggregate = block_product(adjacency_tiles, positions, gathered)
     rows = aggregate.shape[0] // n_rep
-    agg_rows = lax.all_to_all(aggregate, "rep", 0, 0, tiled=True).reshape(n_rep, rows, feat_dev)
+    agg_rows = lax.all_to_all(aggregate, REP, 0, 0, tiled=True).reshape(n_rep, rows, feat_dev)
     preact = jnp.einsum("irf,ifo->ro", agg_rows, w_split, preferred_element_type=jnp.float32)
     gating = jax.nn.sigmoid(preact)
     activated = (preact * gating).astype(jnp.bfloat16)
@@ -97,28 +114,31 @@
     grad_split = jnp.einsum(
         "rf,jof->jro", grad_pre, w_split, preferred_element_type=jnp.float32
     ).astype(jnp.bfloat16)
-    grad_agg = lax.all_to_all(grad_split.reshape(n_rep * rows, feat_dev), "rep", 0, 0, tiled=True)
-    gathered_grad = lax.all_gather(grad_agg, "blk", axis=0, tiled=True)
+    grad_agg = lax.all_to_all(grad_split.reshape(n_rep * rows, feat_dev), REP, 0, 0, tiled=True)
+    gathered_grad = hier_gather(grad_agg)
     feature_grad = block_product(adjacency_tiles, positions, gathered_grad)
     weight_part = jnp.einsum("irf,ro->ifo", agg_rows, grad_pre, preferred_element_type=jnp.float32)
-    weight_rows = halving_scatter(weight_part, "rep")
-    node_total = node_features.shape[0] * lax.axis_size("blk")
-    weight_grad = butterfly_sum(weight_rows, "blk") * (1.0 / math.sqrt(node_total))
+    weight_rows = halving_scatter(weight_part, REP, n_rep)
+    node_total = node_features.shape[0] * n_blk
+    weight_grad = butterfly_sum(weight_rows, BLK, n_blk) * (1.0 / math.sqrt(node_total))
     return (activated, feature_grad, weight_grad)
 
 
 def solution(mesh):
+    n_blk, n_rep = mesh.shape["blk"], mesh.shape["rep"]
+    sizes = (n_blk // 8, 2, 4, n_rep // 2, 2)
+    fine = Mesh(mesh.devices.reshape(sizes), BLK + REP)
     return jax.shard_map(
-        local,
-        mesh=mesh,
+        functools.partial(local, sizes),
+        mesh=fine,
         in_specs=(
-            P("blk", "rep"),
+            P(BLK, REP),
             P(),
-            P(("blk", "rep"), None),
-            P("blk", None, None, None),
-            P("blk", None),
+            P(BLK + REP, None),
+            P(BLK, None, None, None),
+            P(BLK, None),
             P(),
         ),
-        out_specs=(P(("blk", "rep"), None), P("blk", "rep"), P("rep", None)),
+        out_specs=(P(BLK + REP, None), P(BLK, REP), P(REP, None)),
         check_vma=False,
     )

time: 361 us -> 310 us (0.86)
  waiting for transfers between devices: 261 us -> 179 us
  blocking collectives: 21.7 us -> 47.5 us
  starting transfers between devices: 10.1 us -> 14.3 us
    all_gather x2, waiting for transfers between devices: 200 us -> 120 us  [hier_gather(): return lax.all_gather(pair, ('z', 'y'), axis=0, tiled=True)]
    all_gather x0 -> x2, blocking collectives: none -> 27.1 us  [hier_gather(): pair = lax.all_gather(x, 'xh', axis=0, tiled=True)]
    ppermute x5, starting transfers between devices: 6.28 us -> 10.3 us  [butterfly_sum(): x = x + lax.ppermute(x, axis, xor_pairs(size, bit))]
where the time goes in v3:
time: 310 us; the launch traced here: 309 us
  waiting for transfers between devices  179 us (58%)
  Pallas kernels  48.1 us (16%)
  blocking collectives  47.5 us (15%)
  starting transfers between devices  14.3 us (5%)
  between operations  14.2 us (5%)
    all_gather x2, waiting for transfers between devices, hier_gather(): return lax.all_gather(pair, ('z', 'y'), axis=0, tiled=True)  120 us
    pallas_call x2, Pallas kernels, block_product(): pl.pallas_call(_product_kernel, grid_spec=pltpu.PrefetchScalarGridSpec(nu...  48.1 us
    ppermute x5, waiting for transfers between devices, butterfly_sum(): x = x + lax.ppermute(x, axis, xor_pairs(size, bit))  47.5 us
    all_gather x2, blocking collectives, hier_gather(): pair = lax.all_gather(x, 'xh', axis=0, tiled=True)  27.1 us
    ppermute x2, waiting for transfers between devices, halving_scatter(): parts = keep + lax.ppermute(send, axis, xor_pairs(size, bit))  11.8 us
    all_to_all x1, blocking collectives, local(): lax.all_to_all(aggregate, REP, 0, 0, tiled=True)  10.7 us
    ppermute x5, starting transfers between devices, butterfly_sum(): x = x + lax.ppermute(x, axis, xor_pairs(size, bit))  10.3 us
    all_to_all x1, blocking collectives, local(): lax.all_to_all(grad_split.reshape(n_rep * rows, feat_dev), REP, 0, 0, til...  9.81 us
  transfers between devices with their start and end apart: 9, of which 9 were waited for; matrix products, arithmetic and copies ran while one was open for 1% of the time, Pallas kernels for 0%

profile of v3, /device:TPU:1, one launch (start us, length us, event | category | flops | bytes accessed | tf_op | source)
XLA Modules:
  0.0 309.0 jit_solution(12646258822061737787)
XLA Ops:
  7.2 0.0 copy-start
  7.2 0.0 all-gather.3.cloned.1.call-start
  7.2 15.2 %all_gather.12 = bf16[3072,128]{1,0:T(8,128)(2,1)} all-gather(bf16[1536,128]{1,0:T(8,128)(2,1)} %param.6), channel_id=1, replica_groups=mesh['z'=4,'xh'=2,'y'=4,'xl'=2,'c'=2] {'xh'}, dimensions={0}, use_global_device_ids=true | all-gather | bytes 1179648 | tf_op jit(solution)/shard_map/all_gather | solution.py:86
  22.4 0.0 all-gather.3.cloned.1.call-update
  22.5 0.0 all-gather.5.cloned.1.call-start
  22.5 1.1 select_reduce_fusion
  23.6 0.1 div.32
  23.7 0.1 rem.63
  23.8 0.1 ne.69
  23.9 0.6 fusion.10.pos_ref
  24.5 89.3 %all-gather.3.cloned.1.call-done = bf16[49152,128]{1,0:T(8,128)(2,1)} async-done(((bf16[3072,128]{1,0:T(8,128)(2,1)}), bf16[49152,128]{1,0:T(8,128)(2,1)}) %all-gather.3.cloned.1.call-update) | async-done | bytes 12582928 | tf_op jit(solution)/shard_map/all_gather | solution.py:87
  113.9 0.0 copy-start.1
  113.9 24.1 %shard_map.85 = bf16[12,128,128]{2,1,0:T(8,128)(2,1)} custom-call(s32[672]{0:T(1024)} %fusion.10.pos_ref, bf16[12,56,128,128]{3,2,1,0:T(8,128)(2,1)} %a_ref.3, bf16[384,128,128]{2,1,0:T(8,128)(2,1)} %bitcast.106, bf16[384,128,128]{2,1,0:T(8,128)(2,1)} %bitcast.134, bf16[384,128,128]{2,1,0:T(8,128)(2,1)} %bitcast.81, bf16[384,128,128]{2,1,0:T(8,128)(2,1)} %bitcast.82, ...), custom_call_target="tpu_custom_call" | custom-call | flops 2818572288 | bytes 44433408 | tf_op jit(solution)/shard_map/pallas_call | solution.py:40
  138.0 10.7 %all_to_all.18 = bf16[4,384,128]{2,1,0:T(8,128)(2,1)S(1)} all-to-all(bf16[4,384,128]{2,1,0:T(8,128)(2,1)} %bitcast.136), channel_id=1, replica_groups=mesh['z'=4,'xh'=2,'y'=4,'xl'=2,'c'=2] {'xl','c'}, dimensions={0} | all-to-all | bytes 786432 | tf_op jit(solution)/shard_map/all_to_all | solution.py:108
  148.6 0.0 copy-done
  148.6 0.0 copy-done.1
  148.6 1.4 multiply_convert_fusion
  150.0 0.4 fusion
  150.4 9.8 %all_to_all.19 = bf16[4,384,128]{2,1,0:T(8,128)(2,1)S(1)} all-to-all(bf16[4,384,128]{2,1,0:T(8,128)(2,1)S(1)} %fusion), channel_id=1, replica_groups=mesh['z'=4,'xh'=2,'y'=4,'xl'=2,'c'=2] {'xl','c'}, dimensions={0} | all-to-all | bytes 786432 | tf_op jit(solution)/shard_map/all_to_all | solution.py:117
  160.2 11.9 %all_gather.14 = bf16[3072,128]{1,0:T(8,128)(2,1)} all-gather(bf16[1536,128]{1,0:T(8,128)(2,1)S(1)} %bitcast.135), channel_id=1, replica_groups=mesh['z'=4,'xh'=2,'y'=4,'xl'=2,'c'=2] {'xh'}, dimensions={0}, use_global_device_ids=true | all-gather | bytes 1179648 | tf_op jit(solution)/shard_map/all_gather | solution.py:86
  172.1 0.0 all-gather.5.cloned.1.call-update
  172.2 0.5 fusion.1
  172.6 0.1 slice_select_fusion
  172.7 1.0 collective-permute-start
  173.7 10.6 %collective-permute-done = f32[2,128,512]{2,1,0:T(8,128)S(1)} collective-permute-done((f32[2,128,512]{2,1,0:T(8,128)S(1)}, f32[2,128,512]{2,1,0:T(8,128)S(1)}, u32[]{:S(2)}, u32[]{:S(2)}) %collective-permute-start) | collective-permute-done | bytes 524320 | tf_op jit(solution)/shard_map/ppermute | solution.py:76
  184.4 0.1 select_add_fusion
  184.6 2.8 collective-permute-start.1
  187.4 1.2 collective-permute-done.1
  188.6 0.1 add_bitcast_fusion
  188.6 1.6 collective-permute-start.2
  190.3 12.1 %collective-permute-done.2 = f32[128,512]{1,0:T(8,128)S(1)} collective-permute-done((f32[128,512]{1,0:T(8,128)S(1)}, f32[128,512]{1,0:T(8,128)S(1)}, u32[]{:S(2)}, u32[]{:S(2)}) %collective-permute-start.2) | collective-permute-done | bytes 262176 | tf_op jit(solution)/shard_map/ppermute | solution.py:62
  202.4 2.5 collective-permute-start.3
  204.9 6.0 %collective-permute-done.3 = f32[128,512]{1,0:T(8,128)S(1)} collective-permute-done((f32[128,512]{1,0:T(8,128)S(1)}, f32[128,512]{1,0:T(8,128)S(1)}, u32[]{:S(2)}, u32[]{:S(2)}) %collective-permute-start.3) | collective-permute-done | bytes 262176 | tf_op jit(solution)/shard_map/ppermute | solution.py:62
  210.9 2.4 collective-permute-start.4
  213.3 5.3 %collective-permute-done.4 = f32[128,512]{1,0:T(8,128)S(1)} collective-permute-done((f32[128,512]{1,0:T(8,128)S(1)}, f32[128,512]{1,0:T(8,128)S(1)}, u32[]{:S(2)}, u32[]{:S(2)}) %collective-permute-start.4) | collective-permute-done | bytes 262176 | tf_op jit(solution)/shard_map/ppermute | solution.py:62
  218.6 1.2 collective-permute-start.5
  219.9 12.0 %collective-permute-done.5 = f32[128,512]{1,0:T(8,128)S(1)} collective-permute-done((f32[128,512]{1,0:T(8,128)S(1)}, f32[128,512]{1,0:T(8,128)S(1)}, u32[]{:S(2)}, u32[]{:S(2)}) %collective-permute-start.5) | collective-permute-done | bytes 262176 | tf_op jit(solution)/shard_map/ppermute | solution.py:62
  231.9 2.6 collective-permute-start.6
  234.5 12.1 %collective-permute-done.6 = f32[128,512]{1,0:T(8,128)S(1)} collective-permute-done((f32[128,512]{1,0:T(8,128)S(1)}, f32[128,512]{1,0:T(8,128)S(1)}, u32[]{:S(2)}, u32[]{:S(2)}) %collective-permute-start.6) | collective-permute-done | bytes 262176 | tf_op jit(solution)/shard_map/ppermute | solution.py:62
  246.6 0.7 add_multiply_fusion
  247.3 30.9 %all-gather.5.cloned.1.call-done = bf16[49152,128]{1,0:T(8,128)(2,1)} async-done(((bf16[3072,128]{1,0:T(8,128)(2,1)}), bf16[49152,128]{1,0:T(8,128)(2,1)}) %all-gather.5.cloned.1.call-update) | async-done | bytes 12582928 | tf_op jit(solution)/shard_map/all_gather | solution.py:87
  278.2 24.0 %shard_map.86 = bf16[12,128,128]{2,1,0:T(8,128)(2,1)} custom-call(s32[672]{0:T(1024)} %fusion.10.pos_ref, bf16[12,56,128,128]{3,2,1,0:T(8,128)(2,1)} %a_ref.3, bf16[384,128,128]{2,1,0:T(8,128)(2,1)} %bitcast.50, bf16[384,128,128]{2,1,0:T(8,128)(2,1)} %bitcast.78, bf16[384,128,128]{2,1,0:T(8,128)(2,1)} %bitcast.25, bf16[384,128,128]{2,1,0:T(8,128)(2,1)} %bitcast.26, ...), custom_call_target="tpu_custom_call" | custom-call | flops 2818572288 | bytes 44433408 | tf_op jit(solution)/shard_map/pallas_call | solution.py:40
  (7 shorter events, 0.2 us)
Async XLA Ops:
  7.2 141.5 %copy-start = (bf16[512,512]{1,0:T(8,128)(2,1)S(1)}, bf16[512,512]{1,0:T(8,128)(2,1)}, u32[]{:S(2)}) copy-start(bf16[512,512]{1,0:T(8,128)(2,1)} %param.7) | copy-start | bytes 1572868
  7.2 106.7 %all-gather.3.cloned.1.call-start = ((), (), s32[]{:S(2)}) async-start(), calls=%async_computation.2 | async-start | bytes 13369344 | tf_op jit(solution)/shard_map/all_gather | solution.py:87
  22.5 255.8 %all-gather.5.cloned.1.call-start = ((), (), s32[]{:S(2)}) async-start(), calls=%async_computation.3 | async-start | bytes 13369344 | tf_op jit(solution)/shard_map/all_gather | solution.py:87
  113.9 34.8 %copy-start.1 = (bf16[384,512]{1,0:T(8,128)(2,1)S(1)}, bf16[384,512]{1,0:T(8,128)(2,1)}, u32[]{:S(2)}) copy-start(bf16[384,512]{1,0:T(8,128)(2,1)} %param.8) | copy-start | bytes 1179652
  172.7 11.7 %collective-permute-start = (f32[2,128,512]{2,1,0:T(8,128)S(1)}, f32[2,128,512]{2,1,0:T(8,128)S(1)}, u32[]{:S(2)}, u32[]{:S(2)}) collective-permute-start(f32[2,128,512]{2,1,0:T(8,128)S(1)} %slice_select_fusion), channel_id=1, source_target_pairs={{0,2},{1,3},{2,0},{3,1},{4,6},{5,7},{6,4},{7,5},{8,10},{9,11},{10,... | collective-permute-start | bytes 1572872 | tf_op jit(solution)/shard_map/ppermute | solution.py:76
  184.6 4.0 %collective-permute-start.1 = (f32[1,128,512]{2,1,0:T(8,128)S(1)}, f32[1,128,512]{2,1,0:T(8,128)S(1)}, u32[]{:S(2)}, u32[]{:S(2)}) collective-permute-start(f32[1,128,512]{2,1,0:T(8,128)S(1)} %slice_select_fusion.1), channel_id=1, source_target_pairs={{0,1},{1,0},{2,3},{3,2},{4,5},{5,4},{6,7},{7,6},{8,9},{9,8},{10,11... | collective-permute-start | bytes 786440 | tf_op jit(solution)/shard_map/ppermute | solution.py:76
  188.6 13.7 %collective-permute-start.2 = (f32[128,512]{1,0:T(8,128)S(1)}, f32[128,512]{1,0:T(8,128)S(1)}, u32[]{:S(2)}, u32[]{:S(2)}) collective-permute-start(f32[128,512]{1,0:T(8,128)S(1)} %add_bitcast_fusion), channel_id=1, source_target_pairs={{0,4},{4,0},{8,12},{12,8},{16,20},{20,16},{24,28},{28,24},{32,36},... | collective-permute-start | bytes 786440 | tf_op jit(solution)/shard_map/ppermute | solution.py:62
  202.4 8.5 %collective-permute-start.3 = (f32[128,512]{1,0:T(8,128)S(1)}, f32[128,512]{1,0:T(8,128)S(1)}, u32[]{:S(2)}, u32[]{:S(2)}) collective-permute-start(f32[128,512]{1,0:T(8,128)S(1)} %add.76), channel_id=1, source_target_pairs={{0,8},{4,12},{8,0},{12,4},{16,24},{20,28},{24,16},{28,20},{32,40},... | collective-permute-start | bytes 786440 | tf_op jit(solution)/shard_map/ppermute | solution.py:62
  210.9 7.6 %collective-permute-start.4 = (f32[128,512]{1,0:T(8,128)S(1)}, f32[128,512]{1,0:T(8,128)S(1)}, u32[]{:S(2)}, u32[]{:S(2)}) collective-permute-start(f32[128,512]{1,0:T(8,128)S(1)} %add.77), channel_id=1, source_target_pairs={{0,16},{4,20},{8,24},{12,28},{16,0},{20,4},{24,8},{28,12},{32,48},... | collective-permute-start | bytes 786440 | tf_op jit(solution)/shard_map/ppermute | solution.py:62
  218.6 13.3 %collective-permute-start.5 = (f32[128,512]{1,0:T(8,128)S(1)}, f32[128,512]{1,0:T(8,128)S(1)}, u32[]{:S(2)}, u32[]{:S(2)}) collective-permute-start(f32[128,512]{1,0:T(8,128)S(1)} %add.78), channel_id=1, source_target_pairs={{0,32},{4,36},{8,40},{12,44},{16,48},{20,52},{24,56},{28,60},{32,0... | collective-permute-start | bytes 786440 | tf_op jit(solution)/shard_map/ppermute | solution.py:62
  231.9 14.7 %collective-permute-start.6 = (f32[128,512]{1,0:T(8,128)S(1)}, f32[128,512]{1,0:T(8,128)S(1)}, u32[]{:S(2)}, u32[]{:S(2)}) collective-permute-start(f32[128,512]{1,0:T(8,128)S(1)} %add.79), channel_id=1, source_target_pairs={{0,64},{4,68},{8,72},{12,76},{16,80},{20,84},{24,88},{28,92},{32,9... | collective-permute-start | bytes 786440 | tf_op jit(solution)/shard_map/ppermute | solution.py:62
Sparse Core Ops, SparseCore 0:
  22.6 91.2 all-gather.2
  172.3 105.8 all-gather.4

commit v4 on v3

--- a/solution.py
+++ b/solution.py
@@ -82,15 +82,26 @@
 REP = ("xl", "c")
 
 
+def exchange(parts, axis, size):
+    me = lax.axis_index(axis)
+    got = [lax.dynamic_index_in_dim(parts, me, 0, keepdims=False)]
+    for s in range(1, size):
+        send = lax.dynamic_index_in_dim(parts, me ^ s, 0, keepdims=False)
+        got.append(lax.ppermute(send, axis, xor_pairs(size, s)))
+    return jnp.take(jnp.stack(got), jnp.arange(size) ^ me, axis=0)
+
+
 def hier_gather(x):
-    pair = lax.all_gather(x, "xh", axis=0, tiled=True)
+    partner = lax.ppermute(x, "xh", xor_pairs(2, 1))
+    pair = jnp.concatenate([x, partner], axis=0)
     return lax.all_gather(pair, ("z", "y"), axis=0, tiled=True)
 
 
 def hier_positions(positions, local_blocks, n_xh, n_y):
     owner, block = positions // local_blocks, positions % local_blocks
     z, xh, y = owner // (n_xh * n_y), (owner // n_y) % n_xh, owner % n_y
-    return ((z * n_y + y) * n_xh + xh) * local_blocks + block
+    slot = xh ^ lax.axis_index("xh")
+    return ((z * n_y + y) * n_xh + slot) * local_blocks + block
 
 
 def local(sizes, node_features, weight, cotangent, adjacency_tiles, block_cols, block_perm):
@@ -105,7 +116,7 @@
     gathered = hier_gather(node_features)
     aggregate = block_product(adjacency_tiles, positions, gathered)
     rows = aggregate.shape[0] // n_rep
-    agg_rows = lax.all_to_all(aggregate, REP, 0, 0, tiled=True).reshape(n_rep, rows, feat_dev)
+    agg_rows = exchange(aggregate.reshape(n_rep, rows, feat_dev), REP, n_rep)
     preact = jnp.einsum("irf,ifo->ro", agg_rows, w_split, preferred_element_type=jnp.float32)
     gating = jax.nn.sigmoid(preact)
     activated = (preact * gating).astype(jnp.bfloat16)
@@ -114,7 +125,7 @@
     grad_split = jnp.einsum(
         "rf,jof->jro", grad_pre, w_split, preferred_element_type=jnp.float32
     ).astype(jnp.bfloat16)
-    grad_agg = lax.all_to_all(grad_split.reshape(n_rep * rows, feat_dev), REP, 0, 0, tiled=True)
+    grad_agg = exchange(grad_split, REP, n_rep).reshape(n_rep * rows, feat_dev)
     gathered_grad = hier_gather(grad_agg)
     feature_grad = block_product(adjacency_tiles, positions, gathered_grad)
     weight_part = jnp.einsum("irf,ro->ifo", agg_rows, grad_pre, preferred_element_type=jnp.float32)

time: 310 us -> 307 us (level)
  blocking collectives: 47.5 us -> 0 us
  waiting for transfers between devices: 179 us -> 208 us
  starting transfers between devices: 14.3 us -> 25.4 us
    ppermute x0 -> x8, waiting for transfers between devices: none -> 27.2 us  [the longest x2 17.7 us: hier_gather(): partner = lax.ppermute(x, 'xh', xor_pairs(2, 1))]
    all_gather x2 -> x0, blocking collectives: 27.1 us -> none  [hier_gather(): pair = lax.all_gather(x, 'xh', axis=0, tiled=True)]
    all_to_all x2 -> x0, blocking collectives: 20.5 us -> none  [the longest x1 10.7 us: local(): lax.all_to_all(aggregate, REP, 0, 0, tiled=True)]
    ppermute x0 -> x8, starting transfers between devices: none -> 11.4 us  [the longest x2 6.54 us: hier_gather(): partner = lax.ppermute(x, 'xh', xor_pairs(2, 1))]
  transfers between devices with their start and end apart: 9 -> 17, of which waited for: 9 -> 15; matrix products, arithmetic and copies ran while one was open for 1% -> 1% of each run, Pallas kernels for 0% -> 0%
where the time goes in v4:
time: 307 us
  waiting for transfers between devices  208 us (68%)
  Pallas kernels  48.2 us (16%)
  starting transfers between devices  25.4 us (8%)
  between operations  14.3 us (5%)
  other arithmetic  6.09 us (2%)
    all_gather x2, waiting for transfers between devices, hier_gather(): return lax.all_gather(pair, ('z', 'y'), axis=0, tiled=True)  121 us
    pallas_call x2, Pallas kernels, block_product(): pl.pallas_call(_product_kernel, grid_spec=pltpu.PrefetchScalarGridSpec(nu...  48.2 us
    ppermute x5, waiting for transfers between devices, butterfly_sum(): x = x + lax.ppermute(x, axis, xor_pairs(size, bit))  48.1 us
    ppermute x2, waiting for transfers between devices, hier_gather(): partner = lax.ppermute(x, 'xh', xor_pairs(2, 1))  17.7 us
    ppermute x2, waiting for transfers between devices, halving_scatter(): parts = keep + lax.ppermute(send, axis, xor_pairs(size, bit))  12.2 us
    ppermute x5, starting transfers between devices, butterfly_sum(): x = x + lax.ppermute(x, axis, xor_pairs(size, bit))  10.2 us
    ppermute x6, waiting for transfers between devices, exchange(): got.append(lax.ppermute(send, axis, xor_pairs(size, s)))  9.51 us
    ppermute x2, starting transfers between devices, hier_gather(): partner = lax.ppermute(x, 'xh', xor_pairs(2, 1))  6.54 us
  transfers between devices with their start and end apart: 17, of which 15 were waited for; matrix products, arithmetic and copies ran while one was open for 1% of the time, Pallas kernels for 0%

profile of v4, /device:TPU:1, one launch (start us, length us, event | category | flops | bytes accessed | tf_op | source)
XLA Modules:
  0.0 307.4 jit_solution(15975143108527936641)
XLA Ops:
  7.2 0.0 copy-start
  7.2 0.0 copy-start.1
  7.2 0.0 copy-start.2
  7.2 0.0 all-gather.3.cloned.1.call-start
  7.2 3.6 %collective-permute-start = (bf16[1536,128]{1,0:T(8,128)(2,1)}, bf16[1536,128]{1,0:T(8,128)(2,1)S(1)}, u32[]{:S(2)}, u32[]{:S(2)}) collective-permute-start(bf16[1536,128]{1,0:T(8,128)(2,1)} %param.8), channel_id=1, source_target_pairs={{0,16},{16,0},{1,17},{17,1},{2,18},{18,2},{3,19},{19,3},{4,20},{20... | collective-permute-start | bytes 1179656 | tf_op jit(solution)/shard_map/ppermute | solution.py:95
  10.9 8.6 %collective-permute-done = bf16[1536,128]{1,0:T(8,128)(2,1)S(1)} collective-permute-done((bf16[1536,128]{1,0:T(8,128)(2,1)}, bf16[1536,128]{1,0:T(8,128)(2,1)S(1)}, u32[]{:S(2)}, u32[]{:S(2)}) %collective-permute-start) | collective-permute-done | bytes 393248 | tf_op jit(solution)/shard_map/ppermute | solution.py:95
  19.5 2.0 pad_maximum_fusion
  21.5 0.0 all-gather.3.cloned.1.call-update
  21.6 0.0 all-gather.5.cloned.1.call-start
  21.6 0.0 copy-done.1
  21.6 0.4 select_reduce_fusion
  22.1 0.1 div.32
  22.2 0.1 rem.63
  22.3 0.1 ne.69
  22.4 0.6 pad_clamp_fusion
  23.0 0.6 fusion.9.pos_ref
  23.6 91.4 %all-gather.3.cloned.1.call-done = bf16[49152,128]{1,0:T(8,128)(2,1)} async-done(((bf16[3072,128]{1,0:T(8,128)(2,1)}), bf16[49152,128]{1,0:T(8,128)(2,1)}) %all-gather.3.cloned.1.call-update) | async-done | bytes 12582928 | tf_op jit(solution)/shard_map/all_gather | solution.py:97
  115.0 24.1 %shard_map.85 = bf16[12,128,128]{2,1,0:T(8,128)(2,1)} custom-call(s32[672]{0:T(1024)} %fusion.9.pos_ref, bf16[12,56,128,128]{3,2,1,0:T(8,128)(2,1)} %a_ref.3, bf16[384,128,128]{2,1,0:T(8,128)(2,1)} %bitcast.122, bf16[384,128,128]{2,1,0:T(8,128)(2,1)} %bitcast.150, bf16[384,128,128]{2,1,0:T(8,128)(2,1)} %bitcast.97, bf16[384,128,128]{2,1,0:T(8,128)(2,1)} %bitcast.98, ...), custom_call_target="tpu_custom_call" | custom-call | flops 2818572288 | bytes 44433408 | tf_op jit(solution)/shard_map/pallas_call | solution.py:40
  139.2 0.0 copy-start.3
  139.2 1.1 constant_dynamic-slice_fusion
  140.3 0.9 collective-permute-start.1
  141.2 1.2 collective-permute-start.2
  142.4 0.5 collective-permute-start.3
  142.9 0.0 collective-permute-done.1
  142.9 2.5 collective-permute-done.2
  145.5 2.4 collective-permute-done.3
  147.8 0.1 pad_maximum_fusion.2
  147.9 0.7 gather_fusion
  148.7 1.4 multiply_convert_fusion
  150.1 0.4 convolution_convert_fusion
  150.5 0.2 collective-permute-start.4
  150.8 1.2 collective-permute-start.5
  152.0 0.8 collective-permute-start.6
  152.8 0.0 collective-permute-done.4
  152.8 2.0 collective-permute-done.5
  154.7 2.6 collective-permute-done.6
  157.4 0.1 pad_maximum_fusion.3
  157.4 0.7 gather_fusion.1
  158.2 0.1 broadcast_select_fusion
  158.3 2.9 collective-permute-start.7
  161.2 9.1 %collective-permute-done.7 = bf16[1536,128]{1,0:T(8,128)(2,1)S(1)} collective-permute-done((bf16[1536,128]{1,0:T(8,128)(2,1)S(1)}, bf16[1536,128]{1,0:T(8,128)(2,1)S(1)}, u32[]{:S(2)}, u32[]{:S(2)}) %collective-permute-start.7) | collective-permute-done | bytes 393248 | tf_op jit(solution)/shard_map/ppermute | solution.py:95
  170.3 1.0 pad_maximum_fusion.1
  171.3 0.0 all-gather.5.cloned.1.call-update
  171.3 0.6 fusion
  171.9 0.1 slice_select_fusion
  172.0 1.7 collective-permute-start.8
  173.7 11.0 %collective-permute-done.8 = f32[2,128,512]{2,1,0:T(8,128)S(1)} collective-permute-done((f32[2,128,512]{2,1,0:T(8,128)S(1)}, f32[2,128,512]{2,1,0:T(8,128)S(1)}, u32[]{:S(2)}, u32[]{:S(2)}) %collective-permute-start.8) | collective-permute-done | bytes 524320 | tf_op jit(solution)/shard_map/ppermute | solution.py:76
  184.7 0.1 select_add_fusion
  184.9 1.9 collective-permute-start.9
  186.8 1.2 collective-permute-done.9
  188.0 0.1 add_bitcast_fusion
  188.1 1.1 collective-permute-start.10
  189.2 11.8 %collective-permute-done.10 = f32[128,512]{1,0:T(8,128)S(1)} collective-permute-done((f32[128,512]{1,0:T(8,128)S(1)}, f32[128,512]{1,0:T(8,128)S(1)}, u32[]{:S(2)}, u32[]{:S(2)}) %collective-permute-start.10) | collective-permute-done | bytes 262176 | tf_op jit(solution)/shard_map/ppermute | solution.py:62
  201.0 3.9 %collective-permute-start.11 = (f32[128,512]{1,0:T(8,128)S(1)}, f32[128,512]{1,0:T(8,128)S(1)}, u32[]{:S(2)}, u32[]{:S(2)}) collective-permute-start(f32[128,512]{1,0:T(8,128)S(1)} %add.102), channel_id=1, source_target_pairs={{0,8},{4,12},{8,0},{12,4},{16,24},{20,28},{24,16},{28,20},{32,40},... | collective-permute-start | bytes 786440 | tf_op jit(solution)/shard_map/ppermute | solution.py:62
  204.9 5.7 %collective-permute-done.11 = f32[128,512]{1,0:T(8,128)S(1)} collective-permute-done((f32[128,512]{1,0:T(8,128)S(1)}, f32[128,512]{1,0:T(8,128)S(1)}, u32[]{:S(2)}, u32[]{:S(2)}) %collective-permute-start.11) | collective-permute-done | bytes 262176 | tf_op jit(solution)/shard_map/ppermute | solution.py:62
  210.7 2.3 collective-permute-start.12
  213.0 5.6 %collective-permute-done.12 = f32[128,512]{1,0:T(8,128)S(1)} collective-permute-done((f32[128,512]{1,0:T(8,128)S(1)}, f32[128,512]{1,0:T(8,128)S(1)}, u32[]{:S(2)}, u32[]{:S(2)}) %collective-permute-start.12) | collective-permute-done | bytes 262176 | tf_op jit(solution)/shard_map/ppermute | solution.py:62
  218.6 0.9 collective-permute-start.13
  219.5 12.5 %collective-permute-done.13 = f32[128,512]{1,0:T(8,128)S(1)} collective-permute-done((f32[128,512]{1,0:T(8,128)S(1)}, f32[128,512]{1,0:T(8,128)S(1)}, u32[]{:S(2)}, u32[]{:S(2)}) %collective-permute-start.13) | collective-permute-done | bytes 262176 | tf_op jit(solution)/shard_map/ppermute | solution.py:62
  232.0 2.1 collective-permute-start.14
  234.1 12.5 %collective-permute-done.14 = f32[128,512]{1,0:T(8,128)S(1)} collective-permute-done((f32[128,512]{1,0:T(8,128)S(1)}, f32[128,512]{1,0:T(8,128)S(1)}, u32[]{:S(2)}, u32[]{:S(2)}) %collective-permute-start.14) | collective-permute-done | bytes 262176 | tf_op jit(solution)/shard_map/ppermute | solution.py:62
  246.6 0.7 add_multiply_fusion
  247.3 29.1 %all-gather.5.cloned.1.call-done = bf16[49152,128]{1,0:T(8,128)(2,1)} async-done(((bf16[3072,128]{1,0:T(8,128)(2,1)}), bf16[49152,128]{1,0:T(8,128)(2,1)}) %all-gather.5.cloned.1.call-update) | async-done | bytes 12582928 | tf_op jit(solution)/shard_map/all_gather | solution.py:97
  276.5 24.1 %shard_map.86 = bf16[12,128,128]{2,1,0:T(8,128)(2,1)} custom-call(s32[672]{0:T(1024)} %fusion.9.pos_ref, bf16[12,56,128,128]{3,2,1,0:T(8,128)(2,1)} %a_ref.3, bf16[384,128,128]{2,1,0:T(8,128)(2,1)} %bitcast.66, bf16[384,128,128]{2,1,0:T(8,128)(2,1)} %bitcast.94, bf16[384,128,128]{2,1,0:T(8,128)(2,1)} %bitcast.41, bf16[384,128,128]{2,1,0:T(8,128)(2,1)} %bitcast.42, ...), custom_call_target="tpu_custom_call" | custom-call | flops 2818572288 | bytes 44433408 | tf_op jit(solution)/shard_map/pallas_call | solution.py:40
  (13 shorter events, 0.3 us)
Async XLA Ops:
  7.2 141.5 %copy-start = (bf16[512,512]{1,0:T(8,128)(2,1)S(1)}, bf16[512,512]{1,0:T(8,128)(2,1)}, u32[]{:S(2)}) copy-start(bf16[512,512]{1,0:T(8,128)(2,1)} %param.9) | copy-start | bytes 1572868
  7.2 14.4 %copy-start.1 = (s32[12,56]{1,0:T(8,128)S(1)}, s32[12,56]{1,0:T(8,128)}, u32[]{:S(2)}) copy-start(s32[12,56]{1,0:T(8,128)} %param.12) | copy-start | bytes 8068
  7.2 14.4 %copy-start.2 = (s32[384]{0:T(512)S(1)}, s32[384]{0:T(512)}, u32[]{:S(2)}) copy-start(s32[384]{0:T(512)} %param.13) | copy-start | bytes 4612
  7.2 107.8 %all-gather.3.cloned.1.call-start = ((), (), s32[]{:S(2)}) async-start(), calls=%async_computation | async-start | bytes 13369344 | tf_op jit(solution)/shard_map/all_gather | solution.py:97
  7.2 12.3 %collective-permute-start = (bf16[1536,128]{1,0:T(8,128)(2,1)}, bf16[1536,128]{1,0:T(8,128)(2,1)S(1)}, u32[]{:S(2)}, u32[]{:S(2)}) collective-permute-start(bf16[1536,128]{1,0:T(8,128)(2,1)} %param.8), channel_id=1, source_target_pairs={{0,16},{16,0},{1,17},{17,1},{2,18},{18,2},{3,19},{19,3},{4,20},{20... | collective-permute-start | bytes 1179656 | tf_op jit(solution)/shard_map/ppermute | solution.py:95
  21.6 254.9 %all-gather.5.cloned.1.call-start = ((), (), s32[]{:S(2)}) async-start(), calls=%async_computation.1 | async-start | bytes 13369344 | tf_op jit(solution)/shard_map/all_gather | solution.py:97
  139.2 9.5 %copy-start.3 = (bf16[384,512]{1,0:T(8,128)(2,1)S(1)}, bf16[384,512]{1,0:T(8,128)(2,1)}, u32[]{:S(2)}) copy-start(bf16[384,512]{1,0:T(8,128)(2,1)} %param.10) | copy-start | bytes 1179652
  140.3 2.7 collective-permute-start.1
  141.2 4.3 %collective-permute-start.2 = (bf16[384,128]{1,0:T(8,128)(2,1)S(1)}, bf16[384,128]{1,0:T(8,128)(2,1)S(1)}, u32[]{:S(2)}, u32[]{:S(2)}) collective-permute-start(bf16[384,128]{1,0:T(8,128)(2,1)S(1)} %get-tuple-element.12), channel_id=1, source_target_pairs={{0,2},{1,3},{2,0},{3,1},{4,6},{5,7},{6,4},{7,5},{8,10},{9,11},{10,... | collective-permute-start | bytes 294920 | tf_op jit(solution)/shard_map/ppermute | solution.py:90
  142.4 5.4 %collective-permute-start.3 = (bf16[384,128]{1,0:T(8,128)(2,1)S(1)}, bf16[384,128]{1,0:T(8,128)(2,1)S(1)}, u32[]{:S(2)}, u32[]{:S(2)}) collective-permute-start(bf16[384,128]{1,0:T(8,128)(2,1)S(1)} %get-tuple-element.11), channel_id=1, source_target_pairs={{0,3},{1,2},{2,1},{3,0},{4,7},{5,6},{6,5},{7,4},{8,11},{9,10},{10,... | collective-permute-start | bytes 294920 | tf_op jit(solution)/shard_map/ppermute | solution.py:90
  150.5 2.2 collective-permute-start.4
  150.8 4.0 %collective-permute-start.5 = (bf16[384,128]{1,0:T(8,128)(2,1)S(1)}, bf16[384,128]{1,0:T(8,128)(2,1)S(1)}, u32[]{:S(2)}, u32[]{:S(2)}) collective-permute-start(bf16[384,128]{1,0:T(8,128)(2,1)S(1)} %get-tuple-element.8), channel_id=1, source_target_pairs={{0,2},{1,3},{2,0},{3,1},{4,6},{5,7},{6,4},{7,5},{8,10},{9,11},{10,... | collective-permute-start | bytes 294920 | tf_op jit(solution)/shard_map/ppermute | solution.py:90
  152.0 5.4 %collective-permute-start.6 = (bf16[384,128]{1,0:T(8,128)(2,1)S(1)}, bf16[384,128]{1,0:T(8,128)(2,1)S(1)}, u32[]{:S(2)}, u32[]{:S(2)}) collective-permute-start(bf16[384,128]{1,0:T(8,128)(2,1)S(1)} %get-tuple-element.7), channel_id=1, source_target_pairs={{0,3},{1,2},{2,1},{3,0},{4,7},{5,6},{6,5},{7,4},{8,11},{9,10},{10,... | collective-permute-start | bytes 294920 | tf_op jit(solution)/shard_map/ppermute | solution.py:90
  158.3 11.9 %collective-permute-start.7 = (bf16[1536,128]{1,0:T(8,128)(2,1)S(1)}, bf16[1536,128]{1,0:T(8,128)(2,1)S(1)}, u32[]{:S(2)}, u32[]{:S(2)}) collective-permute-start(bf16[1536,128]{1,0:T(8,128)(2,1)S(1)} %bitcast.151), channel_id=1, source_target_pairs={{0,16},{16,0},{1,17},{17,1},{2,18},{18,2},{3,19},{19,3},{4,20},{20... | collective-permute-start | bytes 1179656 | tf_op jit(solution)/shard_map/ppermute | solution.py:95
  172.0 12.8 %collective-permute-start.8 = (f32[2,128,512]{2,1,0:T(8,128)S(1)}, f32[2,128,512]{2,1,0:T(8,128)S(1)}, u32[]{:S(2)}, u32[]{:S(2)}) collective-permute-start(f32[2,128,512]{2,1,0:T(8,128)S(1)} %slice_select_fusion), channel_id=1, source_target_pairs={{0,2},{1,3},{2,0},{3,1},{4,6},{5,7},{6,4},{7,5},{8,10},{9,11},{10,... | collective-permute-start | bytes 1572872 | tf_op jit(solution)/shard_map/ppermute | solution.py:76
  184.9 3.1 %collective-permute-start.9 = (f32[1,128,512]{2,1,0:T(8,128)S(1)}, f32[1,128,512]{2,1,0:T(8,128)S(1)}, u32[]{:S(2)}, u32[]{:S(2)}) collective-permute-start(f32[1,128,512]{2,1,0:T(8,128)S(1)} %slice_select_fusion.1), channel_id=1, source_target_pairs={{0,1},{1,0},{2,3},{3,2},{4,5},{5,4},{6,7},{7,6},{8,9},{9,8},{10,11... | collective-permute-start | bytes 786440 | tf_op jit(solution)/shard_map/ppermute | solution.py:76
  188.1 12.9 %collective-permute-start.10 = (f32[128,512]{1,0:T(8,128)S(1)}, f32[128,512]{1,0:T(8,128)S(1)}, u32[]{:S(2)}, u32[]{:S(2)}) collective-permute-start(f32[128,512]{1,0:T(8,128)S(1)} %add_bitcast_fusion), channel_id=1, source_target_pairs={{0,4},{4,0},{8,12},{12,8},{16,20},{20,16},{24,28},{28,24},{32,36},... | collective-permute-start | bytes 786440 | tf_op jit(solution)/shard_map/ppermute | solution.py:62
  201.0 9.6 %collective-permute-start.11 = (f32[128,512]{1,0:T(8,128)S(1)}, f32[128,512]{1,0:T(8,128)S(1)}, u32[]{:S(2)}, u32[]{:S(2)}) collective-permute-start(f32[128,512]{1,0:T(8,128)S(1)} %add.102), channel_id=1, source_target_pairs={{0,8},{4,12},{8,0},{12,4},{16,24},{20,28},{24,16},{28,20},{32,40},... | collective-permute-start | bytes 786440 | tf_op jit(solution)/shard_map/ppermute | solution.py:62
  210.7 7.9 %collective-permute-start.12 = (f32[128,512]{1,0:T(8,128)S(1)}, f32[128,512]{1,0:T(8,128)S(1)}, u32[]{:S(2)}, u32[]{:S(2)}) collective-permute-start(f32[128,512]{1,0:T(8,128)S(1)} %add.103), channel_id=1, source_target_pairs={{0,16},{4,20},{8,24},{12,28},{16,0},{20,4},{24,8},{28,12},{32,48},... | collective-permute-start | bytes 786440 | tf_op jit(solution)/shard_map/ppermute | solution.py:62
  218.6 13.3 %collective-permute-start.13 = (f32[128,512]{1,0:T(8,128)S(1)}, f32[128,512]{1,0:T(8,128)S(1)}, u32[]{:S(2)}, u32[]{:S(2)}) collective-permute-start(f32[128,512]{1,0:T(8,128)S(1)} %add.104), channel_id=1, source_target_pairs={{0,32},{4,36},{8,40},{12,44},{16,48},{20,52},{24,56},{28,60},{32,0... | collective-permute-start | bytes 786440 | tf_op jit(solution)/shard_map/ppermute | solution.py:62
  232.0 14.6 %collective-permute-start.14 = (f32[128,512]{1,0:T(8,128)S(1)}, f32[128,512]{1,0:T(8,128)S(1)}, u32[]{:S(2)}, u32[]{:S(2)}) collective-permute-start(f32[128,512]{1,0:T(8,128)S(1)} %add.105), channel_id=1, source_target_pairs={{0,64},{4,68},{8,72},{12,76},{16,80},{20,84},{24,88},{28,92},{32,9... | collective-permute-start | bytes 786440 | tf_op jit(solution)/shard_map/ppermute | solution.py:62
Sparse Core Ops, SparseCore 0:
  21.7 93.3 all-gather.2
  171.4 105.0 all-gather.4

commit v5 on v4

--- a/solution.py
+++ b/solution.py
@@ -15,41 +15,66 @@
     return jnp.sum(jnp.where(matches, block_perm[None, None, :], 0), axis=-1)
 
 
-def _product_kernel(pos_ref, a_ref, *refs):
-    x_refs, o_ref = refs[:-1], refs[-1]
-    acc = jnp.zeros(o_ref.shape[1:], jnp.float32)
+def _product_kernel(has_init, pos_ref, use_ref, a_ref, *refs):
+    if has_init:
+        init_ref, refs = refs[0], refs[1:]
+    x_refs, o_ref, acc_ref = refs[:-2], refs[-2], refs[-1]
+    p = pl.program_id(0)
+    tiles = len(x_refs)
+    if has_init:
+        acc_ref[...] = init_ref[0]
+    else:
+        acc_ref[...] = jnp.zeros(acc_ref.shape, jnp.float32)
     for k, x_ref in enumerate(x_refs):
-        acc = acc + jnp.dot(a_ref[0, k], x_ref[0], preferred_element_type=jnp.float32)
-    o_ref[0] = acc.astype(o_ref.dtype)
+
+        @pl.when(use_ref[p * tiles + k] != 0)
+        def _():
+            acc_ref[...] += jnp.dot(a_ref[0, k], x_ref[0], preferred_element_type=jnp.float32)
+
+    o_ref[0] = acc_ref[...].astype(o_ref.dtype)
 
 
-def block_product(adjacency_tiles, positions, gathered):
+def block_product(adjacency_tiles, index, use, gathered, init, out_dtype):
     rows, tiles, bs, _ = adjacency_tiles.shape
     width = gathered.shape[1]
     blocks = gathered.reshape(-1, bs, width)
-    in_specs = [pl.BlockSpec((1, tiles, bs, bs), lambda p, pos: (p, 0, 0, 0))]
+    has_init = init is not None
+    in_specs = [pl.BlockSpec((1, tiles, bs, bs), lambda p, pos, use: (p, 0, 0, 0))]
+    operands = [adjacency_tiles]
+    if has_init:
+        in_specs.append(pl.BlockSpec((1, bs, width), lambda p, pos, use: (p, 0, 0)))
+        operands.append(init)
     for k in range(tiles):
         in_specs.append(
-            pl.BlockSpec((1, bs, width), lambda p, pos, k=k: (pos[p * tiles + k], 0, 0))
+            pl.BlockSpec((1, bs, width), lambda p, pos, use, k=k: (pos[p * tiles + k], 0, 0))
         )
+    operands += [blocks] * tiles
     cost = pl.CostEstimate(
-        flops=2 * rows * tiles * bs * bs * width,
-        bytes_accessed=2 * rows * tiles * bs * (bs + width) + 2 * rows * bs * width,
+        flops=rows * tiles * bs * bs * width,
+        bytes_accessed=2 * rows * tiles * bs * bs + rows * tiles * bs * width + 6 * rows * bs * width,
         transcendentals=0,
     )
     out = pl.pallas_call(
-        _product_kernel,
+        functools.partial(_product_kernel, has_init),
         grid_spec=pltpu.PrefetchScalarGridSpec(
-            num_scalar_prefetch=1,
+            num_scalar_prefetch=2,
             grid=(rows,),
             in_specs=in_specs,
-            out_specs=pl.BlockSpec((1, bs, width), lambda p, pos: (p, 0, 0)),
+            out_specs=pl.BlockSpec((1, bs, width), lambda p, pos, use: (p, 0, 0)),
+            scratch_shapes=[pltpu.VMEM((bs, width), jnp.float32)],
         ),
-        out_shape=jax.ShapeDtypeStruct((rows, bs, width), jnp.bfloat16),
+        out_shape=jax.ShapeDtypeStruct((rows, bs, width), out_dtype),
         compiler_params=pltpu.CompilerParams(dimension_semantics=("arbitrary",)),
         cost_estimate=cost,
-    )(positions.reshape(-1), adjacency_tiles, *([blocks] * tiles))
-    return out.reshape(rows * bs, width)
+    )(index.reshape(-1), use.reshape(-1), *operands)
+    return out
+
+
+def split_product(adjacency_tiles, plan, near, far):
+    near_index, near_use, far_index, far_use = plan
+    partial = block_product(adjacency_tiles, near_index, near_use, near, None, jnp.float32)
+    out = block_product(adjacency_tiles, far_index, far_use, far, partial, jnp.bfloat16)
+    return out.reshape(-1, near.shape[1])
 
 
 def xor_pairs(size, bit):
@@ -91,17 +116,25 @@
     return jnp.take(jnp.stack(got), jnp.arange(size) ^ me, axis=0)
 
 
-def hier_gather(x):
+def split_gather(x):
+    near = lax.all_gather(x, ("z", "y"), axis=0, tiled=True)
     partner = lax.ppermute(x, "xh", xor_pairs(2, 1))
-    pair = jnp.concatenate([x, partner], axis=0)
-    return lax.all_gather(pair, ("z", "y"), axis=0, tiled=True)
+    far = lax.all_gather(partner, ("z", "y"), axis=0, tiled=True)
+    return near, far
 
 
-def hier_positions(positions, local_blocks, n_xh, n_y):
+def split_plan(positions, local_blocks, n_xh, n_y):
     owner, block = positions // local_blocks, positions % local_blocks
     z, xh, y = owner // (n_xh * n_y), (owner // n_y) % n_xh, owner % n_y
-    slot = xh ^ lax.axis_index("xh")
-    return ((z * n_y + y) * n_xh + slot) * local_blocks + block
+    index = (z * n_y + y) * local_blocks + block
+    near = xh == lax.axis_index("xh")
+    zero = jnp.zeros_like(index)
+    return (
+        jnp.where(near, index, zero),
+        near.astype(jnp.int32),
+        jnp.where(near, zero, index),
+        (~near).astype(jnp.int32),
+    )
 
 
 def local(sizes, node_features, weight, cotangent, adjacency_tiles, block_cols, block_perm):
@@ -112,9 +145,8 @@
     bs = adjacency_tiles.shape[2]
     w_split = weight.reshape(n_rep, feat_dev, f_all)
     positions = column_positions(block_cols, block_perm)
-    positions = hier_positions(positions, node_features.shape[0] // bs, n_xh, n_y)
-    gathered = hier_gather(node_features)
-    aggregate = block_product(adjacency_tiles, positions, gathered)
+    plan = split_plan(positions, node_features.shape[0] // bs, n_xh, n_y)
+    aggregate = split_product(adjacency_tiles, plan, *split_gather(node_features))
     rows = aggregate.shape[0] // n_rep
     agg_rows = exchange(aggregate.reshape(n_rep, rows, feat_dev), REP, n_rep)
     preact = jnp.einsum("irf,ifo->ro", agg_rows, w_split, preferred_element_type=jnp.float32)
@@ -126,8 +158,7 @@
         "rf,jof->jro", grad_pre, w_split, preferred_element_type=jnp.float32
     ).astype(jnp.bfloat16)
     grad_agg = exchange(grad_split, REP, n_rep).reshape(n_rep * rows, feat_dev)
-    gathered_grad = hier_gather(grad_agg)
-    feature_grad = block_product(adjacency_tiles, positions, gathered_grad)
+    feature_grad = split_product(adjacency_tiles, plan, *split_gather(grad_agg))
     weight_part = jnp.einsum("irf,ro->ifo", agg_rows, grad_pre, preferred_element_type=jnp.float32)
     weight_rows = halving_scatter(weight_part, REP, n_rep)
     node_total = node_features.shape[0] * n_blk

time: 307 us -> 453 us (1.48); the launches traced: 307 us -> 446 us
  Pallas kernels: 48.2 us -> 263 us
  waiting for transfers between devices: 208 us -> 139 us
  starting transfers between devices: 25.4 us -> 17.1 us
    pallas_call x2 -> x4, Pallas kernels: 48.2 us -> 263 us  [block_product(): pl.pallas_call(functools.partial(_product_kernel, has_init), grid_spec=pl...]
    all_gather x2 -> x4, waiting for transfers between devices: 121 us -> 50.4 us  [the longest x2 49 us: split_gather(): near = lax.all_gather(x, ('z', 'y'), axis=0, tiled=True)]
    ppermute x5, starting transfers between devices: 10.2 us -> 3.13 us  [butterfly_sum(): x = x + lax.ppermute(x, axis, xor_pairs(size, bit))]
  transfers between devices with their start and end apart: 17 -> 19, of which waited for: 15 -> 15; matrix products, arithmetic and copies ran while one was open for 1% -> 1% of each run, Pallas kernels for 0% -> 28%
where the time goes in v5:
time: 453 us; the launch traced here: 446 us
  Pallas kernels  263 us (58%)
  waiting for transfers between devices  139 us (31%)
  starting transfers between devices  17.1 us (4%)
  between operations  14.1 us (3%)
  other arithmetic  6.34 us (1%)
    pallas_call x4, Pallas kernels, block_product(): pl.pallas_call(functools.partial(_product_kernel, has_init), grid_spec=pl...  263 us
    all_gather x2, waiting for transfers between devices, split_gather(): near = lax.all_gather(x, ('z', 'y'), axis=0, tiled=True)  49 us
    ppermute x5, waiting for transfers between devices, butterfly_sum(): x = x + lax.ppermute(x, axis, xor_pairs(size, bit))  46.7 us
    ppermute x2, waiting for transfers between devices, split_gather(): partner = lax.ppermute(x, 'xh', xor_pairs(2, 1))  19.2 us
    ppermute x2, waiting for transfers between devices, halving_scatter(): parts = keep + lax.ppermute(send, axis, xor_pairs(size, bit))  12.2 us
    ppermute x6, waiting for transfers between devices, exchange(): got.append(lax.ppermute(send, axis, xor_pairs(size, s)))  9.51 us
  transfers between devices with their start and end apart: 19, of which 15 were waited for; matrix products, arithmetic and copies ran while one was open for 1% of the time, Pallas kernels for 28%

profile of v5, /device:TPU:1, one launch (start us, length us, event | category | flops | bytes accessed | tf_op | source)
XLA Modules:
  0.0 446.1 jit_solution(17136229942853682477)
XLA Ops:
  7.2 0.0 all-gather.5.cloned.1.call-start
  7.2 0.7 all-gather.5.cloned.1.call-update
  7.9 0.0 all-gather.7.cloned.1.call-start
  8.0 3.6 collective-permute-start
  11.6 8.6 %collective-permute-done = bf16[1536,128]{1,0:T(8,128)(2,1)S(1)} collective-permute-done((bf16[1536,128]{1,0:T(8,128)(2,1)}, bf16[1536,128]{1,0:T(8,128)(2,1)S(1)}, u32[]{:S(2)}, u32[]{:S(2)}) %collective-permute-start) | collective-permute-done | bytes 393248 | tf_op jit(solution)/shard_map/ppermute | solution.py:121
  20.2 0.7 copy-done.2
  21.0 0.0 all-gather.9.cloned.1.call-start
  21.1 1.1 select_reduce_fusion
  22.2 0.1 div.35
  22.3 0.1 rem.75
  22.4 0.1 ne.93
  22.5 0.6 pad_clamp_fusion
  23.1 0.6 fusion.16
  23.8 0.6 not_convert_fusion.use_ref
  24.3 0.6 broadcast_select_fusion.4
  25.0 0.6 broadcast_select_fusion.5.pos_ref
  25.6 49.0 %all-gather.5.cloned.1.call-done = bf16[24576,128]{1,0:T(8,128)(2,1)} async-done(((bf16[1536,128]{1,0:T(8,128)(2,1)}), bf16[24576,128]{1,0:T(8,128)(2,1)}) %all-gather.5.cloned.1.call-update) | async-done | bytes 6291472 | tf_op jit(solution)/shard_map/all_gather | solution.py:120
  74.6 62.4 %shard_map.85.refs_0_ = f32[12,128,128]{2,1,0:T(8,128)} custom-call(s32[672]{0:T(1024)} %get-tuple-element.6.pos_ref, s32[672]{0:T(1024)} %get-tuple-element.4.use_ref, bf16[12,56,128,128]{3,2,1,0:T(8,128)(2,1)} %a_ref.7, bf16[192,128,128]{2,1,0:T(8,128)(2,1)} %bitcast.124, bf16[192,128,128]{2,1,0:T(8,128)(2,1)} %bitcast.152, ...), custom_call_target="tpu_custom_call" | custom-call | flops 1409286144 | bytes 34209792 | tf_op jit(solution)/shard_map/pallas_call | solution.py:57
  137.0 1.3 all-gather.7.cloned.1.call-done
  138.3 69.1 %shard_map.86 = bf16[12,128,128]{2,1,0:T(8,128)(2,1)} custom-call(s32[672]{0:T(1024)} %broadcast_select_fusion.5.pos_ref, s32[672]{0:T(1024)} %not_convert_fusion.use_ref, bf16[12,56,128,128]{3,2,1,0:T(8,128)(2,1)} %a_ref.7, f32[12,128,128]{2,1,0:T(8,128)} %shard_map.85.refs_0_, bf16[192,128,128]{2,1,0:T(8,128)(2,1)} %bitcast.236, ...), custom_call_target="tpu_custom_call" | custom-call | flops 1409286144 | bytes 34209792 | tf_op jit(solution)/shard_map/pallas_call | solution.py:57
  207.4 1.1 constant_dynamic-slice_fusion
  208.5 1.0 collective-permute-start.1
  209.5 1.2 collective-permute-start.2
  210.7 0.5 collective-permute-start.3
  211.2 2.5 collective-permute-done.2
  213.7 2.4 collective-permute-done.3
  216.1 0.1 pad_maximum_fusion
  216.2 0.7 gather_fusion
  216.9 1.4 multiply_convert_fusion
  218.4 0.4 convolution_convert_fusion
  218.8 0.2 collective-permute-start.4
  219.0 1.2 collective-permute-start.5
  220.2 0.8 collective-permute-start.6
  221.0 2.0 collective-permute-done.5
  223.0 2.7 collective-permute-done.6
  225.6 0.1 pad_maximum_fusion.1
  225.7 0.7 gather_fusion.1
  226.5 0.8 broadcast_select_fusion
  227.3 0.0 all-gather.11.cloned.1.call-start
  227.4 1.6 collective-permute-start.7
  229.0 10.6 %collective-permute-done.7 = bf16[1536,128]{1,0:T(8,128)(2,1)S(1)} collective-permute-done((bf16[1536,128]{1,0:T(8,128)(2,1)}, bf16[1536,128]{1,0:T(8,128)(2,1)S(1)}, u32[]{:S(2)}, u32[]{:S(2)}) %collective-permute-start.7) | collective-permute-done | bytes 393248 | tf_op jit(solution)/shard_map/ppermute | solution.py:121
  239.5 0.8 copy-done.1
  240.3 0.6 fusion
  240.9 0.1 slice_select_fusion
  241.0 1.7 collective-permute-start.8
  242.7 11.0 %collective-permute-done.8 = f32[2,128,512]{2,1,0:T(8,128)S(1)} collective-permute-done((f32[2,128,512]{2,1,0:T(8,128)S(1)}, f32[2,128,512]{2,1,0:T(8,128)S(1)}, u32[]{:S(2)}, u32[]{:S(2)}) %collective-permute-start.8) | collective-permute-done | bytes 524320 | tf_op jit(solution)/shard_map/ppermute | solution.py:101
  253.8 0.1 select_add_fusion
  254.0 1.9 collective-permute-start.9
  255.9 1.2 collective-permute-done.9
  257.1 0.1 add_bitcast_fusion
  257.1 0.1 collective-permute-start.10
  257.2 13.6 %collective-permute-done.10 = f32[128,512]{1,0:T(8,128)S(1)} collective-permute-done((f32[128,512]{1,0:T(8,128)S(1)}, f32[128,512]{1,0:T(8,128)S(1)}, u32[]{:S(2)}, u32[]{:S(2)}) %collective-permute-start.10) | collective-permute-done | bytes 262176 | tf_op jit(solution)/shard_map/ppermute | solution.py:87
  270.9 0.1 collective-permute-start.11
  270.9 15.1 %collective-permute-done.11 = f32[128,512]{1,0:T(8,128)S(1)} collective-permute-done((f32[128,512]{1,0:T(8,128)S(1)}, f32[128,512]{1,0:T(8,128)S(1)}, u32[]{:S(2)}, u32[]{:S(2)}) %collective-permute-start.11) | collective-permute-done | bytes 262176 | tf_op jit(solution)/shard_map/ppermute | solution.py:87
  286.1 0.1 collective-permute-start.12
  286.2 7.6 %collective-permute-done.12 = f32[128,512]{1,0:T(8,128)S(1)} collective-permute-done((f32[128,512]{1,0:T(8,128)S(1)}, f32[128,512]{1,0:T(8,128)S(1)}, u32[]{:S(2)}, u32[]{:S(2)}) %collective-permute-start.12) | collective-permute-done | bytes 262176 | tf_op jit(solution)/shard_map/ppermute | solution.py:87
  293.8 2.8 collective-permute-start.13
  296.6 3.8 collective-permute-done.13
  300.4 0.1 collective-permute-start.14
  300.5 6.7 %collective-permute-done.14 = f32[128,512]{1,0:T(8,128)S(1)} collective-permute-done((f32[128,512]{1,0:T(8,128)S(1)}, f32[128,512]{1,0:T(8,128)S(1)}, u32[]{:S(2)}, u32[]{:S(2)}) %collective-permute-start.14) | collective-permute-done | bytes 262176 | tf_op jit(solution)/shard_map/ppermute | solution.py:87
  307.2 0.7 add_multiply_fusion
  307.9 62.7 %shard_map.87.refs_0_ = f32[12,128,128]{2,1,0:T(8,128)} custom-call(s32[672]{0:T(1024)} %get-tuple-element.6.pos_ref, s32[672]{0:T(1024)} %get-tuple-element.4.use_ref, bf16[12,56,128,128]{3,2,1,0:T(8,128)(2,1)} %a_ref.7, bf16[192,128,128]{2,1,0:T(8,128)(2,1)} %bitcast.68, bf16[192,128,128]{2,1,0:T(8,128)(2,1)} %bitcast.96, bf16[192,128,128]{2,1,0:T(8,128)(2,1)} %bitcast.43, ...), custom_call_target="tpu_custom_call" | custom-call | flops 1409286144 | bytes 34209792 | tf_op jit(solution)/shard_map/pallas_call | solution.py:57
  370.6 0.0 all-gather.11.cloned.1.call-done
  370.6 68.9 %shard_map.88 = bf16[12,128,128]{2,1,0:T(8,128)(2,1)} custom-call(s32[672]{0:T(1024)} %broadcast_select_fusion.5.pos_ref, s32[672]{0:T(1024)} %not_convert_fusion.use_ref, bf16[12,56,128,128]{3,2,1,0:T(8,128)(2,1)} %a_ref.7, f32[12,128,128]{2,1,0:T(8,128)} %shard_map.87.refs_0_, bf16[192,128,128]{2,1,0:T(8,128)(2,1)} %bitcast.180, ...), custom_call_target="tpu_custom_call" | custom-call | flops 1409286144 | bytes 34209792 | tf_op jit(solution)/shard_map/pallas_call | solution.py:57
  (22 shorter events, 0.3 us)
Async XLA Ops:
  7.2 209.7 %copy-start = (bf16[512,512]{1,0:T(8,128)(2,1)S(1)}, bf16[512,512]{1,0:T(8,128)(2,1)}, u32[]{:S(2)}) copy-start(bf16[512,512]{1,0:T(8,128)(2,1)} %param.9) | copy-start | bytes 1572868
  7.2 67.4 %all-gather.5.cloned.1.call-start = ((), (), s32[]{:S(2)}) async-start(), calls=%async_computation | async-start | bytes 6684672 | tf_op jit(solution)/shard_map/all_gather | solution.py:120
  7.9 130.4 %all-gather.7.cloned.1.call-start = ((), (), s32[]{:S(2)}) async-start(), calls=%async_computation.1 | async-start | bytes 6684672 | tf_op jit(solution)/shard_map/all_gather | solution.py:122
  8.0 12.3 %collective-permute-start = (bf16[1536,128]{1,0:T(8,128)(2,1)}, bf16[1536,128]{1,0:T(8,128)(2,1)S(1)}, u32[]{:S(2)}, u32[]{:S(2)}) collective-permute-start(bf16[1536,128]{1,0:T(8,128)(2,1)} %param.8), channel_id=1, source_target_pairs={{0,16},{16,0},{1,17},{17,1},{2,18},{18,2},{3,19},{19,3},{4,20},{20... | collective-permute-start | bytes 1179656 | tf_op jit(solution)/shard_map/ppermute | solution.py:121
  20.2 0.7 copy-start.2
  21.0 286.9 %all-gather.9.cloned.1.call-start = ((), (), s32[]{:S(2)}) async-start(), calls=%async_computation.2 | async-start | bytes 6684672 | tf_op jit(solution)/shard_map/all_gather | solution.py:120
  138.3 78.6 %copy-start.3 = (bf16[384,512]{1,0:T(8,128)(2,1)S(1)}, bf16[384,512]{1,0:T(8,128)(2,1)}, u32[]{:S(2)}) copy-start(bf16[384,512]{1,0:T(8,128)(2,1)} %param.10) | copy-start | bytes 1179652
  208.5 2.7 collective-permute-start.1
  209.5 4.3 collective-permute-start.2
  210.7 5.4 %collective-permute-start.3 = (bf16[384,128]{1,0:T(8,128)(2,1)S(1)}, bf16[384,128]{1,0:T(8,128)(2,1)S(1)}, u32[]{:S(2)}, u32[]{:S(2)}) collective-permute-start(bf16[384,128]{1,0:T(8,128)(2,1)S(1)} %get-tuple-element.15), channel_id=1, source_target_pairs={{0,3},{1,2},{2,1},{3,0},{4,7},{5,6},{6,5},{7,4},{8,11},{9,10},{10,... | collective-permute-start | bytes 294920 | tf_op jit(solution)/shard_map/ppermute | solution.py:115
  218.8 2.2 collective-permute-start.4
  219.0 4.0 collective-permute-start.5
  220.2 5.4 %collective-permute-start.6 = (bf16[384,128]{1,0:T(8,128)(2,1)S(1)}, bf16[384,128]{1,0:T(8,128)(2,1)S(1)}, u32[]{:S(2)}, u32[]{:S(2)}) collective-permute-start(bf16[384,128]{1,0:T(8,128)(2,1)S(1)} %get-tuple-element.11), channel_id=1, source_target_pairs={{0,3},{1,2},{2,1},{3,0},{4,7},{5,6},{6,5},{7,4},{8,11},{9,10},{10,... | collective-permute-start | bytes 294920 | tf_op jit(solution)/shard_map/ppermute | solution.py:115
  227.3 143.3 %all-gather.11.cloned.1.call-start = ((), (), s32[]{:S(2)}) async-start(), calls=%async_computation.3 | async-start | bytes 6684672 | tf_op jit(solution)/shard_map/all_gather | solution.py:122
  227.4 12.2 %collective-permute-start.7 = (bf16[1536,128]{1,0:T(8,128)(2,1)}, bf16[1536,128]{1,0:T(8,128)(2,1)S(1)}, u32[]{:S(2)}, u32[]{:S(2)}) collective-permute-start(bf16[1536,128]{1,0:T(8,128)(2,1)} %bitcast.267), channel_id=1, source_target_pairs={{0,16},{16,0},{1,17},{17,1},{2,18},{18,2},{3,19},{19,3},{4,20},{20... | collective-permute-start | bytes 1179656 | tf_op jit(solution)/shard_map/ppermute | solution.py:121
  239.5 0.8 copy-start.1
  241.0 12.8 %collective-permute-start.8 = (f32[2,128,512]{2,1,0:T(8,128)S(1)}, f32[2,128,512]{2,1,0:T(8,128)S(1)}, u32[]{:S(2)}, u32[]{:S(2)}) collective-permute-start(f32[2,128,512]{2,1,0:T(8,128)S(1)} %slice_select_fusion), channel_id=1, source_target_pairs={{0,2},{1,3},{2,0},{3,1},{4,6},{5,7},{6,4},{7,5},{8,10},{9,11},{10,... | collective-permute-start | bytes 1572872 | tf_op jit(solution)/shard_map/ppermute | solution.py:101
  254.0 3.1 collective-permute-start.9
  257.1 13.7 %collective-permute-start.10 = (f32[128,512]{1,0:T(8,128)S(1)}, f32[128,512]{1,0:T(8,128)S(1)}, u32[]{:S(2)}, u32[]{:S(2)}) collective-permute-start(f32[128,512]{1,0:T(8,128)S(1)} %add_bitcast_fusion), channel_id=1, source_target_pairs={{0,4},{4,0},{8,12},{12,8},{16,20},{20,16},{24,28},{28,24},{32,36},... | collective-permute-start | bytes 786440 | tf_op jit(solution)/shard_map/ppermute | solution.py:87
  270.9 15.2 %collective-permute-start.11 = (f32[128,512]{1,0:T(8,128)S(1)}, f32[128,512]{1,0:T(8,128)S(1)}, u32[]{:S(2)}, u32[]{:S(2)}) collective-permute-start(f32[128,512]{1,0:T(8,128)S(1)} %add.111), channel_id=1, source_target_pairs={{0,8},{4,12},{8,0},{12,4},{16,24},{20,28},{24,16},{28,20},{32,40},... | collective-permute-start | bytes 786440 | tf_op jit(solution)/shard_map/ppermute | solution.py:87
  286.1 7.7 %collective-permute-start.12 = (f32[128,512]{1,0:T(8,128)S(1)}, f32[128,512]{1,0:T(8,128)S(1)}, u32[]{:S(2)}, u32[]{:S(2)}) collective-permute-start(f32[128,512]{1,0:T(8,128)S(1)} %add.112), channel_id=1, source_target_pairs={{0,16},{4,20},{8,24},{12,28},{16,0},{20,4},{24,8},{28,12},{32,48},... | collective-permute-start | bytes 786440 | tf_op jit(solution)/shard_map/ppermute | solution.py:87
  293.8 6.6 %collective-permute-start.13 = (f32[128,512]{1,0:T(8,128)S(1)}, f32[128,512]{1,0:T(8,128)S(1)}, u32[]{:S(2)}, u32[]{:S(2)}) collective-permute-start(f32[128,512]{1,0:T(8,128)S(1)} %add.113), channel_id=1, source_target_pairs={{0,32},{4,36},{8,40},{12,44},{16,48},{20,52},{24,56},{28,60},{32,0... | collective-permute-start | bytes 786440 | tf_op jit(solution)/shard_map/ppermute | solution.py:87
  300.4 6.8 %collective-permute-start.14 = (f32[128,512]{1,0:T(8,128)S(1)}, f32[128,512]{1,0:T(8,128)S(1)}, u32[]{:S(2)}, u32[]{:S(2)}) collective-permute-start(f32[128,512]{1,0:T(8,128)S(1)} %add.114), channel_id=1, source_target_pairs={{0,64},{4,68},{8,72},{12,76},{16,80},{20,84},{24,88},{28,92},{32,9... | collective-permute-start | bytes 786440 | tf_op jit(solution)/shard_map/ppermute | solution.py:87
Sparse Core Ops, SparseCore 0:
  10.1 64.4 all-gather.4
  77.3 60.9 all-gather.6
  227.5 69.0 all-gather.8
  298.6 59.6 all-gather.10

commit v6 on v4

--- a/solution.py
+++ b/solution.py
@@ -17,10 +17,9 @@
 
 def _product_kernel(pos_ref, a_ref, *refs):
     x_refs, o_ref = refs[:-1], refs[-1]
-    acc = jnp.zeros(o_ref.shape[1:], jnp.float32)
-    for k, x_ref in enumerate(x_refs):
-        acc = acc + jnp.dot(a_ref[0, k], x_ref[0], preferred_element_type=jnp.float32)
-    o_ref[0] = acc.astype(o_ref.dtype)
+    lhs = jnp.concatenate([a_ref[0, k] for k in range(len(x_refs))], axis=1)
+    rhs = jnp.concatenate([x_ref[0] for x_ref in x_refs], axis=0)
+    o_ref[0] = jnp.dot(lhs, rhs, preferred_element_type=jnp.float32).astype(o_ref.dtype)
 
 
 def block_product(adjacency_tiles, positions, gathered):

time: 307 us -> 307 us (level)
  no operation moved by 1% of the time
where the time goes in v6:
time: 307 us
  waiting for transfers between devices  205 us (67%)
  Pallas kernels  47.6 us (16%)
  starting transfers between devices  28.2 us (9%)
  between operations  14.3 us (5%)
  other arithmetic  6.09 us (2%)
    all_gather x2, waiting for transfers between devices, hier_gather(): return lax.all_gather(pair, ('z', 'y'), axis=0, tiled=True)  120 us
    pallas_call x2, Pallas kernels, block_product(): pl.pallas_call(_product_kernel, grid_spec=pltpu.PrefetchScalarGridSpec(nu...  47.6 us
    ppermute x5, waiting for transfers between devices, butterfly_sum(): x = x + lax.ppermute(x, axis, xor_pairs(size, bit))  46 us
    ppermute x2, waiting for transfers between devices, hier_gather(): partner = lax.ppermute(x, 'xh', xor_pairs(2, 1))  17.6 us
    ppermute x5, starting transfers between devices, butterfly_sum(): x = x + lax.ppermute(x, axis, xor_pairs(size, bit))  12.9 us
    ppermute x2, waiting for transfers between devices, halving_scatter(): parts = keep + lax.ppermute(send, axis, xor_pairs(size, bit))  12.1 us
    ppermute x6, waiting for transfers between devices, exchange(): got.append(lax.ppermute(send, axis, xor_pairs(size, s)))  9.51 us
    ppermute x2, starting transfers between devices, hier_gather(): partner = lax.ppermute(x, 'xh', xor_pairs(2, 1))  6.82 us
  transfers between devices with their start and end apart: 17, of which 15 were waited for; matrix products, arithmetic and copies ran while one was open for 1% of the time, Pallas kernels for 0%

profile of v6, /device:TPU:1, one launch (start us, length us, event | category | flops | bytes accessed | tf_op | source)
XLA Modules:
  0.0 306.8 jit_solution(10900649188877351838)
XLA Ops:
  7.2 0.0 copy-start
  7.2 0.0 copy-start.1
  7.2 0.0 copy-start.2
  7.2 0.0 all-gather.3.cloned.1.call-start
  7.2 3.6 %collective-permute-start = (bf16[1536,128]{1,0:T(8,128)(2,1)}, bf16[1536,128]{1,0:T(8,128)(2,1)S(1)}, u32[]{:S(2)}, u32[]{:S(2)}) collective-permute-start(bf16[1536,128]{1,0:T(8,128)(2,1)} %param.8), channel_id=1, source_target_pairs={{0,16},{16,0},{1,17},{17,1},{2,18},{18,2},{3,19},{19,3},{4,20},{20... | collective-permute-start | bytes 1179656 | tf_op jit(solution)/shard_map/ppermute | solution.py:94
  10.9 8.6 %collective-permute-done = bf16[1536,128]{1,0:T(8,128)(2,1)S(1)} collective-permute-done((bf16[1536,128]{1,0:T(8,128)(2,1)}, bf16[1536,128]{1,0:T(8,128)(2,1)S(1)}, u32[]{:S(2)}, u32[]{:S(2)}) %collective-permute-start) | collective-permute-done | bytes 393248 | tf_op jit(solution)/shard_map/ppermute | solution.py:94
  19.5 2.0 pad_maximum_fusion
  21.5 0.0 all-gather.3.cloned.1.call-update
  21.6 0.0 all-gather.5.cloned.1.call-start
  21.6 0.0 copy-done.1
  21.6 0.4 select_reduce_fusion
  22.1 0.1 div.32
  22.2 0.1 rem.63
  22.3 0.1 ne.69
  22.4 0.6 pad_clamp_fusion
  23.0 0.6 fusion.9.pos_ref
  23.6 91.4 %all-gather.3.cloned.1.call-done = bf16[49152,128]{1,0:T(8,128)(2,1)} async-done(((bf16[3072,128]{1,0:T(8,128)(2,1)}), bf16[49152,128]{1,0:T(8,128)(2,1)}) %all-gather.3.cloned.1.call-update) | async-done | bytes 12582928 | tf_op jit(solution)/shard_map/all_gather | solution.py:96
  115.0 23.8 %shard_map.85 = bf16[12,128,128]{2,1,0:T(8,128)(2,1)} custom-call(s32[672]{0:T(1024)} %fusion.9.pos_ref, bf16[12,56,128,128]{3,2,1,0:T(8,128)(2,1)} %a_ref.3, bf16[384,128,128]{2,1,0:T(8,128)(2,1)} %bitcast.122, bf16[384,128,128]{2,1,0:T(8,128)(2,1)} %bitcast.150, bf16[384,128,128]{2,1,0:T(8,128)(2,1)} %bitcast.97, bf16[384,128,128]{2,1,0:T(8,128)(2,1)} %bitcast.98, ...), custom_call_target="tpu_custom_call" | custom-call | flops 2818572288 | bytes 44433408 | tf_op jit(solution)/shard_map/pallas_call | solution.py:39
  138.8 0.0 copy-start.3
  138.8 1.1 constant_dynamic-slice_fusion
  140.0 0.9 collective-permute-start.1
  140.8 1.2 collective-permute-start.2
  142.1 0.5 collective-permute-start.3
  142.5 0.0 collective-permute-done.1
  142.6 2.5 collective-permute-done.2
  145.1 2.4 collective-permute-done.3
  147.4 0.1 pad_maximum_fusion.2
  147.5 0.7 gather_fusion
  148.3 1.4 multiply_convert_fusion
  149.7 0.4 convolution_convert_fusion
  150.1 0.2 collective-permute-start.4
  150.4 1.2 collective-permute-start.5
  151.6 0.8 collective-permute-start.6
  152.4 0.0 collective-permute-done.4
  152.4 2.0 collective-permute-done.5
  154.3 2.6 collective-permute-done.6
  157.0 0.1 pad_maximum_fusion.3
  157.0 0.7 gather_fusion.1
  157.8 0.1 broadcast_select_fusion
  157.9 3.2 %collective-permute-start.7 = (bf16[1536,128]{1,0:T(8,128)(2,1)S(1)}, bf16[1536,128]{1,0:T(8,128)(2,1)S(1)}, u32[]{:S(2)}, u32[]{:S(2)}) collective-permute-start(bf16[1536,128]{1,0:T(8,128)(2,1)S(1)} %bitcast.151), channel_id=1, source_target_pairs={{0,16},{16,0},{1,17},{17,1},{2,18},{18,2},{3,19},{19,3},{4,20},{20... | collective-permute-start | bytes 1179656 | tf_op jit(solution)/shard_map/ppermute | solution.py:94
  161.1 9.0 %collective-permute-done.7 = bf16[1536,128]{1,0:T(8,128)(2,1)S(1)} collective-permute-done((bf16[1536,128]{1,0:T(8,128)(2,1)S(1)}, bf16[1536,128]{1,0:T(8,128)(2,1)S(1)}, u32[]{:S(2)}, u32[]{:S(2)}) %collective-permute-start.7) | collective-permute-done | bytes 393248 | tf_op jit(solution)/shard_map/ppermute | solution.py:94
  170.1 1.0 pad_maximum_fusion.1
  171.1 0.0 all-gather.5.cloned.1.call-update
  171.1 0.6 fusion
  171.7 0.1 slice_select_fusion
  171.8 1.6 collective-permute-start.8
  173.4 11.0 %collective-permute-done.8 = f32[2,128,512]{2,1,0:T(8,128)S(1)} collective-permute-done((f32[2,128,512]{2,1,0:T(8,128)S(1)}, f32[2,128,512]{2,1,0:T(8,128)S(1)}, u32[]{:S(2)}, u32[]{:S(2)}) %collective-permute-start.8) | collective-permute-done | bytes 524320 | tf_op jit(solution)/shard_map/ppermute | solution.py:75
  184.3 0.1 select_add_fusion
  184.5 2.0 collective-permute-start.9
  186.5 1.2 collective-permute-done.9
  187.7 0.1 add_bitcast_fusion
  187.7 1.5 collective-permute-start.10
  189.2 11.4 %collective-permute-done.10 = f32[128,512]{1,0:T(8,128)S(1)} collective-permute-done((f32[128,512]{1,0:T(8,128)S(1)}, f32[128,512]{1,0:T(8,128)S(1)}, u32[]{:S(2)}, u32[]{:S(2)}) %collective-permute-start.10) | collective-permute-done | bytes 262176 | tf_op jit(solution)/shard_map/ppermute | solution.py:61
  200.6 4.0 %collective-permute-start.11 = (f32[128,512]{1,0:T(8,128)S(1)}, f32[128,512]{1,0:T(8,128)S(1)}, u32[]{:S(2)}, u32[]{:S(2)}) collective-permute-start(f32[128,512]{1,0:T(8,128)S(1)} %add.102), channel_id=1, source_target_pairs={{0,8},{4,12},{8,0},{12,4},{16,24},{20,28},{24,16},{28,20},{32,40},... | collective-permute-start | bytes 786440 | tf_op jit(solution)/shard_map/ppermute | solution.py:61
  204.6 5.5 %collective-permute-done.11 = f32[128,512]{1,0:T(8,128)S(1)} collective-permute-done((f32[128,512]{1,0:T(8,128)S(1)}, f32[128,512]{1,0:T(8,128)S(1)}, u32[]{:S(2)}, u32[]{:S(2)}) %collective-permute-start.11) | collective-permute-done | bytes 262176 | tf_op jit(solution)/shard_map/ppermute | solution.py:61
  210.2 3.2 %collective-permute-start.12 = (f32[128,512]{1,0:T(8,128)S(1)}, f32[128,512]{1,0:T(8,128)S(1)}, u32[]{:S(2)}, u32[]{:S(2)}) collective-permute-start(f32[128,512]{1,0:T(8,128)S(1)} %add.103), channel_id=1, source_target_pairs={{0,16},{4,20},{8,24},{12,28},{16,0},{20,4},{24,8},{28,12},{32,48},... | collective-permute-start | bytes 786440 | tf_op jit(solution)/shard_map/ppermute | solution.py:61
  213.4 4.8 %collective-permute-done.12 = f32[128,512]{1,0:T(8,128)S(1)} collective-permute-done((f32[128,512]{1,0:T(8,128)S(1)}, f32[128,512]{1,0:T(8,128)S(1)}, u32[]{:S(2)}, u32[]{:S(2)}) %collective-permute-start.12) | collective-permute-done | bytes 262176 | tf_op jit(solution)/shard_map/ppermute | solution.py:61
  218.3 2.0 collective-permute-start.13
  220.3 11.9 %collective-permute-done.13 = f32[128,512]{1,0:T(8,128)S(1)} collective-permute-done((f32[128,512]{1,0:T(8,128)S(1)}, f32[128,512]{1,0:T(8,128)S(1)}, u32[]{:S(2)}, u32[]{:S(2)}) %collective-permute-start.13) | collective-permute-done | bytes 262176 | tf_op jit(solution)/shard_map/ppermute | solution.py:61
  232.2 2.2 collective-permute-start.14
  234.4 12.4 %collective-permute-done.14 = f32[128,512]{1,0:T(8,128)S(1)} collective-permute-done((f32[128,512]{1,0:T(8,128)S(1)}, f32[128,512]{1,0:T(8,128)S(1)}, u32[]{:S(2)}, u32[]{:S(2)}) %collective-permute-start.14) | collective-permute-done | bytes 262176 | tf_op jit(solution)/shard_map/ppermute | solution.py:61
  246.8 0.7 add_multiply_fusion
  247.6 28.6 %all-gather.5.cloned.1.call-done = bf16[49152,128]{1,0:T(8,128)(2,1)} async-done(((bf16[3072,128]{1,0:T(8,128)(2,1)}), bf16[49152,128]{1,0:T(8,128)(2,1)}) %all-gather.5.cloned.1.call-update) | async-done | bytes 12582928 | tf_op jit(solution)/shard_map/all_gather | solution.py:96
  276.2 23.8 %shard_map.86 = bf16[12,128,128]{2,1,0:T(8,128)(2,1)} custom-call(s32[672]{0:T(1024)} %fusion.9.pos_ref, bf16[12,56,128,128]{3,2,1,0:T(8,128)(2,1)} %a_ref.3, bf16[384,128,128]{2,1,0:T(8,128)(2,1)} %bitcast.66, bf16[384,128,128]{2,1,0:T(8,128)(2,1)} %bitcast.94, bf16[384,128,128]{2,1,0:T(8,128)(2,1)} %bitcast.41, bf16[384,128,128]{2,1,0:T(8,128)(2,1)} %bitcast.42, ...), custom_call_target="tpu_custom_call" | custom-call | flops 2818572288 | bytes 44433408 | tf_op jit(solution)/shard_map/pallas_call | solution.py:39
  (13 shorter events, 0.3 us)
Async XLA Ops:
  7.2 141.1 %copy-start = (bf16[512,512]{1,0:T(8,128)(2,1)S(1)}, bf16[512,512]{1,0:T(8,128)(2,1)}, u32[]{:S(2)}) copy-start(bf16[512,512]{1,0:T(8,128)(2,1)} %param.9) | copy-start | bytes 1572868
  7.2 14.4 %copy-start.1 = (s32[12,56]{1,0:T(8,128)S(1)}, s32[12,56]{1,0:T(8,128)}, u32[]{:S(2)}) copy-start(s32[12,56]{1,0:T(8,128)} %param.12) | copy-start | bytes 8068
  7.2 14.4 %copy-start.2 = (s32[384]{0:T(512)S(1)}, s32[384]{0:T(512)}, u32[]{:S(2)}) copy-start(s32[384]{0:T(512)} %param.13) | copy-start | bytes 4612
  7.2 107.8 %all-gather.3.cloned.1.call-start = ((), (), s32[]{:S(2)}) async-start(), calls=%async_computation | async-start | bytes 13369344 | tf_op jit(solution)/shard_map/all_gather | solution.py:96
  7.2 12.3 %collective-permute-start = (bf16[1536,128]{1,0:T(8,128)(2,1)}, bf16[1536,128]{1,0:T(8,128)(2,1)S(1)}, u32[]{:S(2)}, u32[]{:S(2)}) collective-permute-start(bf16[1536,128]{1,0:T(8,128)(2,1)} %param.8), channel_id=1, source_target_pairs={{0,16},{16,0},{1,17},{17,1},{2,18},{18,2},{3,19},{19,3},{4,20},{20... | collective-permute-start | bytes 1179656 | tf_op jit(solution)/shard_map/ppermute | solution.py:94
  21.6 254.6 %all-gather.5.cloned.1.call-start = ((), (), s32[]{:S(2)}) async-start(), calls=%async_computation.1 | async-start | bytes 13369344 | tf_op jit(solution)/shard_map/all_gather | solution.py:96
  138.8 9.4 %copy-start.3 = (bf16[384,512]{1,0:T(8,128)(2,1)S(1)}, bf16[384,512]{1,0:T(8,128)(2,1)}, u32[]{:S(2)}) copy-start(bf16[384,512]{1,0:T(8,128)(2,1)} %param.10) | copy-start | bytes 1179652
  140.0 2.6 collective-permute-start.1
  140.8 4.3 %collective-permute-start.2 = (bf16[384,128]{1,0:T(8,128)(2,1)S(1)}, bf16[384,128]{1,0:T(8,128)(2,1)S(1)}, u32[]{:S(2)}, u32[]{:S(2)}) collective-permute-start(bf16[384,128]{1,0:T(8,128)(2,1)S(1)} %get-tuple-element.12), channel_id=1, source_target_pairs={{0,2},{1,3},{2,0},{3,1},{4,6},{5,7},{6,4},{7,5},{8,10},{9,11},{10,... | collective-permute-start | bytes 294920 | tf_op jit(solution)/shard_map/ppermute | solution.py:89
  142.1 5.4 %collective-permute-start.3 = (bf16[384,128]{1,0:T(8,128)(2,1)S(1)}, bf16[384,128]{1,0:T(8,128)(2,1)S(1)}, u32[]{:S(2)}, u32[]{:S(2)}) collective-permute-start(bf16[384,128]{1,0:T(8,128)(2,1)S(1)} %get-tuple-element.11), channel_id=1, source_target_pairs={{0,3},{1,2},{2,1},{3,0},{4,7},{5,6},{6,5},{7,4},{8,11},{9,10},{10,... | collective-permute-start | bytes 294920 | tf_op jit(solution)/shard_map/ppermute | solution.py:89
  150.1 2.2 collective-permute-start.4
  150.4 4.0 %collective-permute-start.5 = (bf16[384,128]{1,0:T(8,128)(2,1)S(1)}, bf16[384,128]{1,0:T(8,128)(2,1)S(1)}, u32[]{:S(2)}, u32[]{:S(2)}) collective-permute-start(bf16[384,128]{1,0:T(8,128)(2,1)S(1)} %get-tuple-element.8), channel_id=1, source_target_pairs={{0,2},{1,3},{2,0},{3,1},{4,6},{5,7},{6,4},{7,5},{8,10},{9,11},{10,... | collective-permute-start | bytes 294920 | tf_op jit(solution)/shard_map/ppermute | solution.py:89
  151.6 5.4 %collective-permute-start.6 = (bf16[384,128]{1,0:T(8,128)(2,1)S(1)}, bf16[384,128]{1,0:T(8,128)(2,1)S(1)}, u32[]{:S(2)}, u32[]{:S(2)}) collective-permute-start(bf16[384,128]{1,0:T(8,128)(2,1)S(1)} %get-tuple-element.7), channel_id=1, source_target_pairs={{0,3},{1,2},{2,1},{3,0},{4,7},{5,6},{6,5},{7,4},{8,11},{9,10},{10,... | collective-permute-start | bytes 294920 | tf_op jit(solution)/shard_map/ppermute | solution.py:89
  157.9 12.2 %collective-permute-start.7 = (bf16[1536,128]{1,0:T(8,128)(2,1)S(1)}, bf16[1536,128]{1,0:T(8,128)(2,1)S(1)}, u32[]{:S(2)}, u32[]{:S(2)}) collective-permute-start(bf16[1536,128]{1,0:T(8,128)(2,1)S(1)} %bitcast.151), channel_id=1, source_target_pairs={{0,16},{16,0},{1,17},{17,1},{2,18},{18,2},{3,19},{19,3},{4,20},{20... | collective-permute-start | bytes 1179656 | tf_op jit(solution)/shard_map/ppermute | solution.py:94
  171.8 12.5 %collective-permute-start.8 = (f32[2,128,512]{2,1,0:T(8,128)S(1)}, f32[2,128,512]{2,1,0:T(8,128)S(1)}, u32[]{:S(2)}, u32[]{:S(2)}) collective-permute-start(f32[2,128,512]{2,1,0:T(8,128)S(1)} %slice_select_fusion), channel_id=1, source_target_pairs={{0,2},{1,3},{2,0},{3,1},{4,6},{5,7},{6,4},{7,5},{8,10},{9,11},{10,... | collective-permute-start | bytes 1572872 | tf_op jit(solution)/shard_map/ppermute | solution.py:75
  184.5 3.2 %collective-permute-start.9 = (f32[1,128,512]{2,1,0:T(8,128)S(1)}, f32[1,128,512]{2,1,0:T(8,128)S(1)}, u32[]{:S(2)}, u32[]{:S(2)}) collective-permute-start(f32[1,128,512]{2,1,0:T(8,128)S(1)} %slice_select_fusion.1), channel_id=1, source_target_pairs={{0,1},{1,0},{2,3},{3,2},{4,5},{5,4},{6,7},{7,6},{8,9},{9,8},{10,11... | collective-permute-start | bytes 786440 | tf_op jit(solution)/shard_map/ppermute | solution.py:75
  187.7 12.8 %collective-permute-start.10 = (f32[128,512]{1,0:T(8,128)S(1)}, f32[128,512]{1,0:T(8,128)S(1)}, u32[]{:S(2)}, u32[]{:S(2)}) collective-permute-start(f32[128,512]{1,0:T(8,128)S(1)} %add_bitcast_fusion), channel_id=1, source_target_pairs={{0,4},{4,0},{8,12},{12,8},{16,20},{20,16},{24,28},{28,24},{32,36},... | collective-permute-start | bytes 786440 | tf_op jit(solution)/shard_map/ppermute | solution.py:61
  200.6 9.6 %collective-permute-start.11 = (f32[128,512]{1,0:T(8,128)S(1)}, f32[128,512]{1,0:T(8,128)S(1)}, u32[]{:S(2)}, u32[]{:S(2)}) collective-permute-start(f32[128,512]{1,0:T(8,128)S(1)} %add.102), channel_id=1, source_target_pairs={{0,8},{4,12},{8,0},{12,4},{16,24},{20,28},{24,16},{28,20},{32,40},... | collective-permute-start | bytes 786440 | tf_op jit(solution)/shard_map/ppermute | solution.py:61
  210.2 8.1 %collective-permute-start.12 = (f32[128,512]{1,0:T(8,128)S(1)}, f32[128,512]{1,0:T(8,128)S(1)}, u32[]{:S(2)}, u32[]{:S(2)}) collective-permute-start(f32[128,512]{1,0:T(8,128)S(1)} %add.103), channel_id=1, source_target_pairs={{0,16},{4,20},{8,24},{12,28},{16,0},{20,4},{24,8},{28,12},{32,48},... | collective-permute-start | bytes 786440 | tf_op jit(solution)/shard_map/ppermute | solution.py:61
  218.3 13.8 %collective-permute-start.13 = (f32[128,512]{1,0:T(8,128)S(1)}, f32[128,512]{1,0:T(8,128)S(1)}, u32[]{:S(2)}, u32[]{:S(2)}) collective-permute-start(f32[128,512]{1,0:T(8,128)S(1)} %add.104), channel_id=1, source_target_pairs={{0,32},{4,36},{8,40},{12,44},{16,48},{20,52},{24,56},{28,60},{32,0... | collective-permute-start | bytes 786440 | tf_op jit(solution)/shard_map/ppermute | solution.py:61
  232.2 14.6 %collective-permute-start.14 = (f32[128,512]{1,0:T(8,128)S(1)}, f32[128,512]{1,0:T(8,128)S(1)}, u32[]{:S(2)}, u32[]{:S(2)}) collective-permute-start(f32[128,512]{1,0:T(8,128)S(1)} %add.105), channel_id=1, source_target_pairs={{0,64},{4,68},{8,72},{12,76},{16,80},{20,84},{24,88},{28,92},{32,9... | collective-permute-start | bytes 786440 | tf_op jit(solution)/shard_map/ppermute | solution.py:61
Sparse Core Ops, SparseCore 0:
  21.7 93.3 all-gather.2
  171.2 104.8 all-gather.4

commit v7 on v6

--- a/solution.py
+++ b/solution.py
@@ -15,10 +15,11 @@
     return jnp.sum(jnp.where(matches, block_perm[None, None, :], 0), axis=-1)
 
 
-def _product_kernel(pos_ref, a_ref, *refs):
-    x_refs, o_ref = refs[:-1], refs[-1]
-    lhs = jnp.concatenate([a_ref[0, k] for k in range(len(x_refs))], axis=1)
-    rhs = jnp.concatenate([x_ref[0] for x_ref in x_refs], axis=0)
+def _product_kernel(pos_ref, a_ref, x_ref, o_ref):
+    p = pl.program_id(0)
+    tiles = a_ref.shape[1]
+    lhs = jnp.concatenate([a_ref[0, k] for k in range(tiles)], axis=1)
+    rhs = jnp.concatenate([x_ref[pos_ref[p * tiles + k]] for k in range(tiles)], axis=0)
     o_ref[0] = jnp.dot(lhs, rhs, preferred_element_type=jnp.float32).astype(o_ref.dtype)
 
 
@@ -26,14 +27,9 @@
     rows, tiles, bs, _ = adjacency_tiles.shape
     width = gathered.shape[1]
     blocks = gathered.reshape(-1, bs, width)
-    in_specs = [pl.BlockSpec((1, tiles, bs, bs), lambda p, pos: (p, 0, 0, 0))]
-    for k in range(tiles):
-        in_specs.append(
-            pl.BlockSpec((1, bs, width), lambda p, pos, k=k: (pos[p * tiles + k], 0, 0))
-        )
     cost = pl.CostEstimate(
         flops=2 * rows * tiles * bs * bs * width,
-        bytes_accessed=2 * rows * tiles * bs * (bs + width) + 2 * rows * bs * width,
+        bytes_accessed=2 * rows * tiles * bs * bs + 2 * blocks.size + 2 * rows * bs * width,
         transcendentals=0,
     )
     out = pl.pallas_call(
@@ -41,13 +37,18 @@
         grid_spec=pltpu.PrefetchScalarGridSpec(
             num_scalar_prefetch=1,
             grid=(rows,),
-            in_specs=in_specs,
+            in_specs=[
+                pl.BlockSpec((1, tiles, bs, bs), lambda p, pos: (p, 0, 0, 0)),
+                pl.BlockSpec(blocks.shape, lambda p, pos: (0, 0, 0), pipeline_mode=pl.Buffered(1)),
+            ],
             out_specs=pl.BlockSpec((1, bs, width), lambda p, pos: (p, 0, 0)),
         ),
         out_shape=jax.ShapeDtypeStruct((rows, bs, width), jnp.bfloat16),
-        compiler_params=pltpu.CompilerParams(dimension_semantics=("arbitrary",)),
+        compiler_params=pltpu.CompilerParams(
+            dimension_semantics=("arbitrary",), vmem_limit_bytes=48 * 1024 * 1024
+        ),
         cost_estimate=cost,
-    )(positions.reshape(-1), adjacency_tiles, *([blocks] * tiles))
+    )(positions.reshape(-1), adjacency_tiles, blocks)
     return out.reshape(rows * bs, width)
 
 

time: 307 us -> 296 us (0.964)
  Pallas kernels: 47.6 us -> 37.5 us
    pallas_call x2, Pallas kernels: 47.6 us -> 37.5 us  [block_product(): pl.pallas_call(_product_kernel, grid_spec=pltpu.PrefetchScalarGridSpec(nu...]
where the time goes in v7:
time: 296 us; the launch traced here: 295 us
  waiting for transfers between devices  208 us (70%)
  Pallas kernels  37.5 us (13%)
  starting transfers between devices  26.5 us (9%)
  between operations  14.3 us (5%)
  other arithmetic  4.91 us (2%)
    all_gather x2, waiting for transfers between devices, hier_gather(): return lax.all_gather(pair, ('z', 'y'), axis=0, tiled=True)  122 us
    ppermute x5, waiting for transfers between devices, butterfly_sum(): x = x + lax.ppermute(x, axis, xor_pairs(size, bit))  46.1 us
    pallas_call x2, Pallas kernels, block_product(): pl.pallas_call(_product_kernel, grid_spec=pltpu.PrefetchScalarGridSpec(nu...  37.5 us
    ppermute x2, waiting for transfers between devices, hier_gather(): partner = lax.ppermute(x, 'xh', xor_pairs(2, 1))  17.8 us
    ppermute x2, waiting for transfers between devices, halving_scatter(): parts = keep + lax.ppermute(send, axis, xor_pairs(size, bit))  12.2 us
    ppermute x5, starting transfers between devices, butterfly_sum(): x = x + lax.ppermute(x, axis, xor_pairs(size, bit))  11.5 us
    ppermute x6, waiting for transfers between devices, exchange(): got.append(lax.ppermute(send, axis, xor_pairs(size, s)))  9.51 us
    ppermute x2, starting transfers between devices, hier_gather(): partner = lax.ppermute(x, 'xh', xor_pairs(2, 1))  6.42 us
  transfers between devices with their start and end apart: 17, of which 15 were waited for; matrix products, arithmetic and copies ran while one was open for 1% of the time, Pallas kernels for 0%

profile of v7, /device:TPU:1, one launch (start us, length us, event | category | flops | bytes accessed | tf_op | source)
XLA Modules:
  0.0 295.1 jit_solution(3922989546902842082)
XLA Ops:
  7.2 0.0 copy-start
  7.2 0.0 copy-start.1
  7.2 0.0 copy-start.2
  7.2 0.0 all-gather.3.cloned.1.call-start
  7.2 3.6 %collective-permute-start = (bf16[1536,128]{1,0:T(8,128)(2,1)}, bf16[1536,128]{1,0:T(8,128)(2,1)S(1)}, u32[]{:S(2)}, u32[]{:S(2)}) collective-permute-start(bf16[1536,128]{1,0:T(8,128)(2,1)} %param.8), channel_id=1, source_target_pairs={{0,16},{16,0},{1,17},{17,1},{2,18},{18,2},{3,19},{19,3},{4,20},{20... | collective-permute-start | bytes 1179656 | tf_op jit(solution)/shard_map/ppermute | solution.py:95
  10.9 8.6 %collective-permute-done = bf16[1536,128]{1,0:T(8,128)(2,1)S(1)} collective-permute-done((bf16[1536,128]{1,0:T(8,128)(2,1)}, bf16[1536,128]{1,0:T(8,128)(2,1)S(1)}, u32[]{:S(2)}, u32[]{:S(2)}) %collective-permute-start) | collective-permute-done | bytes 393248 | tf_op jit(solution)/shard_map/ppermute | solution.py:95
  19.5 2.0 pad_maximum_fusion
  21.5 0.0 all-gather.3.cloned.1.call-update
  21.6 0.0 all-gather.5.cloned.1.call-start
  21.6 0.0 copy-done.1
  21.6 0.0 copy-done.2
  21.6 0.4 select_reduce_fusion
  22.1 0.1 div.32
  22.2 0.1 rem.63
  22.3 0.1 ne.69
  22.4 92.6 %all-gather.3.cloned.1.call-done = bf16[49152,128]{1,0:T(8,128)(2,1)} async-done(((bf16[3072,128]{1,0:T(8,128)(2,1)}), bf16[49152,128]{1,0:T(8,128)(2,1)}) %all-gather.3.cloned.1.call-update) | async-done | bytes 12582928 | tf_op jit(solution)/shard_map/all_gather | solution.py:97
  115.0 18.4 %shard_map.85 = bf16[12,128,128]{2,1,0:T(8,128)(2,1)S(1)} custom-call(s32[672]{0:T(1024)S(1)} %fusion.9.pos_ref, bf16[12,56,128,128]{3,2,1,0:T(8,128)(2,1)} %a_ref.3, bf16[384,128,128]{2,1,0:T(8,128)(2,1)} %bitcast.41), custom_call_target="tpu_custom_call" | custom-call | flops 2818572288 | bytes 34996224 | tf_op jit(solution)/shard_map/pallas_call | solution.py:35
  133.5 0.0 copy-start.3
  133.5 0.9 collective-permute-start.1
  134.4 1.2 collective-permute-start.2
  135.6 0.5 collective-permute-start.3
  136.2 0.0 collective-permute-done.1
  136.2 2.5 collective-permute-done.2
  138.7 2.4 collective-permute-done.3
  141.1 0.1 pad_maximum_fusion.2
  141.1 0.6 gather_fusion
  141.8 0.0 copy-done
  141.8 0.0 copy-done.3
  141.8 1.4 multiply_convert_fusion
  143.2 0.4 convolution_convert_fusion
  143.7 0.2 collective-permute-start.4
  143.9 1.2 collective-permute-start.5
  145.1 0.8 collective-permute-start.6
  145.9 0.0 collective-permute-done.4
  145.9 2.0 collective-permute-done.5
  147.8 2.6 collective-permute-done.6
  150.5 0.1 pad_maximum_fusion.3
  150.6 0.6 gather_fusion.1
  151.2 0.1 broadcast_select_fusion
  151.3 2.8 collective-permute-start.7
  154.1 9.2 %collective-permute-done.7 = bf16[1536,128]{1,0:T(8,128)(2,1)S(1)} collective-permute-done((bf16[1536,128]{1,0:T(8,128)(2,1)S(1)}, bf16[1536,128]{1,0:T(8,128)(2,1)S(1)}, u32[]{:S(2)}, u32[]{:S(2)}) %collective-permute-start.7) | collective-permute-done | bytes 393248 | tf_op jit(solution)/shard_map/ppermute | solution.py:95
  163.2 1.0 pad_maximum_fusion.1
  164.2 0.0 all-gather.5.cloned.1.call-update
  164.3 0.6 fusion
  164.9 0.1 slice_select_fusion
  164.9 1.7 collective-permute-start.8
  166.7 11.0 %collective-permute-done.8 = f32[2,128,512]{2,1,0:T(8,128)S(1)} collective-permute-done((f32[2,128,512]{2,1,0:T(8,128)S(1)}, f32[2,128,512]{2,1,0:T(8,128)S(1)}, u32[]{:S(2)}, u32[]{:S(2)}) %collective-permute-start.8) | collective-permute-done | bytes 524320 | tf_op jit(solution)/shard_map/ppermute | solution.py:76
  177.7 0.1 select_add_fusion
  177.9 1.9 collective-permute-start.9
  179.8 1.2 collective-permute-done.9
  181.0 0.1 add_bitcast_fusion
  181.1 1.3 collective-permute-start.10
  182.3 12.2 %collective-permute-done.10 = f32[128,512]{1,0:T(8,128)S(1)} collective-permute-done((f32[128,512]{1,0:T(8,128)S(1)}, f32[128,512]{1,0:T(8,128)S(1)}, u32[]{:S(2)}, u32[]{:S(2)}) %collective-permute-start.10) | collective-permute-done | bytes 262176 | tf_op jit(solution)/shard_map/ppermute | solution.py:62
  194.6 3.0 %collective-permute-start.11 = (f32[128,512]{1,0:T(8,128)S(1)}, f32[128,512]{1,0:T(8,128)S(1)}, u32[]{:S(2)}, u32[]{:S(2)}) collective-permute-start(f32[128,512]{1,0:T(8,128)S(1)} %add.102), channel_id=1, source_target_pairs={{0,8},{4,12},{8,0},{12,4},{16,24},{20,28},{24,16},{28,20},{32,40},... | collective-permute-start | bytes 786440 | tf_op jit(solution)/shard_map/ppermute | solution.py:62
  197.6 5.2 %collective-permute-done.11 = f32[128,512]{1,0:T(8,128)S(1)} collective-permute-done((f32[128,512]{1,0:T(8,128)S(1)}, f32[128,512]{1,0:T(8,128)S(1)}, u32[]{:S(2)}, u32[]{:S(2)}) %collective-permute-start.11) | collective-permute-done | bytes 262176 | tf_op jit(solution)/shard_map/ppermute | solution.py:62
  202.9 3.3 %collective-permute-start.12 = (f32[128,512]{1,0:T(8,128)S(1)}, f32[128,512]{1,0:T(8,128)S(1)}, u32[]{:S(2)}, u32[]{:S(2)}) collective-permute-start(f32[128,512]{1,0:T(8,128)S(1)} %add.103), channel_id=1, source_target_pairs={{0,16},{4,20},{8,24},{12,28},{16,0},{20,4},{24,8},{28,12},{32,48},... | collective-permute-start | bytes 786440 | tf_op jit(solution)/shard_map/ppermute | solution.py:62
  206.2 4.6 %collective-permute-done.12 = f32[128,512]{1,0:T(8,128)S(1)} collective-permute-done((f32[128,512]{1,0:T(8,128)S(1)}, f32[128,512]{1,0:T(8,128)S(1)}, u32[]{:S(2)}, u32[]{:S(2)}) %collective-permute-start.12) | collective-permute-done | bytes 262176 | tf_op jit(solution)/shard_map/ppermute | solution.py:62
  210.9 1.2 collective-permute-start.13
  212.1 12.1 %collective-permute-done.13 = f32[128,512]{1,0:T(8,128)S(1)} collective-permute-done((f32[128,512]{1,0:T(8,128)S(1)}, f32[128,512]{1,0:T(8,128)S(1)}, u32[]{:S(2)}, u32[]{:S(2)}) %collective-permute-start.13) | collective-permute-done | bytes 262176 | tf_op jit(solution)/shard_map/ppermute | solution.py:62
  224.2 2.7 collective-permute-start.14
  226.9 12.0 %collective-permute-done.14 = f32[128,512]{1,0:T(8,128)S(1)} collective-permute-done((f32[128,512]{1,0:T(8,128)S(1)}, f32[128,512]{1,0:T(8,128)S(1)}, u32[]{:S(2)}, u32[]{:S(2)}) %collective-permute-start.14) | collective-permute-done | bytes 262176 | tf_op jit(solution)/shard_map/ppermute | solution.py:62
  238.9 0.7 add_multiply_fusion
  239.6 29.6 %all-gather.5.cloned.1.call-done = bf16[49152,128]{1,0:T(8,128)(2,1)} async-done(((bf16[3072,128]{1,0:T(8,128)(2,1)}), bf16[49152,128]{1,0:T(8,128)(2,1)}) %all-gather.5.cloned.1.call-update) | async-done | bytes 12582928 | tf_op jit(solution)/shard_map/all_gather | solution.py:97
  269.2 19.1 %shard_map.86 = bf16[12,128,128]{2,1,0:T(8,128)(2,1)} custom-call(s32[672]{0:T(1024)S(1)} %fusion.9.pos_ref, bf16[12,56,128,128]{3,2,1,0:T(8,128)(2,1)} %a_ref.3, bf16[384,128,128]{2,1,0:T(8,128)(2,1)} %bitcast.40), custom_call_target="tpu_custom_call" | custom-call | flops 2818572288 | bytes 34996224 | tf_op jit(solution)/shard_map/pallas_call | solution.py:35
  (13 shorter events, 0.3 us)
Async XLA Ops:
  7.2 134.6 %copy-start = (bf16[512,512]{1,0:T(8,128)(2,1)S(1)}, bf16[512,512]{1,0:T(8,128)(2,1)}, u32[]{:S(2)}) copy-start(bf16[512,512]{1,0:T(8,128)(2,1)} %param.9) | copy-start | bytes 1572868
  7.2 14.4 %copy-start.1 = (s32[12,56]{1,0:T(8,128)S(1)}, s32[12,56]{1,0:T(8,128)}, u32[]{:S(2)}) copy-start(s32[12,56]{1,0:T(8,128)} %param.12) | copy-start | bytes 8068
  7.2 14.4 %copy-start.2 = (s32[384]{0:T(512)S(1)}, s32[384]{0:T(512)}, u32[]{:S(2)}) copy-start(s32[384]{0:T(512)} %param.13) | copy-start | bytes 4612
  7.2 107.8 %all-gather.3.cloned.1.call-start = ((), (), s32[]{:S(2)}) async-start(), calls=%async_computation | async-start | bytes 13369344 | tf_op jit(solution)/shard_map/all_gather | solution.py:97
  7.2 12.3 %collective-permute-start = (bf16[1536,128]{1,0:T(8,128)(2,1)}, bf16[1536,128]{1,0:T(8,128)(2,1)S(1)}, u32[]{:S(2)}, u32[]{:S(2)}) collective-permute-start(bf16[1536,128]{1,0:T(8,128)(2,1)} %param.8), channel_id=1, source_target_pairs={{0,16},{16,0},{1,17},{17,1},{2,18},{18,2},{3,19},{19,3},{4,20},{20... | collective-permute-start | bytes 1179656 | tf_op jit(solution)/shard_map/ppermute | solution.py:95
  21.6 247.6 %all-gather.5.cloned.1.call-start = ((), (), s32[]{:S(2)}) async-start(), calls=%async_computation.1 | async-start | bytes 13369344 | tf_op jit(solution)/shard_map/all_gather | solution.py:97
  133.5 8.3 %copy-start.3 = (bf16[384,512]{1,0:T(8,128)(2,1)S(1)}, bf16[384,512]{1,0:T(8,128)(2,1)}, u32[]{:S(2)}) copy-start(bf16[384,512]{1,0:T(8,128)(2,1)} %param.10) | copy-start | bytes 1179652
  133.5 2.7 collective-permute-start.1
  134.4 4.3 %collective-permute-start.2 = (bf16[384,128]{1,0:T(8,128)(2,1)S(1)}, bf16[384,128]{1,0:T(8,128)(2,1)S(1)}, u32[]{:S(2)}, u32[]{:S(2)}) collective-permute-start(bf16[384,128]{1,0:T(8,128)(2,1)S(1)} %get-tuple-element.12), channel_id=1, source_target_pairs={{0,2},{1,3},{2,0},{3,1},{4,6},{5,7},{6,4},{7,5},{8,10},{9,11},{10,... | collective-permute-start | bytes 294920 | tf_op jit(solution)/shard_map/ppermute | solution.py:90
  135.6 5.4 %collective-permute-start.3 = (bf16[384,128]{1,0:T(8,128)(2,1)S(1)}, bf16[384,128]{1,0:T(8,128)(2,1)S(1)}, u32[]{:S(2)}, u32[]{:S(2)}) collective-permute-start(bf16[384,128]{1,0:T(8,128)(2,1)S(1)} %get-tuple-element.11), channel_id=1, source_target_pairs={{0,3},{1,2},{2,1},{3,0},{4,7},{5,6},{6,5},{7,4},{8,11},{9,10},{10,... | collective-permute-start | bytes 294920 | tf_op jit(solution)/shard_map/ppermute | solution.py:90
  143.7 2.2 collective-permute-start.4
  143.9 4.0 %collective-permute-start.5 = (bf16[384,128]{1,0:T(8,128)(2,1)S(1)}, bf16[384,128]{1,0:T(8,128)(2,1)S(1)}, u32[]{:S(2)}, u32[]{:S(2)}) collective-permute-start(bf16[384,128]{1,0:T(8,128)(2,1)S(1)} %get-tuple-element.8), channel_id=1, source_target_pairs={{0,2},{1,3},{2,0},{3,1},{4,6},{5,7},{6,4},{7,5},{8,10},{9,11},{10,... | collective-permute-start | bytes 294920 | tf_op jit(solution)/shard_map/ppermute | solution.py:90
  145.1 5.4 %collective-permute-start.6 = (bf16[384,128]{1,0:T(8,128)(2,1)S(1)}, bf16[384,128]{1,0:T(8,128)(2,1)S(1)}, u32[]{:S(2)}, u32[]{:S(2)}) collective-permute-start(bf16[384,128]{1,0:T(8,128)(2,1)S(1)} %get-tuple-element.7), channel_id=1, source_target_pairs={{0,3},{1,2},{2,1},{3,0},{4,7},{5,6},{6,5},{7,4},{8,11},{9,10},{10,... | collective-permute-start | bytes 294920 | tf_op jit(solution)/shard_map/ppermute | solution.py:90
  151.3 11.9 %collective-permute-start.7 = (bf16[1536,128]{1,0:T(8,128)(2,1)S(1)}, bf16[1536,128]{1,0:T(8,128)(2,1)S(1)}, u32[]{:S(2)}, u32[]{:S(2)}) collective-permute-start(bf16[1536,128]{1,0:T(8,128)(2,1)S(1)} %bitcast.42), channel_id=1, source_target_pairs={{0,16},{16,0},{1,17},{17,1},{2,18},{18,2},{3,19},{19,3},{4,20},{20... | collective-permute-start | bytes 1179656 | tf_op jit(solution)/shard_map/ppermute | solution.py:95
  164.9 12.8 %collective-permute-start.8 = (f32[2,128,512]{2,1,0:T(8,128)S(1)}, f32[2,128,512]{2,1,0:T(8,128)S(1)}, u32[]{:S(2)}, u32[]{:S(2)}) collective-permute-start(f32[2,128,512]{2,1,0:T(8,128)S(1)} %slice_select_fusion), channel_id=1, source_target_pairs={{0,2},{1,3},{2,0},{3,1},{4,6},{5,7},{6,4},{7,5},{8,10},{9,11},{10,... | collective-permute-start | bytes 1572872 | tf_op jit(solution)/shard_map/ppermute | solution.py:76
  177.9 3.1 %collective-permute-start.9 = (f32[1,128,512]{2,1,0:T(8,128)S(1)}, f32[1,128,512]{2,1,0:T(8,128)S(1)}, u32[]{:S(2)}, u32[]{:S(2)}) collective-permute-start(f32[1,128,512]{2,1,0:T(8,128)S(1)} %slice_select_fusion.1), channel_id=1, source_target_pairs={{0,1},{1,0},{2,3},{3,2},{4,5},{5,4},{6,7},{7,6},{8,9},{9,8},{10,11... | collective-permute-start | bytes 786440 | tf_op jit(solution)/shard_map/ppermute | solution.py:76
  181.1 13.5 %collective-permute-start.10 = (f32[128,512]{1,0:T(8,128)S(1)}, f32[128,512]{1,0:T(8,128)S(1)}, u32[]{:S(2)}, u32[]{:S(2)}) collective-permute-start(f32[128,512]{1,0:T(8,128)S(1)} %add_bitcast_fusion), channel_id=1, source_target_pairs={{0,4},{4,0},{8,12},{12,8},{16,20},{20,16},{24,28},{28,24},{32,36},... | collective-permute-start | bytes 786440 | tf_op jit(solution)/shard_map/ppermute | solution.py:62
  194.6 8.2 %collective-permute-start.11 = (f32[128,512]{1,0:T(8,128)S(1)}, f32[128,512]{1,0:T(8,128)S(1)}, u32[]{:S(2)}, u32[]{:S(2)}) collective-permute-start(f32[128,512]{1,0:T(8,128)S(1)} %add.102), channel_id=1, source_target_pairs={{0,8},{4,12},{8,0},{12,4},{16,24},{20,28},{24,16},{28,20},{32,40},... | collective-permute-start | bytes 786440 | tf_op jit(solution)/shard_map/ppermute | solution.py:62
  202.9 8.0 %collective-permute-start.12 = (f32[128,512]{1,0:T(8,128)S(1)}, f32[128,512]{1,0:T(8,128)S(1)}, u32[]{:S(2)}, u32[]{:S(2)}) collective-permute-start(f32[128,512]{1,0:T(8,128)S(1)} %add.103), channel_id=1, source_target_pairs={{0,16},{4,20},{8,24},{12,28},{16,0},{20,4},{24,8},{28,12},{32,48},... | collective-permute-start | bytes 786440 | tf_op jit(solution)/shard_map/ppermute | solution.py:62
  210.9 13.3 %collective-permute-start.13 = (f32[128,512]{1,0:T(8,128)S(1)}, f32[128,512]{1,0:T(8,128)S(1)}, u32[]{:S(2)}, u32[]{:S(2)}) collective-permute-start(f32[128,512]{1,0:T(8,128)S(1)} %add.104), channel_id=1, source_target_pairs={{0,32},{4,36},{8,40},{12,44},{16,48},{20,52},{24,56},{28,60},{32,0... | collective-permute-start | bytes 786440 | tf_op jit(solution)/shard_map/ppermute | solution.py:62
  224.2 14.7 %collective-permute-start.14 = (f32[128,512]{1,0:T(8,128)S(1)}, f32[128,512]{1,0:T(8,128)S(1)}, u32[]{:S(2)}, u32[]{:S(2)}) collective-permute-start(f32[128,512]{1,0:T(8,128)S(1)} %add.105), channel_id=1, source_target_pairs={{0,64},{4,68},{8,72},{12,76},{16,80},{20,84},{24,88},{28,92},{32,9... | collective-permute-start | bytes 786440 | tf_op jit(solution)/shard_map/ppermute | solution.py:62
Sparse Core Ops, SparseCore 0:
  21.7 93.3 all-gather.2
  164.4 104.7 all-gather.4

commit v8 on v7

--- a/solution.py
+++ b/solution.py
@@ -82,12 +82,17 @@
 REP = ("xl", "c")
 
 
-def exchange(parts, axis, size):
-    me = lax.axis_index(axis)
-    got = [lax.dynamic_index_in_dim(parts, me, 0, keepdims=False)]
-    for s in range(1, size):
+def exchange(parts, size, far=False):
+    me = lax.axis_index(REP)
+    axis = ("xh",) + REP if far else REP
+    got = []
+    for s in range(size):
         send = lax.dynamic_index_in_dim(parts, me ^ s, 0, keepdims=False)
-        got.append(lax.ppermute(send, axis, xor_pairs(size, s)))
+        if far:
+            send = lax.ppermute(send, axis, xor_pairs(2 * size, size + s))
+        elif s:
+            send = lax.ppermute(send, axis, xor_pairs(size, s))
+        got.append(send)
     return jnp.take(jnp.stack(got), jnp.arange(size) ^ me, axis=0)
 
 
@@ -116,7 +121,7 @@
     gathered = hier_gather(node_features)
     aggregate = block_product(adjacency_tiles, positions, gathered)
     rows = aggregate.shape[0] // n_rep
-    agg_rows = exchange(aggregate.reshape(n_rep, rows, feat_dev), REP, n_rep)
+    agg_rows = exchange(aggregate.reshape(n_rep, rows, feat_dev), n_rep)
     preact = jnp.einsum("irf,ifo->ro", agg_rows, w_split, preferred_element_type=jnp.float32)
     gating = jax.nn.sigmoid(preact)
     activated = (preact * gating).astype(jnp.bfloat16)
@@ -125,8 +130,8 @@
     grad_split = jnp.einsum(
         "rf,jof->jro", grad_pre, w_split, preferred_element_type=jnp.float32
     ).astype(jnp.bfloat16)
-    grad_agg = exchange(grad_split, REP, n_rep).reshape(n_rep * rows, feat_dev)
-    gathered_grad = hier_gather(grad_agg)
+    pair = jnp.concatenate([exchange(grad_split, n_rep), exchange(grad_split, n_rep, far=True)])
+    gathered_grad = lax.all_gather(pair.reshape(-1, feat_dev), ("z", "y"), axis=0, tiled=True)
     feature_grad = block_product(adjacency_tiles, positions, gathered_grad)
     weight_part = jnp.einsum("irf,ro->ifo", agg_rows, grad_pre, preferred_element_type=jnp.float32)
     weight_rows = halving_scatter(weight_part, REP, n_rep)

time: 296 us -> 290 us (0.980)
  waiting for transfers between devices: 208 us -> 200 us
    all_gather x2 -> x1, waiting for transfers between devices: 122 us -> 91.9 us  [hier_gather(): return lax.all_gather(pair, ('z', 'y'), axis=0, tiled=True)]
    all_gather x0 -> x1, waiting for transfers between devices: none -> 27.7 us  [local(): lax.all_gather(pair.reshape(-1, feat_dev), ('z', 'y'), axis=0, tiled=True)]
    ppermute x2 -> x1, waiting for transfers between devices: 17.8 us -> 8.64 us  [hier_gather(): partner = lax.ppermute(x, 'xh', xor_pairs(2, 1))]
    ppermute x6 -> x10, starting transfers between devices: 4.87 us -> 10.2 us  [the longest x4 6.29 us: exchange(): send = lax.ppermute(send, axis, xor_pairs(2 * size, size + s))]
    ppermute x2 -> x1, starting transfers between devices: 6.42 us -> 3.64 us  [hier_gather(): partner = lax.ppermute(x, 'xh', xor_pairs(2, 1))]
    ppermute x6 -> x10, waiting for transfers between devices: 9.51 us -> 10.8 us  [the longest x4 5.87 us: exchange(): send = lax.ppermute(send, axis, xor_pairs(2 * size, size + s))]
  transfers between devices with their start and end apart: 17 -> 20, of which waited for: 15 -> 15; matrix products, arithmetic and copies ran while one was open for 1% -> 1% of each run, Pallas kernels for 0% -> 0%
where the time goes in v8:
time: 290 us; the launch traced here: 289 us
  waiting for transfers between devices  200 us (69%)
  Pallas kernels  37.5 us (13%)
  starting transfers between devices  26.4 us (9%)
  between operations  14.3 us (5%)
  other arithmetic  5.74 us (2%)
    all_gather x1, waiting for transfers between devices, hier_gather(): return lax.all_gather(pair, ('z', 'y'), axis=0, tiled=True)  91.9 us
    ppermute x5, waiting for transfers between devices, butterfly_sum(): x = x + lax.ppermute(x, axis, xor_pairs(size, bit))  47.4 us
    pallas_call x2, Pallas kernels, block_product(): pl.pallas_call(_product_kernel, grid_spec=pltpu.PrefetchScalarGridSpec(nu...  37.5 us
    all_gather x1, waiting for transfers between devices, local(): lax.all_gather(pair.reshape(-1, feat_dev), ('z', 'y'), axis=0, tiled=True)  27.7 us
    ppermute x2, waiting for transfers between devices, halving_scatter(): parts = keep + lax.ppermute(send, axis, xor_pairs(size, bit))  13.9 us
    ppermute x5, starting transfers between devices, butterfly_sum(): x = x + lax.ppermute(x, axis, xor_pairs(size, bit))  10.7 us
    ppermute x1, waiting for transfers between devices, hier_gather(): partner = lax.ppermute(x, 'xh', xor_pairs(2, 1))  8.64 us
    ppermute x4, starting transfers between devices, exchange(): send = lax.ppermute(send, axis, xor_pairs(2 * size, size + s))  6.29 us
  transfers between devices with their start and end apart: 20, of which 15 were waited for; matrix products, arithmetic and copies ran while one was open for 1% of the time, Pallas kernels for 0%

profile of v8, /device:TPU:1, one launch (start us, length us, event | category | flops | bytes accessed | tf_op | source)
XLA Modules:
  0.0 289.0 jit_solution(18072243303174413879)
XLA Ops:
  7.2 0.0 copy-start
  7.2 0.0 all-gather.3.cloned.1.call-start
  7.2 3.6 %collective-permute-start = (bf16[1536,128]{1,0:T(8,128)(2,1)}, bf16[1536,128]{1,0:T(8,128)(2,1)S(1)}, u32[]{:S(2)}, u32[]{:S(2)}) collective-permute-start(bf16[1536,128]{1,0:T(8,128)(2,1)} %param.8), channel_id=1, source_target_pairs={{0,16},{16,0},{1,17},{17,1},{2,18},{18,2},{3,19},{19,3},{4,20},{20... | collective-permute-start | bytes 1179656 | tf_op jit(solution)/shard_map/ppermute | solution.py:100
  10.9 8.6 %collective-permute-done = bf16[1536,128]{1,0:T(8,128)(2,1)S(1)} collective-permute-done((bf16[1536,128]{1,0:T(8,128)(2,1)}, bf16[1536,128]{1,0:T(8,128)(2,1)S(1)}, u32[]{:S(2)}, u32[]{:S(2)}) %collective-permute-start) | collective-permute-done | bytes 393248 | tf_op jit(solution)/shard_map/ppermute | solution.py:100
  19.5 2.0 pad_maximum_fusion
  21.5 0.0 all-gather.3.cloned.1.call-update
  21.5 0.0 all-gather.5.cloned.1.call-start
  21.6 1.1 select_reduce_fusion
  22.8 0.1 div.32
  22.8 0.1 rem.63
  22.9 0.1 ne.69
  23.1 91.9 %all-gather.3.cloned.1.call-done = bf16[49152,128]{1,0:T(8,128)(2,1)} async-done(((bf16[3072,128]{1,0:T(8,128)(2,1)}), bf16[49152,128]{1,0:T(8,128)(2,1)}) %all-gather.3.cloned.1.call-update) | async-done | bytes 12582928 | tf_op jit(solution)/shard_map/all_gather | solution.py:102
  115.0 18.4 %shard_map.85 = bf16[12,128,128]{2,1,0:T(8,128)(2,1)S(1)} custom-call(s32[672]{0:T(1024)S(1)} %fusion.9.pos_ref, bf16[12,56,128,128]{3,2,1,0:T(8,128)(2,1)} %a_ref.3, bf16[384,128,128]{2,1,0:T(8,128)(2,1)} %bitcast.47), custom_call_target="tpu_custom_call" | custom-call | flops 2818572288 | bytes 34996224 | tf_op jit(solution)/shard_map/pallas_call | solution.py:35
  133.5 0.9 collective-permute-start.1
  134.4 1.2 collective-permute-start.2
  135.6 0.5 collective-permute-start.3
  136.1 0.0 collective-permute-done.1
  136.1 2.5 collective-permute-done.2
  138.7 2.4 collective-permute-done.3
  141.0 0.1 pad_maximum_fusion.2
  141.1 0.6 gather_fusion
  141.7 1.4 multiply_convert_fusion
  143.2 0.4 convolution_convert_fusion
  143.6 0.1 dynamic-slice_bitcast_fusion.7
  143.6 2.8 collective-permute-start.7
  146.4 0.6 collective-permute-start.8
  147.0 2.4 collective-permute-start.9
  149.4 0.5 collective-permute-start.10
  149.9 0.1 collective-permute-start.4
  150.1 0.0 collective-permute-done.7
  150.1 0.6 collective-permute-start.5
  150.6 2.2 collective-permute-done.8
  152.8 0.6 collective-permute-start.6
  153.5 1.6 collective-permute-done.9
  155.0 2.1 collective-permute-done.10
  157.1 0.1 pad_maximum_fusion.4
  157.2 0.6 gather_fusion.2
  157.8 0.0 collective-permute-done.6
  157.8 0.1 pad_maximum_fusion.3
  157.9 0.6 gather_fusion.1
  158.5 0.1 broadcast_select_fusion.1
  158.7 1.0 pad_maximum_fusion.1
  159.7 0.0 all-gather.5.cloned.1.call-update
  159.7 0.6 fusion
  160.3 0.1 slice_select_fusion
  160.4 0.5 collective-permute-start.11
  160.9 12.8 %collective-permute-done.11 = f32[2,128,512]{2,1,0:T(8,128)S(1)} collective-permute-done((f32[2,128,512]{2,1,0:T(8,128)S(1)}, f32[2,128,512]{2,1,0:T(8,128)S(1)}, u32[]{:S(2)}, u32[]{:S(2)}) %collective-permute-start.11) | collective-permute-done | bytes 524320 | tf_op jit(solution)/shard_map/ppermute | solution.py:76
  173.7 0.1 select_add_fusion
  173.9 1.2 collective-permute-start.12
  175.1 1.2 collective-permute-done.12
  176.3 0.1 add_bitcast_fusion
  176.3 1.3 collective-permute-start.13
  177.6 12.2 %collective-permute-done.13 = f32[128,512]{1,0:T(8,128)S(1)} collective-permute-done((f32[128,512]{1,0:T(8,128)S(1)}, f32[128,512]{1,0:T(8,128)S(1)}, u32[]{:S(2)}, u32[]{:S(2)}) %collective-permute-start.13) | collective-permute-done | bytes 262176 | tf_op jit(solution)/shard_map/ppermute | solution.py:62
  189.8 2.6 collective-permute-start.14
  192.4 6.0 %collective-permute-done.14 = f32[128,512]{1,0:T(8,128)S(1)} collective-permute-done((f32[128,512]{1,0:T(8,128)S(1)}, f32[128,512]{1,0:T(8,128)S(1)}, u32[]{:S(2)}, u32[]{:S(2)}) %collective-permute-start.14) | collective-permute-done | bytes 262176 | tf_op jit(solution)/shard_map/ppermute | solution.py:62
  198.5 2.0 collective-permute-start.15
  200.4 5.7 %collective-permute-done.15 = f32[128,512]{1,0:T(8,128)S(1)} collective-permute-done((f32[128,512]{1,0:T(8,128)S(1)}, f32[128,512]{1,0:T(8,128)S(1)}, u32[]{:S(2)}, u32[]{:S(2)}) %collective-permute-start.15) | collective-permute-done | bytes 262176 | tf_op jit(solution)/shard_map/ppermute | solution.py:62
  206.2 1.7 collective-permute-start.16
  207.9 11.8 %collective-permute-done.16 = f32[128,512]{1,0:T(8,128)S(1)} collective-permute-done((f32[128,512]{1,0:T(8,128)S(1)}, f32[128,512]{1,0:T(8,128)S(1)}, u32[]{:S(2)}, u32[]{:S(2)}) %collective-permute-start.16) | collective-permute-done | bytes 262176 | tf_op jit(solution)/shard_map/ppermute | solution.py:62
  219.8 3.2 %collective-permute-start.17 = (f32[128,512]{1,0:T(8,128)S(1)}, f32[128,512]{1,0:T(8,128)S(1)}, u32[]{:S(2)}, u32[]{:S(2)}) collective-permute-start(f32[128,512]{1,0:T(8,128)S(1)} %add.110), channel_id=1, source_target_pairs={{0,64},{4,68},{8,72},{12,76},{16,80},{20,84},{24,88},{28,92},{32,9... | collective-permute-start | bytes 786440 | tf_op jit(solution)/shard_map/ppermute | solution.py:62
  222.9 11.7 %collective-permute-done.17 = f32[128,512]{1,0:T(8,128)S(1)} collective-permute-done((f32[128,512]{1,0:T(8,128)S(1)}, f32[128,512]{1,0:T(8,128)S(1)}, u32[]{:S(2)}, u32[]{:S(2)}) %collective-permute-start.17) | collective-permute-done | bytes 262176 | tf_op jit(solution)/shard_map/ppermute | solution.py:62
  234.6 0.7 add_multiply_fusion
  235.4 27.7 %all-gather.5.cloned.1.call-done = bf16[49152,128]{1,0:T(8,128)(2,1)} async-done(((bf16[3072,128]{1,0:T(8,128)(2,1)}), bf16[49152,128]{1,0:T(8,128)(2,1)}) %all-gather.5.cloned.1.call-update) | async-done | bytes 12582928 | tf_op jit(solution)/shard_map/all_gather | solution.py:134
  263.1 19.1 %shard_map.86 = bf16[12,128,128]{2,1,0:T(8,128)(2,1)} custom-call(s32[672]{0:T(1024)S(1)} %fusion.9.pos_ref, bf16[12,56,128,128]{3,2,1,0:T(8,128)(2,1)} %a_ref.3, bf16[384,128,128]{2,1,0:T(8,128)(2,1)} %bitcast.46), custom_call_target="tpu_custom_call" | custom-call | flops 2818572288 | bytes 34996224 | tf_op jit(solution)/shard_map/pallas_call | solution.py:35
  (17 shorter events, 0.3 us)
Async XLA Ops:
  7.2 134.6 %copy-start = (bf16[512,512]{1,0:T(8,128)(2,1)S(1)}, bf16[512,512]{1,0:T(8,128)(2,1)}, u32[]{:S(2)}) copy-start(bf16[512,512]{1,0:T(8,128)(2,1)} %param.9) | copy-start | bytes 1572868
  7.2 107.8 %all-gather.3.cloned.1.call-start = ((), (), s32[]{:S(2)}) async-start(), calls=%async_computation | async-start | bytes 13369344 | tf_op jit(solution)/shard_map/all_gather | solution.py:102
  7.2 12.3 %collective-permute-start = (bf16[1536,128]{1,0:T(8,128)(2,1)}, bf16[1536,128]{1,0:T(8,128)(2,1)S(1)}, u32[]{:S(2)}, u32[]{:S(2)}) collective-permute-start(bf16[1536,128]{1,0:T(8,128)(2,1)} %param.8), channel_id=1, source_target_pairs={{0,16},{16,0},{1,17},{17,1},{2,18},{18,2},{3,19},{19,3},{4,20},{20... | collective-permute-start | bytes 1179656 | tf_op jit(solution)/shard_map/ppermute | solution.py:100
  21.5 241.5 %all-gather.5.cloned.1.call-start = ((), (), s32[]{:S(2)}) async-start(), calls=%async_computation.1 | async-start | bytes 13369344 | tf_op jit(solution)/shard_map/all_gather | solution.py:134
  115.0 26.7 %copy-start.1 = (bf16[384,512]{1,0:T(8,128)(2,1)S(1)}, bf16[384,512]{1,0:T(8,128)(2,1)}, u32[]{:S(2)}) copy-start(bf16[384,512]{1,0:T(8,128)(2,1)} %param.10) | copy-start | bytes 1179652
  133.5 2.7 collective-permute-start.1
  134.4 4.3 %collective-permute-start.2 = (bf16[384,128]{1,0:T(8,128)(2,1)S(1)}, bf16[384,128]{1,0:T(8,128)(2,1)S(1)}, u32[]{:S(2)}, u32[]{:S(2)}) collective-permute-start(bf16[384,128]{1,0:T(8,128)(2,1)S(1)} %get-tuple-element.13), channel_id=1, source_target_pairs={{0,2},{1,3},{2,0},{3,1},{4,6},{5,7},{6,4},{7,5},{8,10},{9,11},{10,... | collective-permute-start | bytes 294920 | tf_op jit(solution)/shard_map/ppermute | solution.py:94
  135.6 5.4 %collective-permute-start.3 = (bf16[384,128]{1,0:T(8,128)(2,1)S(1)}, bf16[384,128]{1,0:T(8,128)(2,1)S(1)}, u32[]{:S(2)}, u32[]{:S(2)}) collective-permute-start(bf16[384,128]{1,0:T(8,128)(2,1)S(1)} %get-tuple-element.12), channel_id=1, source_target_pairs={{0,3},{1,2},{2,1},{3,0},{4,7},{5,6},{6,5},{7,4},{8,11},{9,10},{10,... | collective-permute-start | bytes 294920 | tf_op jit(solution)/shard_map/ppermute | solution.py:94
  143.6 6.4 %collective-permute-start.7 = (bf16[384,128]{1,0:T(8,128)(2,1)S(1)}, bf16[384,128]{1,0:T(8,128)(2,1)S(1)}, u32[]{:S(2)}, u32[]{:S(2)}) collective-permute-start(bf16[384,128]{1,0:T(8,128)(2,1)S(1)} %get-tuple-element.7), channel_id=1, source_target_pairs={{0,16},{1,17},{2,18},{3,19},{16,0},{17,1},{18,2},{19,3},{4,20},{5,... | collective-permute-start | bytes 294920 | tf_op jit(solution)/shard_map/ppermute | solution.py:92
  146.4 6.4 %collective-permute-start.8 = (bf16[384,128]{1,0:T(8,128)(2,1)S(1)}, bf16[384,128]{1,0:T(8,128)(2,1)S(1)}, u32[]{:S(2)}, u32[]{:S(2)}) collective-permute-start(bf16[384,128]{1,0:T(8,128)(2,1)S(1)} %get-tuple-element.10), channel_id=1, source_target_pairs={{0,17},{1,16},{2,19},{3,18},{16,1},{17,0},{18,3},{19,2},{4,21},{5,... | collective-permute-start | bytes 294920 | tf_op jit(solution)/shard_map/ppermute | solution.py:92
  147.0 8.0 %collective-permute-start.9 = (bf16[384,128]{1,0:T(8,128)(2,1)S(1)}, bf16[384,128]{1,0:T(8,128)(2,1)S(1)}, u32[]{:S(2)}, u32[]{:S(2)}) collective-permute-start(bf16[384,128]{1,0:T(8,128)(2,1)S(1)} %get-tuple-element.9), channel_id=1, source_target_pairs={{0,18},{1,19},{2,16},{3,17},{16,2},{17,3},{18,0},{19,1},{4,22},{5,... | collective-permute-start | bytes 294920 | tf_op jit(solution)/shard_map/ppermute | solution.py:92
  149.4 7.7 %collective-permute-start.10 = (bf16[384,128]{1,0:T(8,128)(2,1)S(1)}, bf16[384,128]{1,0:T(8,128)(2,1)S(1)}, u32[]{:S(2)}, u32[]{:S(2)}) collective-permute-start(bf16[384,128]{1,0:T(8,128)(2,1)S(1)} %get-tuple-element.8), channel_id=1, source_target_pairs={{0,19},{1,18},{2,17},{3,16},{16,3},{17,2},{18,1},{19,0},{4,23},{5,... | collective-permute-start | bytes 294920 | tf_op jit(solution)/shard_map/ppermute | solution.py:92
  149.9 7.9 %collective-permute-start.4 = (bf16[384,128]{1,0:T(8,128)(2,1)S(1)}, bf16[384,128]{1,0:T(8,128)(2,1)S(1)}, u32[]{:S(2)}, u32[]{:S(2)}) collective-permute-start(bf16[384,128]{1,0:T(8,128)(2,1)S(1)} %get-tuple-element.10), channel_id=1, source_target_pairs={{0,1},{1,0},{2,3},{3,2},{4,5},{5,4},{6,7},{7,6},{8,9},{9,8},{10,11... | collective-permute-start | bytes 294920 | tf_op jit(solution)/shard_map/ppermute | solution.py:94
  150.1 7.7 %collective-permute-start.5 = (bf16[384,128]{1,0:T(8,128)(2,1)S(1)}, bf16[384,128]{1,0:T(8,128)(2,1)S(1)}, u32[]{:S(2)}, u32[]{:S(2)}) collective-permute-start(bf16[384,128]{1,0:T(8,128)(2,1)S(1)} %get-tuple-element.9), channel_id=1, source_target_pairs={{0,2},{1,3},{2,0},{3,1},{4,6},{5,7},{6,4},{7,5},{8,10},{9,11},{10,... | collective-permute-start | bytes 294920 | tf_op jit(solution)/shard_map/ppermute | solution.py:94
  152.8 5.0 %collective-permute-start.6 = (bf16[384,128]{1,0:T(8,128)(2,1)S(1)}, bf16[384,128]{1,0:T(8,128)(2,1)S(1)}, u32[]{:S(2)}, u32[]{:S(2)}) collective-permute-start(bf16[384,128]{1,0:T(8,128)(2,1)S(1)} %get-tuple-element.8), channel_id=1, source_target_pairs={{0,3},{1,2},{2,1},{3,0},{4,7},{5,6},{6,5},{7,4},{8,11},{9,10},{10,... | collective-permute-start | bytes 294920 | tf_op jit(solution)/shard_map/ppermute | solution.py:94
  160.4 13.3 %collective-permute-start.11 = (f32[2,128,512]{2,1,0:T(8,128)S(1)}, f32[2,128,512]{2,1,0:T(8,128)S(1)}, u32[]{:S(2)}, u32[]{:S(2)}) collective-permute-start(f32[2,128,512]{2,1,0:T(8,128)S(1)} %slice_select_fusion), channel_id=1, source_target_pairs={{0,2},{1,3},{2,0},{3,1},{4,6},{5,7},{6,4},{7,5},{8,10},{9,11},{10,... | collective-permute-start | bytes 1572872 | tf_op jit(solution)/shard_map/ppermute | solution.py:76
  173.9 2.4 collective-permute-start.12
  176.3 13.5 %collective-permute-start.13 = (f32[128,512]{1,0:T(8,128)S(1)}, f32[128,512]{1,0:T(8,128)S(1)}, u32[]{:S(2)}, u32[]{:S(2)}) collective-permute-start(f32[128,512]{1,0:T(8,128)S(1)} %add_bitcast_fusion), channel_id=1, source_target_pairs={{0,4},{4,0},{8,12},{12,8},{16,20},{20,16},{24,28},{28,24},{32,36},... | collective-permute-start | bytes 786440 | tf_op jit(solution)/shard_map/ppermute | solution.py:62
  189.8 8.6 %collective-permute-start.14 = (f32[128,512]{1,0:T(8,128)S(1)}, f32[128,512]{1,0:T(8,128)S(1)}, u32[]{:S(2)}, u32[]{:S(2)}) collective-permute-start(f32[128,512]{1,0:T(8,128)S(1)} %add.107), channel_id=1, source_target_pairs={{0,8},{4,12},{8,0},{12,4},{16,24},{20,28},{24,16},{28,20},{32,40},... | collective-permute-start | bytes 786440 | tf_op jit(solution)/shard_map/ppermute | solution.py:62
  198.5 7.7 %collective-permute-start.15 = (f32[128,512]{1,0:T(8,128)S(1)}, f32[128,512]{1,0:T(8,128)S(1)}, u32[]{:S(2)}, u32[]{:S(2)}) collective-permute-start(f32[128,512]{1,0:T(8,128)S(1)} %add.108), channel_id=1, source_target_pairs={{0,16},{4,20},{8,24},{12,28},{16,0},{20,4},{24,8},{28,12},{32,48},... | collective-permute-start | bytes 786440 | tf_op jit(solution)/shard_map/ppermute | solution.py:62
  206.2 13.5 %collective-permute-start.16 = (f32[128,512]{1,0:T(8,128)S(1)}, f32[128,512]{1,0:T(8,128)S(1)}, u32[]{:S(2)}, u32[]{:S(2)}) collective-permute-start(f32[128,512]{1,0:T(8,128)S(1)} %add.109), channel_id=1, source_target_pairs={{0,32},{4,36},{8,40},{12,44},{16,48},{20,52},{24,56},{28,60},{32,0... | collective-permute-start | bytes 786440 | tf_op jit(solution)/shard_map/ppermute | solution.py:62
  219.8 14.9 %collective-permute-start.17 = (f32[128,512]{1,0:T(8,128)S(1)}, f32[128,512]{1,0:T(8,128)S(1)}, u32[]{:S(2)}, u32[]{:S(2)}) collective-permute-start(f32[128,512]{1,0:T(8,128)S(1)} %add.110), channel_id=1, source_target_pairs={{0,64},{4,68},{8,72},{12,76},{16,80},{20,84},{24,88},{28,92},{32,9... | collective-permute-start | bytes 786440 | tf_op jit(solution)/shard_map/ppermute | solution.py:62
Sparse Core Ops, SparseCore 0:
  21.7 93.3 all-gather.2
  159.8 103.1 all-gather.4

commit v9 on v8

--- a/solution.py
+++ b/solution.py
@@ -16,16 +16,19 @@
 
 
 def _product_kernel(pos_ref, a_ref, x_ref, o_ref):
-    p = pl.program_id(0)
-    tiles = a_ref.shape[1]
-    lhs = jnp.concatenate([a_ref[0, k] for k in range(tiles)], axis=1)
-    rhs = jnp.concatenate([x_ref[pos_ref[p * tiles + k]] for k in range(tiles)], axis=0)
-    o_ref[0] = jnp.dot(lhs, rhs, preferred_element_type=jnp.float32).astype(o_ref.dtype)
+    step = pl.program_id(0)
+    group, tiles = a_ref.shape[0], a_ref.shape[1]
+    for g in range(group):
+        base = (step * group + g) * tiles
+        lhs = jnp.concatenate([a_ref[g, k] for k in range(tiles)], axis=1)
+        rhs = jnp.concatenate([x_ref[pos_ref[base + k]] for k in range(tiles)], axis=0)
+        o_ref[g] = jnp.dot(lhs, rhs, preferred_element_type=jnp.float32).astype(o_ref.dtype)
 
 
 def block_product(adjacency_tiles, positions, gathered):
     rows, tiles, bs, _ = adjacency_tiles.shape
     width = gathered.shape[1]
+    group = 2 if rows % 2 == 0 else 1
     blocks = gathered.reshape(-1, bs, width)
     cost = pl.CostEstimate(
         flops=2 * rows * tiles * bs * bs * width,
@@ -36,12 +39,12 @@
         _product_kernel,
         grid_spec=pltpu.PrefetchScalarGridSpec(
             num_scalar_prefetch=1,
-            grid=(rows,),
+            grid=(rows // group,),
             in_specs=[
-                pl.BlockSpec((1, tiles, bs, bs), lambda p, pos: (p, 0, 0, 0)),
+                pl.BlockSpec((group, tiles, bs, bs), lambda p, pos: (p, 0, 0, 0)),
                 pl.BlockSpec(blocks.shape, lambda p, pos: (0, 0, 0), pipeline_mode=pl.Buffered(1)),
             ],
-            out_specs=pl.BlockSpec((1, bs, width), lambda p, pos: (p, 0, 0)),
+            out_specs=pl.BlockSpec((group, bs, width), lambda p, pos: (p, 0, 0)),
         ),
         out_shape=jax.ShapeDtypeStruct((rows, bs, width), jnp.bfloat16),
         compiler_params=pltpu.CompilerParams(
@@ -97,8 +100,9 @@
 
 
 def hier_gather(x):
-    partner = lax.ppermute(x, "xh", xor_pairs(2, 1))
-    pair = jnp.concatenate([x, partner], axis=0)
+    pieces = jnp.split(x, 4, axis=0)
+    partner = [lax.ppermute(piece, "xh", xor_pairs(2, 1)) for piece in pieces]
+    pair = jnp.concatenate([x] + partner, axis=0)
     return lax.all_gather(pair, ("z", "y"), axis=0, tiled=True)
 
 

time: 290 us -> 283 us (0.976)
  Pallas kernels: 37.5 us -> 31.2 us
  waiting for transfers between devices: 200 us -> 196 us
  local copies, waits for them, and re-layouts: 2.22 us -> 5.32 us
  starting transfers between devices: 26.4 us -> 29.4 us
    pallas_call x2, Pallas kernels: 37.5 us -> 31.2 us  [block_product(): pl.pallas_call(_product_kernel, grid_spec=pltpu.PrefetchScalarGridSpec(nu...]
    ppermute x1 -> x4, waiting for transfers between devices: 8.64 us -> 5.13 us  [hier_gather(): partner = [lax.ppermute(piece, 'xh', xor_pairs(2, 1)) for piece in pieces]]
    ppermute x1 -> x4, starting transfers between devices: 3.64 us -> 6.7 us  [hier_gather(): partner = [lax.ppermute(piece, 'xh', xor_pairs(2, 1)) for piece in pieces]]
  transfers between devices with their start and end apart: 20 -> 23, of which waited for: 15 -> 17; matrix products, arithmetic and copies ran while one was open for 1% -> 2% of each run, Pallas kernels for 0% -> 0%
where the time goes in v9:
time: 283 us
  waiting for transfers between devices  196 us (69%)
  Pallas kernels  31.2 us (11%)
  starting transfers between devices  29.4 us (10%)
  between operations  14.4 us (5%)
  local copies, waits for them, and re-layouts  5.32 us (2%)
  other arithmetic  3.69 us (1%)
    all_gather x1, waiting for transfers between devices, hier_gather(): return lax.all_gather(pair, ('z', 'y'), axis=0, tiled=True)  91 us
    ppermute x5, waiting for transfers between devices, butterfly_sum(): x = x + lax.ppermute(x, axis, xor_pairs(size, bit))  47.4 us
    pallas_call x2, Pallas kernels, block_product(): pl.pallas_call(_product_kernel, grid_spec=pltpu.PrefetchScalarGridSpec(nu...  31.2 us
    all_gather x1, waiting for transfers between devices, local(): lax.all_gather(pair.reshape(-1, feat_dev), ('z', 'y'), axis=0, tiled=True)  27.7 us
    ppermute x2, waiting for transfers between devices, halving_scatter(): parts = keep + lax.ppermute(send, axis, xor_pairs(size, bit))  13.9 us
    ppermute x5, starting transfers between devices, butterfly_sum(): x = x + lax.ppermute(x, axis, xor_pairs(size, bit))  10.7 us
    ppermute x4, starting transfers between devices, hier_gather(): partner = [lax.ppermute(piece, 'xh', xor_pairs(2, 1)) for piece in pieces]  6.7 us
    ppermute x4, starting transfers between devices, exchange(): send = lax.ppermute(send, axis, xor_pairs(2 * size, size + s))  6.29 us
  transfers between devices with their start and end apart: 23, of which 17 were waited for; matrix products, arithmetic and copies ran while one was open for 2% of the time, Pallas kernels for 0%

profile of v9, /device:TPU:1, one launch (start us, length us, event | category | flops | bytes accessed | tf_op | source)
XLA Modules:
  0.0 282.5 jit_solution(6028598839126409280)
XLA Ops:
  7.2 1.1 fusion.16
  8.3 3.6 %collective-permute-start = (bf16[384,128]{1,0:T(8,128)(2,1)S(1)}, bf16[384,128]{1,0:T(8,128)(2,1)S(1)}, u32[]{:S(2)}, u32[]{:S(2)}) collective-permute-start(bf16[384,128]{1,0:T(8,128)(2,1)S(1)} %get-tuple-element.18), channel_id=1, source_target_pairs={{0,16},{16,0},{1,17},{17,1},{2,18},{18,2},{3,19},{19,3},{4,20},{20... | collective-permute-start | bytes 294920 | tf_op jit(solution)/shard_map/ppermute | solution.py:104
  12.0 0.1 collective-permute-start.1
  12.1 2.9 %collective-permute-start.2 = (bf16[384,128]{1,0:T(8,128)(2,1)S(1)}, bf16[384,128]{1,0:T(8,128)(2,1)S(1)}, u32[]{:S(2)}, u32[]{:S(2)}) collective-permute-start(bf16[384,128]{1,0:T(8,128)(2,1)S(1)} %get-tuple-element.16), channel_id=1, source_target_pairs={{0,16},{16,0},{1,17},{17,1},{2,18},{18,2},{3,19},{19,3},{4,20},{20... | collective-permute-start | bytes 294920 | tf_op jit(solution)/shard_map/ppermute | solution.py:104
  15.0 0.1 collective-permute-start.3
  15.0 1.0 constant_dynamic-update-slice_fusion.4
  16.1 0.8 collective-permute-done.1
  17.0 2.0 collective-permute-done.2
  19.0 2.3 collective-permute-done.3
  21.3 0.9 copy-done.1
  22.2 0.0 all-gather.5.cloned.1.call-start
  22.3 1.1 select_reduce_fusion
  23.5 0.1 div.32
  23.5 0.1 rem.63
  23.6 0.1 ne.69
  23.8 91.0 %all-gather.3.cloned.1.call-done = bf16[49152,128]{1,0:T(8,128)(2,1)} async-done(((bf16[3072,128]{1,0:T(8,128)(2,1)}), bf16[49152,128]{1,0:T(8,128)(2,1)}) %all-gather.3.cloned.1.call-update) | async-done | bytes 12582928 | tf_op jit(solution)/shard_map/all_gather | solution.py:106
  114.9 15.3 %shard_map.85 = bf16[12,128,128]{2,1,0:T(8,128)(2,1)S(1)} custom-call(s32[672]{0:T(1024)S(1)} %fusion.9.pos_ref, bf16[12,56,128,128]{3,2,1,0:T(8,128)(2,1)} %a_ref.3, bf16[384,128,128]{2,1,0:T(8,128)(2,1)} %bitcast.47), custom_call_target="tpu_custom_call" | custom-call | flops 2818572288 | bytes 34996224 | tf_op jit(solution)/shard_map/pallas_call | solution.py:38
  130.2 0.9 collective-permute-start.4
  131.1 1.2 collective-permute-start.5
  132.3 0.5 collective-permute-start.6
  132.8 2.5 collective-permute-done.5
  135.4 2.4 collective-permute-done.6
  137.7 0.1 pad_maximum_fusion.1
  137.8 0.6 gather_fusion
  138.4 1.4 multiply_convert_fusion
  139.9 0.4 convolution_convert_fusion
  140.3 0.1 dynamic-slice_bitcast_fusion.7
  140.3 2.8 collective-permute-start.10
  143.1 0.6 collective-permute-start.11
  143.7 2.4 collective-permute-start.12
  146.1 0.5 collective-permute-start.13
  146.6 0.1 collective-permute-start.7
  146.8 0.6 collective-permute-start.8
  147.3 2.2 collective-permute-done.11
  149.5 0.6 collective-permute-start.9
  150.1 1.6 collective-permute-done.12
  151.7 2.1 collective-permute-done.13
  153.8 0.1 pad_maximum_fusion.3
  153.9 0.6 gather_fusion.2
  154.5 0.1 pad_maximum_fusion.2
  154.6 0.6 gather_fusion.1
  155.2 0.1 broadcast_select_fusion.1
  155.4 1.0 pad_maximum_fusion
  156.4 0.6 fusion
  157.0 0.1 slice_select_fusion
  157.1 0.5 collective-permute-start.14
  157.6 12.8 %collective-permute-done.14 = f32[2,128,512]{2,1,0:T(8,128)S(1)} collective-permute-done((f32[2,128,512]{2,1,0:T(8,128)S(1)}, f32[2,128,512]{2,1,0:T(8,128)S(1)}, u32[]{:S(2)}, u32[]{:S(2)}) %collective-permute-start.14) | collective-permute-done | bytes 524320 | tf_op jit(solution)/shard_map/ppermute | solution.py:79
  170.3 0.1 select_add_fusion
  170.5 1.2 collective-permute-start.15
  171.7 1.2 collective-permute-done.15
  172.9 0.1 add_bitcast_fusion
  173.0 1.3 collective-permute-start.16
  174.3 12.2 %collective-permute-done.16 = f32[128,512]{1,0:T(8,128)S(1)} collective-permute-done((f32[128,512]{1,0:T(8,128)S(1)}, f32[128,512]{1,0:T(8,128)S(1)}, u32[]{:S(2)}, u32[]{:S(2)}) %collective-permute-start.16) | collective-permute-done | bytes 262176 | tf_op jit(solution)/shard_map/ppermute | solution.py:65
  186.5 2.5 collective-permute-start.17
  189.0 6.0 %collective-permute-done.17 = f32[128,512]{1,0:T(8,128)S(1)} collective-permute-done((f32[128,512]{1,0:T(8,128)S(1)}, f32[128,512]{1,0:T(8,128)S(1)}, u32[]{:S(2)}, u32[]{:S(2)}) %collective-permute-start.17) | collective-permute-done | bytes 262176 | tf_op jit(solution)/shard_map/ppermute | solution.py:65
  195.1 2.0 collective-permute-start.18
  197.1 5.7 %collective-permute-done.18 = f32[128,512]{1,0:T(8,128)S(1)} collective-permute-done((f32[128,512]{1,0:T(8,128)S(1)}, f32[128,512]{1,0:T(8,128)S(1)}, u32[]{:S(2)}, u32[]{:S(2)}) %collective-permute-start.18) | collective-permute-done | bytes 262176 | tf_op jit(solution)/shard_map/ppermute | solution.py:65
  202.9 1.7 collective-permute-start.19
  204.6 11.8 %collective-permute-done.19 = f32[128,512]{1,0:T(8,128)S(1)} collective-permute-done((f32[128,512]{1,0:T(8,128)S(1)}, f32[128,512]{1,0:T(8,128)S(1)}, u32[]{:S(2)}, u32[]{:S(2)}) %collective-permute-start.19) | collective-permute-done | bytes 262176 | tf_op jit(solution)/shard_map/ppermute | solution.py:65
  216.4 3.2 %collective-permute-start.20 = (f32[128,512]{1,0:T(8,128)S(1)}, f32[128,512]{1,0:T(8,128)S(1)}, u32[]{:S(2)}, u32[]{:S(2)}) collective-permute-start(f32[128,512]{1,0:T(8,128)S(1)} %add.110), channel_id=1, source_target_pairs={{0,64},{4,68},{8,72},{12,76},{16,80},{20,84},{24,88},{28,92},{32,9... | collective-permute-start | bytes 786440 | tf_op jit(solution)/shard_map/ppermute | solution.py:65
  219.6 11.7 %collective-permute-done.20 = f32[128,512]{1,0:T(8,128)S(1)} collective-permute-done((f32[128,512]{1,0:T(8,128)S(1)}, f32[128,512]{1,0:T(8,128)S(1)}, u32[]{:S(2)}, u32[]{:S(2)}) %collective-permute-start.20) | collective-permute-done | bytes 262176 | tf_op jit(solution)/shard_map/ppermute | solution.py:65
  231.2 0.7 add_multiply_fusion
  232.0 27.7 %all-gather.5.cloned.1.call-done = bf16[49152,128]{1,0:T(8,128)(2,1)} async-done(((bf16[3072,128]{1,0:T(8,128)(2,1)}), bf16[49152,128]{1,0:T(8,128)(2,1)}) %all-gather.5.cloned.1.call-update) | async-done | bytes 12582928 | tf_op jit(solution)/shard_map/all_gather | solution.py:138
  259.7 16.0 %shard_map.86 = bf16[12,128,128]{2,1,0:T(8,128)(2,1)} custom-call(s32[672]{0:T(1024)S(1)} %fusion.9.pos_ref, bf16[12,56,128,128]{3,2,1,0:T(8,128)(2,1)} %a_ref.3, bf16[384,128,128]{2,1,0:T(8,128)(2,1)} %bitcast.46), custom_call_target="tpu_custom_call" | custom-call | flops 2818572288 | bytes 34996224 | tf_op jit(solution)/shard_map/pallas_call | solution.py:38
  (30 shorter events, 0.4 us)
Async XLA Ops:
  7.2 131.2 %copy-start = (bf16[512,512]{1,0:T(8,128)(2,1)S(1)}, bf16[512,512]{1,0:T(8,128)(2,1)}, u32[]{:S(2)}) copy-start(bf16[512,512]{1,0:T(8,128)(2,1)} %param.9) | copy-start | bytes 1572868
  7.2 107.7 %all-gather.3.cloned.1.call-start = ((), (), s32[]{:S(2)}) async-start(), calls=%async_computation | async-start | bytes 13369344 | tf_op jit(solution)/shard_map/all_gather | solution.py:106
  8.3 7.7 %collective-permute-start = (bf16[384,128]{1,0:T(8,128)(2,1)S(1)}, bf16[384,128]{1,0:T(8,128)(2,1)S(1)}, u32[]{:S(2)}, u32[]{:S(2)}) collective-permute-start(bf16[384,128]{1,0:T(8,128)(2,1)S(1)} %get-tuple-element.18), channel_id=1, source_target_pairs={{0,16},{16,0},{1,17},{17,1},{2,18},{18,2},{3,19},{19,3},{4,20},{20... | collective-permute-start | bytes 294920 | tf_op jit(solution)/shard_map/ppermute | solution.py:104
  12.0 5.0 %collective-permute-start.1 = (bf16[384,128]{1,0:T(8,128)(2,1)S(1)}, bf16[384,128]{1,0:T(8,128)(2,1)S(1)}, u32[]{:S(2)}, u32[]{:S(2)}) collective-permute-start(bf16[384,128]{1,0:T(8,128)(2,1)S(1)} %get-tuple-element.17), channel_id=1, source_target_pairs={{0,16},{16,0},{1,17},{17,1},{2,18},{18,2},{3,19},{19,3},{4,20},{20... | collective-permute-start | bytes 294920 | tf_op jit(solution)/shard_map/ppermute | solution.py:104
  12.1 6.9 %collective-permute-start.2 = (bf16[384,128]{1,0:T(8,128)(2,1)S(1)}, bf16[384,128]{1,0:T(8,128)(2,1)S(1)}, u32[]{:S(2)}, u32[]{:S(2)}) collective-permute-start(bf16[384,128]{1,0:T(8,128)(2,1)S(1)} %get-tuple-element.16), channel_id=1, source_target_pairs={{0,16},{16,0},{1,17},{17,1},{2,18},{18,2},{3,19},{19,3},{4,20},{20... | collective-permute-start | bytes 294920 | tf_op jit(solution)/shard_map/ppermute | solution.py:104
  15.0 6.3 %collective-permute-start.3 = (bf16[384,128]{1,0:T(8,128)(2,1)S(1)}, bf16[384,128]{1,0:T(8,128)(2,1)S(1)}, u32[]{:S(2)}, u32[]{:S(2)}) collective-permute-start(bf16[384,128]{1,0:T(8,128)(2,1)S(1)} %get-tuple-element.15), channel_id=1, source_target_pairs={{0,16},{16,0},{1,17},{17,1},{2,18},{18,2},{3,19},{19,3},{4,20},{20... | collective-permute-start | bytes 294920 | tf_op jit(solution)/shard_map/ppermute | solution.py:104
  21.3 0.9 copy-start.1
  22.2 237.5 %all-gather.5.cloned.1.call-start = ((), (), s32[]{:S(2)}) async-start(), calls=%async_computation.1 | async-start | bytes 13369344 | tf_op jit(solution)/shard_map/all_gather | solution.py:138
  114.9 23.6 %copy-start.2 = (bf16[384,512]{1,0:T(8,128)(2,1)S(1)}, bf16[384,512]{1,0:T(8,128)(2,1)}, u32[]{:S(2)}) copy-start(bf16[384,512]{1,0:T(8,128)(2,1)} %param.10) | copy-start | bytes 1179652
  130.2 2.7 collective-permute-start.4
  131.1 4.3 %collective-permute-start.5 = (bf16[384,128]{1,0:T(8,128)(2,1)S(1)}, bf16[384,128]{1,0:T(8,128)(2,1)S(1)}, u32[]{:S(2)}, u32[]{:S(2)}) collective-permute-start(bf16[384,128]{1,0:T(8,128)(2,1)S(1)} %get-tuple-element.13), channel_id=1, source_target_pairs={{0,2},{1,3},{2,0},{3,1},{4,6},{5,7},{6,4},{7,5},{8,10},{9,11},{10,... | collective-permute-start | bytes 294920 | tf_op jit(solution)/shard_map/ppermute | solution.py:97
  132.3 5.4 %collective-permute-start.6 = (bf16[384,128]{1,0:T(8,128)(2,1)S(1)}, bf16[384,128]{1,0:T(8,128)(2,1)S(1)}, u32[]{:S(2)}, u32[]{:S(2)}) collective-permute-start(bf16[384,128]{1,0:T(8,128)(2,1)S(1)} %get-tuple-element.12), channel_id=1, source_target_pairs={{0,3},{1,2},{2,1},{3,0},{4,7},{5,6},{6,5},{7,4},{8,11},{9,10},{10,... | collective-permute-start | bytes 294920 | tf_op jit(solution)/shard_map/ppermute | solution.py:97
  140.3 6.4 %collective-permute-start.10 = (bf16[384,128]{1,0:T(8,128)(2,1)S(1)}, bf16[384,128]{1,0:T(8,128)(2,1)S(1)}, u32[]{:S(2)}, u32[]{:S(2)}) collective-permute-start(bf16[384,128]{1,0:T(8,128)(2,1)S(1)} %get-tuple-element.7), channel_id=1, source_target_pairs={{0,16},{1,17},{2,18},{3,19},{16,0},{17,1},{18,2},{19,3},{4,20},{5,... | collective-permute-start | bytes 294920 | tf_op jit(solution)/shard_map/ppermute | solution.py:95
  143.1 6.4 %collective-permute-start.11 = (bf16[384,128]{1,0:T(8,128)(2,1)S(1)}, bf16[384,128]{1,0:T(8,128)(2,1)S(1)}, u32[]{:S(2)}, u32[]{:S(2)}) collective-permute-start(bf16[384,128]{1,0:T(8,128)(2,1)S(1)} %get-tuple-element.10), channel_id=1, source_target_pairs={{0,17},{1,16},{2,19},{3,18},{16,1},{17,0},{18,3},{19,2},{4,21},{5,... | collective-permute-start | bytes 294920 | tf_op jit(solution)/shard_map/ppermute | solution.py:95
  143.7 8.0 %collective-permute-start.12 = (bf16[384,128]{1,0:T(8,128)(2,1)S(1)}, bf16[384,128]{1,0:T(8,128)(2,1)S(1)}, u32[]{:S(2)}, u32[]{:S(2)}) collective-permute-start(bf16[384,128]{1,0:T(8,128)(2,1)S(1)} %get-tuple-element.9), channel_id=1, source_target_pairs={{0,18},{1,19},{2,16},{3,17},{16,2},{17,3},{18,0},{19,1},{4,22},{5,... | collective-permute-start | bytes 294920 | tf_op jit(solution)/shard_map/ppermute | solution.py:95
  146.1 7.7 %collective-permute-start.13 = (bf16[384,128]{1,0:T(8,128)(2,1)S(1)}, bf16[384,128]{1,0:T(8,128)(2,1)S(1)}, u32[]{:S(2)}, u32[]{:S(2)}) collective-permute-start(bf16[384,128]{1,0:T(8,128)(2,1)S(1)} %get-tuple-element.8), channel_id=1, source_target_pairs={{0,19},{1,18},{2,17},{3,16},{16,3},{17,2},{18,1},{19,0},{4,23},{5,... | collective-permute-start | bytes 294920 | tf_op jit(solution)/shard_map/ppermute | solution.py:95
  146.6 7.9 %collective-permute-start.7 = (bf16[384,128]{1,0:T(8,128)(2,1)S(1)}, bf16[384,128]{1,0:T(8,128)(2,1)S(1)}, u32[]{:S(2)}, u32[]{:S(2)}) collective-permute-start(bf16[384,128]{1,0:T(8,128)(2,1)S(1)} %get-tuple-element.10), channel_id=1, source_target_pairs={{0,1},{1,0},{2,3},{3,2},{4,5},{5,4},{6,7},{7,6},{8,9},{9,8},{10,11... | collective-permute-start | bytes 294920 | tf_op jit(solution)/shard_map/ppermute | solution.py:97
  146.8 7.7 %collective-permute-start.8 = (bf16[384,128]{1,0:T(8,128)(2,1)S(1)}, bf16[384,128]{1,0:T(8,128)(2,1)S(1)}, u32[]{:S(2)}, u32[]{:S(2)}) collective-permute-start(bf16[384,128]{1,0:T(8,128)(2,1)S(1)} %get-tuple-element.9), channel_id=1, source_target_pairs={{0,2},{1,3},{2,0},{3,1},{4,6},{5,7},{6,4},{7,5},{8,10},{9,11},{10,... | collective-permute-start | bytes 294920 | tf_op jit(solution)/shard_map/ppermute | solution.py:97
  149.5 5.0 %collective-permute-start.9 = (bf16[384,128]{1,0:T(8,128)(2,1)S(1)}, bf16[384,128]{1,0:T(8,128)(2,1)S(1)}, u32[]{:S(2)}, u32[]{:S(2)}) collective-permute-start(bf16[384,128]{1,0:T(8,128)(2,1)S(1)} %get-tuple-element.8), channel_id=1, source_target_pairs={{0,3},{1,2},{2,1},{3,0},{4,7},{5,6},{6,5},{7,4},{8,11},{9,10},{10,... | collective-permute-start | bytes 294920 | tf_op jit(solution)/shard_map/ppermute | solution.py:97
  157.1 13.3 %collective-permute-start.14 = (f32[2,128,512]{2,1,0:T(8,128)S(1)}, f32[2,128,512]{2,1,0:T(8,128)S(1)}, u32[]{:S(2)}, u32[]{:S(2)}) collective-permute-start(f32[2,128,512]{2,1,0:T(8,128)S(1)} %slice_select_fusion), channel_id=1, source_target_pairs={{0,2},{1,3},{2,0},{3,1},{4,6},{5,7},{6,4},{7,5},{8,10},{9,11},{10,... | collective-permute-start | bytes 1572872 | tf_op jit(solution)/shard_map/ppermute | solution.py:79
  170.5 2.4 collective-permute-start.15
  173.0 13.5 %collective-permute-start.16 = (f32[128,512]{1,0:T(8,128)S(1)}, f32[128,512]{1,0:T(8,128)S(1)}, u32[]{:S(2)}, u32[]{:S(2)}) collective-permute-start(f32[128,512]{1,0:T(8,128)S(1)} %add_bitcast_fusion), channel_id=1, source_target_pairs={{0,4},{4,0},{8,12},{12,8},{16,20},{20,16},{24,28},{28,24},{32,36},... | collective-permute-start | bytes 786440 | tf_op jit(solution)/shard_map/ppermute | solution.py:65
  186.5 8.6 %collective-permute-start.17 = (f32[128,512]{1,0:T(8,128)S(1)}, f32[128,512]{1,0:T(8,128)S(1)}, u32[]{:S(2)}, u32[]{:S(2)}) collective-permute-start(f32[128,512]{1,0:T(8,128)S(1)} %add.107), channel_id=1, source_target_pairs={{0,8},{4,12},{8,0},{12,4},{16,24},{20,28},{24,16},{28,20},{32,40},... | collective-permute-start | bytes 786440 | tf_op jit(solution)/shard_map/ppermute | solution.py:65
  195.1 7.7 %collective-permute-start.18 = (f32[128,512]{1,0:T(8,128)S(1)}, f32[128,512]{1,0:T(8,128)S(1)}, u32[]{:S(2)}, u32[]{:S(2)}) collective-permute-start(f32[128,512]{1,0:T(8,128)S(1)} %add.108), channel_id=1, source_target_pairs={{0,16},{4,20},{8,24},{12,28},{16,0},{20,4},{24,8},{28,12},{32,48},... | collective-permute-start | bytes 786440 | tf_op jit(solution)/shard_map/ppermute | solution.py:65
  202.9 13.5 %collective-permute-start.19 = (f32[128,512]{1,0:T(8,128)S(1)}, f32[128,512]{1,0:T(8,128)S(1)}, u32[]{:S(2)}, u32[]{:S(2)}) collective-permute-start(f32[128,512]{1,0:T(8,128)S(1)} %add.109), channel_id=1, source_target_pairs={{0,32},{4,36},{8,40},{12,44},{16,48},{20,52},{24,56},{28,60},{32,0... | collective-permute-start | bytes 786440 | tf_op jit(solution)/shard_map/ppermute | solution.py:65
  216.4 14.8 %collective-permute-start.20 = (f32[128,512]{1,0:T(8,128)S(1)}, f32[128,512]{1,0:T(8,128)S(1)}, u32[]{:S(2)}, u32[]{:S(2)}) collective-permute-start(f32[128,512]{1,0:T(8,128)S(1)} %add.110), channel_id=1, source_target_pairs={{0,64},{4,68},{8,72},{12,76},{16,80},{20,84},{24,88},{28,92},{32,9... | collective-permute-start | bytes 786440 | tf_op jit(solution)/shard_map/ppermute | solution.py:65
Sparse Core Ops, SparseCore 0:
  22.4 92.4 all-gather.2
  156.5 103.1 all-gather.4

commit v10 on v9

--- a/solution.py
+++ b/solution.py
@@ -28,7 +28,7 @@
 def block_product(adjacency_tiles, positions, gathered):
     rows, tiles, bs, _ = adjacency_tiles.shape
     width = gathered.shape[1]
-    group = 2 if rows % 2 == 0 else 1
+    group = 4 if rows % 4 == 0 else 1
     blocks = gathered.reshape(-1, bs, width)
     cost = pl.CostEstimate(
         flops=2 * rows * tiles * bs * bs * width,
@@ -103,14 +103,14 @@
     pieces = jnp.split(x, 4, axis=0)
     partner = [lax.ppermute(piece, "xh", xor_pairs(2, 1)) for piece in pieces]
     pair = jnp.concatenate([x] + partner, axis=0)
-    return lax.all_gather(pair, ("z", "y"), axis=0, tiled=True)
+    return lax.all_gather(pair, ("y", "z"), axis=0, tiled=True)
 
 
-def hier_positions(positions, local_blocks, n_xh, n_y):
+def hier_positions(positions, local_blocks, n_z, n_xh, n_y):
     owner, block = positions // local_blocks, positions % local_blocks
     z, xh, y = owner // (n_xh * n_y), (owner // n_y) % n_xh, owner % n_y
     slot = xh ^ lax.axis_index("xh")
-    return ((z * n_y + y) * n_xh + slot) * local_blocks + block
+    return ((y * n_z + z) * n_xh + slot) * local_blocks + block
 
 
 def local(sizes, node_features, weight, cotangent, adjacency_tiles, block_cols, block_perm):
@@ -121,7 +121,7 @@
     bs = adjacency_tiles.shape[2]
     w_split = weight.reshape(n_rep, feat_dev, f_all)
     positions = column_positions(block_cols, block_perm)
-    positions = hier_positions(positions, node_features.shape[0] // bs, n_xh, n_y)
+    positions = hier_positions(positions, node_features.shape[0] // bs, n_z, n_xh, n_y)
     gathered = hier_gather(node_features)
     aggregate = block_product(adjacency_tiles, positions, gathered)
     rows = aggregate.shape[0] // n_rep
@@ -135,7 +135,7 @@
         "rf,jof->jro", grad_pre, w_split, preferred_element_type=jnp.float32
     ).astype(jnp.bfloat16)
     pair = jnp.concatenate([exchange(grad_split, n_rep), exchange(grad_split, n_rep, far=True)])
-    gathered_grad = lax.all_gather(pair.reshape(-1, feat_dev), ("z", "y"), axis=0, tiled=True)
+    gathered_grad = lax.all_gather(pair.reshape(-1, feat_dev), ("y", "z"), axis=0, tiled=True)
     feature_grad = block_product(adjacency_tiles, positions, gathered_grad)
     weight_part = jnp.einsum("irf,ro->ifo", agg_rows, grad_pre, preferred_element_type=jnp.float32)
     weight_rows = halving_scatter(weight_part, REP, n_rep)

time: 283 us -> 281 us (level)
  no operation moved by 1% of the time
where the time goes in v10:
time: 281 us
  waiting for transfers between devices  196 us (70%)
  Pallas kernels  29.7 us (11%)
  starting transfers between devices  29.5 us (10%)
  between operations  14.4 us (5%)
  local copies, waits for them, and re-layouts  5.32 us (2%)
  other arithmetic  3.69 us (1%)
    all_gather x1, waiting for transfers between devices, hier_gather(): return lax.all_gather(pair, ('y', 'z'), axis=0, tiled=True)  91 us
    ppermute x5, waiting for transfers between devices, butterfly_sum(): x = x + lax.ppermute(x, axis, xor_pairs(size, bit))  47.4 us
    pallas_call x2, Pallas kernels, block_product(): pl.pallas_call(_product_kernel, grid_spec=pltpu.PrefetchScalarGridSpec(nu...  29.7 us
    all_gather x1, waiting for transfers between devices, local(): lax.all_gather(pair.reshape(-1, feat_dev), ('y', 'z'), axis=0, tiled=True)  27.7 us
    ppermute x2, waiting for transfers between devices, halving_scatter(): parts = keep + lax.ppermute(send, axis, xor_pairs(size, bit))  13.9 us
    ppermute x5, starting transfers between devices, butterfly_sum(): x = x + lax.ppermute(x, axis, xor_pairs(size, bit))  10.7 us
    ppermute x4, starting transfers between devices, hier_gather(): partner = [lax.ppermute(piece, 'xh', xor_pairs(2, 1)) for piece in pieces]  6.7 us
    ppermute x4, starting transfers between devices, exchange(): send = lax.ppermute(send, axis, xor_pairs(2 * size, size + s))  6.29 us
  transfers between devices with their start and end apart: 23, of which 17 were waited for; matrix products, arithmetic and copies ran while one was open for 2% of the time, Pallas kernels for 0%

profile of v10, /device:TPU:1, one launch (start us, length us, event | category | flops | bytes accessed | tf_op | source)
XLA Modules:
  0.0 281.0 jit_solution(3577761695425896316)
XLA Ops:
  7.2 1.1 fusion.18
  8.3 3.6 %collective-permute-start = (bf16[384,128]{1,0:T(8,128)(2,1)S(1)}, bf16[384,128]{1,0:T(8,128)(2,1)S(1)}, u32[]{:S(2)}, u32[]{:S(2)}) collective-permute-start(bf16[384,128]{1,0:T(8,128)(2,1)S(1)} %get-tuple-element.18), channel_id=1, source_target_pairs={{0,16},{16,0},{1,17},{17,1},{2,18},{18,2},{3,19},{19,3},{4,20},{20... | collective-permute-start | bytes 294920 | tf_op jit(solution)/shard_map/ppermute | solution.py:104
  12.0 0.1 collective-permute-start.1
  12.1 2.9 %collective-permute-start.2 = (bf16[384,128]{1,0:T(8,128)(2,1)S(1)}, bf16[384,128]{1,0:T(8,128)(2,1)S(1)}, u32[]{:S(2)}, u32[]{:S(2)}) collective-permute-start(bf16[384,128]{1,0:T(8,128)(2,1)S(1)} %get-tuple-element.16), channel_id=1, source_target_pairs={{0,16},{16,0},{1,17},{17,1},{2,18},{18,2},{3,19},{19,3},{4,20},{20... | collective-permute-start | bytes 294920 | tf_op jit(solution)/shard_map/ppermute | solution.py:104
  15.0 0.1 collective-permute-start.3
  15.0 1.0 constant_dynamic-update-slice_fusion.4
  16.1 0.8 collective-permute-done.1
  17.0 2.0 collective-permute-done.2
  19.0 2.3 collective-permute-done.3
  21.3 0.9 copy-done.1
  22.2 0.0 all-gather.5.cloned.1.call-start
  22.3 1.1 select_reduce_fusion
  23.5 0.1 div.30
  23.5 0.1 rem.67
  23.6 0.1 ne.69
  23.8 91.0 %all-gather.3.cloned.1.call-done = bf16[49152,128]{1,0:T(8,128)(2,1)} async-done(((bf16[3072,128]{1,0:T(8,128)(2,1)}), bf16[49152,128]{1,0:T(8,128)(2,1)}) %all-gather.3.cloned.1.call-update) | async-done | bytes 12582928 | tf_op jit(solution)/shard_map/all_gather | solution.py:106
  114.9 14.5 %shard_map.85 = bf16[12,128,128]{2,1,0:T(8,128)(2,1)S(1)} custom-call(s32[672]{0:T(1024)S(1)} %fusion.8.pos_ref, bf16[12,56,128,128]{3,2,1,0:T(8,128)(2,1)} %a_ref.3, bf16[384,128,128]{2,1,0:T(8,128)(2,1)} %bitcast.47), custom_call_target="tpu_custom_call" | custom-call | flops 2818572288 | bytes 34996224 | tf_op jit(solution)/shard_map/pallas_call | solution.py:38
  129.4 0.9 collective-permute-start.4
  130.3 1.2 collective-permute-start.5
  131.5 0.5 collective-permute-start.6
  132.1 2.5 collective-permute-done.5
  134.6 2.4 collective-permute-done.6
  137.0 0.1 pad_maximum_fusion.1
  137.0 0.6 gather_fusion
  137.7 1.4 multiply_convert_fusion
  139.1 0.4 convolution_convert_fusion
  139.5 0.1 dynamic-slice_bitcast_fusion.7
  139.6 2.8 collective-permute-start.10
  142.3 0.6 collective-permute-start.11
  142.9 2.4 collective-permute-start.12
  145.3 0.5 collective-permute-start.13
  145.8 0.1 collective-permute-start.7
  146.0 0.6 collective-permute-start.8
  146.6 2.2 collective-permute-done.11
  148.8 0.6 collective-permute-start.9
  149.4 1.6 collective-permute-done.12
  150.9 2.1 collective-permute-done.13
  153.0 0.1 pad_maximum_fusion.3
  153.1 0.6 gather_fusion.2
  153.7 0.1 pad_maximum_fusion.2
  153.8 0.6 gather_fusion.1
  154.4 0.1 broadcast_select_fusion.1
  154.6 1.0 pad_maximum_fusion
  155.6 0.6 fusion
  156.2 0.1 slice_select_fusion
  156.3 0.5 collective-permute-start.14
  156.8 12.8 %collective-permute-done.14 = f32[2,128,512]{2,1,0:T(8,128)S(1)} collective-permute-done((f32[2,128,512]{2,1,0:T(8,128)S(1)}, f32[2,128,512]{2,1,0:T(8,128)S(1)}, u32[]{:S(2)}, u32[]{:S(2)}) %collective-permute-start.14) | collective-permute-done | bytes 524320 | tf_op jit(solution)/shard_map/ppermute | solution.py:79
  169.6 0.1 select_add_fusion
  169.7 1.2 collective-permute-start.15
  171.0 1.2 collective-permute-done.15
  172.1 0.1 add_bitcast_fusion
  172.2 1.3 collective-permute-start.16
  173.5 12.2 %collective-permute-done.16 = f32[128,512]{1,0:T(8,128)S(1)} collective-permute-done((f32[128,512]{1,0:T(8,128)S(1)}, f32[128,512]{1,0:T(8,128)S(1)}, u32[]{:S(2)}, u32[]{:S(2)}) %collective-permute-start.16) | collective-permute-done | bytes 262176 | tf_op jit(solution)/shard_map/ppermute | solution.py:65
  185.7 2.5 collective-permute-start.17
  188.3 6.0 %collective-permute-done.17 = f32[128,512]{1,0:T(8,128)S(1)} collective-permute-done((f32[128,512]{1,0:T(8,128)S(1)}, f32[128,512]{1,0:T(8,128)S(1)}, u32[]{:S(2)}, u32[]{:S(2)}) %collective-permute-start.17) | collective-permute-done | bytes 262176 | tf_op jit(solution)/shard_map/ppermute | solution.py:65
  194.3 2.0 collective-permute-start.18
  196.3 5.7 %collective-permute-done.18 = f32[128,512]{1,0:T(8,128)S(1)} collective-permute-done((f32[128,512]{1,0:T(8,128)S(1)}, f32[128,512]{1,0:T(8,128)S(1)}, u32[]{:S(2)}, u32[]{:S(2)}) %collective-permute-start.18) | collective-permute-done | bytes 262176 | tf_op jit(solution)/shard_map/ppermute | solution.py:65
  202.1 1.7 collective-permute-start.19
  203.8 11.8 %collective-permute-done.19 = f32[128,512]{1,0:T(8,128)S(1)} collective-permute-done((f32[128,512]{1,0:T(8,128)S(1)}, f32[128,512]{1,0:T(8,128)S(1)}, u32[]{:S(2)}, u32[]{:S(2)}) %collective-permute-start.19) | collective-permute-done | bytes 262176 | tf_op jit(solution)/shard_map/ppermute | solution.py:65
  215.6 3.2 %collective-permute-start.20 = (f32[128,512]{1,0:T(8,128)S(1)}, f32[128,512]{1,0:T(8,128)S(1)}, u32[]{:S(2)}, u32[]{:S(2)}) collective-permute-start(f32[128,512]{1,0:T(8,128)S(1)} %add.110), channel_id=1, source_target_pairs={{0,64},{4,68},{8,72},{12,76},{16,80},{20,84},{24,88},{28,92},{32,9... | collective-permute-start | bytes 786440 | tf_op jit(solution)/shard_map/ppermute | solution.py:65
  218.8 11.7 %collective-permute-done.20 = f32[128,512]{1,0:T(8,128)S(1)} collective-permute-done((f32[128,512]{1,0:T(8,128)S(1)}, f32[128,512]{1,0:T(8,128)S(1)}, u32[]{:S(2)}, u32[]{:S(2)}) %collective-permute-start.20) | collective-permute-done | bytes 262176 | tf_op jit(solution)/shard_map/ppermute | solution.py:65
  230.5 0.7 add_multiply_fusion
  231.2 27.7 %all-gather.5.cloned.1.call-done = bf16[49152,128]{1,0:T(8,128)(2,1)} async-done(((bf16[3072,128]{1,0:T(8,128)(2,1)}), bf16[49152,128]{1,0:T(8,128)(2,1)}) %all-gather.5.cloned.1.call-update) | async-done | bytes 12582928 | tf_op jit(solution)/shard_map/all_gather | solution.py:138
  259.0 15.2 %shard_map.86 = bf16[12,128,128]{2,1,0:T(8,128)(2,1)} custom-call(s32[672]{0:T(1024)S(1)} %fusion.8.pos_ref, bf16[12,56,128,128]{3,2,1,0:T(8,128)(2,1)} %a_ref.3, bf16[384,128,128]{2,1,0:T(8,128)(2,1)} %bitcast.46), custom_call_target="tpu_custom_call" | custom-call | flops 2818572288 | bytes 34996224 | tf_op jit(solution)/shard_map/pallas_call | solution.py:38
  (30 shorter events, 0.4 us)
Async XLA Ops:
  7.2 130.5 %copy-start = (bf16[512,512]{1,0:T(8,128)(2,1)S(1)}, bf16[512,512]{1,0:T(8,128)(2,1)}, u32[]{:S(2)}) copy-start(bf16[512,512]{1,0:T(8,128)(2,1)} %param.9) | copy-start | bytes 1572868
  7.2 107.7 %all-gather.3.cloned.1.call-start = ((), (), s32[]{:S(2)}) async-start(), calls=%async_computation | async-start | bytes 13369344 | tf_op jit(solution)/shard_map/all_gather | solution.py:106
  8.3 7.7 %collective-permute-start = (bf16[384,128]{1,0:T(8,128)(2,1)S(1)}, bf16[384,128]{1,0:T(8,128)(2,1)S(1)}, u32[]{:S(2)}, u32[]{:S(2)}) collective-permute-start(bf16[384,128]{1,0:T(8,128)(2,1)S(1)} %get-tuple-element.18), channel_id=1, source_target_pairs={{0,16},{16,0},{1,17},{17,1},{2,18},{18,2},{3,19},{19,3},{4,20},{20... | collective-permute-start | bytes 294920 | tf_op jit(solution)/shard_map/ppermute | solution.py:104
  12.0 5.0 %collective-permute-start.1 = (bf16[384,128]{1,0:T(8,128)(2,1)S(1)}, bf16[384,128]{1,0:T(8,128)(2,1)S(1)}, u32[]{:S(2)}, u32[]{:S(2)}) collective-permute-start(bf16[384,128]{1,0:T(8,128)(2,1)S(1)} %get-tuple-element.17), channel_id=1, source_target_pairs={{0,16},{16,0},{1,17},{17,1},{2,18},{18,2},{3,19},{19,3},{4,20},{20... | collective-permute-start | bytes 294920 | tf_op jit(solution)/shard_map/ppermute | solution.py:104
  12.1 6.9 %collective-permute-start.2 = (bf16[384,128]{1,0:T(8,128)(2,1)S(1)}, bf16[384,128]{1,0:T(8,128)(2,1)S(1)}, u32[]{:S(2)}, u32[]{:S(2)}) collective-permute-start(bf16[384,128]{1,0:T(8,128)(2,1)S(1)} %get-tuple-element.16), channel_id=1, source_target_pairs={{0,16},{16,0},{1,17},{17,1},{2,18},{18,2},{3,19},{19,3},{4,20},{20... | collective-permute-start | bytes 294920 | tf_op jit(solution)/shard_map/ppermute | solution.py:104
  15.0 6.3 %collective-permute-start.3 = (bf16[384,128]{1,0:T(8,128)(2,1)S(1)}, bf16[384,128]{1,0:T(8,128)(2,1)S(1)}, u32[]{:S(2)}, u32[]{:S(2)}) collective-permute-start(bf16[384,128]{1,0:T(8,128)(2,1)S(1)} %get-tuple-element.15), channel_id=1, source_target_pairs={{0,16},{16,0},{1,17},{17,1},{2,18},{18,2},{3,19},{19,3},{4,20},{20... | collective-permute-start | bytes 294920 | tf_op jit(solution)/shard_map/ppermute | solution.py:104
  21.3 0.9 copy-start.1
  22.2 236.7 %all-gather.5.cloned.1.call-start = ((), (), s32[]{:S(2)}) async-start(), calls=%async_computation.1 | async-start | bytes 13369344 | tf_op jit(solution)/shard_map/all_gather | solution.py:138
  114.8 22.8 %copy-start.2 = (bf16[384,512]{1,0:T(8,128)(2,1)S(1)}, bf16[384,512]{1,0:T(8,128)(2,1)}, u32[]{:S(2)}) copy-start(bf16[384,512]{1,0:T(8,128)(2,1)} %param.10) | copy-start | bytes 1179652
  129.4 2.7 collective-permute-start.4
  130.3 4.3 %collective-permute-start.5 = (bf16[384,128]{1,0:T(8,128)(2,1)S(1)}, bf16[384,128]{1,0:T(8,128)(2,1)S(1)}, u32[]{:S(2)}, u32[]{:S(2)}) collective-permute-start(bf16[384,128]{1,0:T(8,128)(2,1)S(1)} %get-tuple-element.13), channel_id=1, source_target_pairs={{0,2},{1,3},{2,0},{3,1},{4,6},{5,7},{6,4},{7,5},{8,10},{9,11},{10,... | collective-permute-start | bytes 294920 | tf_op jit(solution)/shard_map/ppermute | solution.py:97
  131.5 5.4 %collective-permute-start.6 = (bf16[384,128]{1,0:T(8,128)(2,1)S(1)}, bf16[384,128]{1,0:T(8,128)(2,1)S(1)}, u32[]{:S(2)}, u32[]{:S(2)}) collective-permute-start(bf16[384,128]{1,0:T(8,128)(2,1)S(1)} %get-tuple-element.12), channel_id=1, source_target_pairs={{0,3},{1,2},{2,1},{3,0},{4,7},{5,6},{6,5},{7,4},{8,11},{9,10},{10,... | collective-permute-start | bytes 294920 | tf_op jit(solution)/shard_map/ppermute | solution.py:97
  139.6 6.4 %collective-permute-start.10 = (bf16[384,128]{1,0:T(8,128)(2,1)S(1)}, bf16[384,128]{1,0:T(8,128)(2,1)S(1)}, u32[]{:S(2)}, u32[]{:S(2)}) collective-permute-start(bf16[384,128]{1,0:T(8,128)(2,1)S(1)} %get-tuple-element.7), channel_id=1, source_target_pairs={{0,16},{1,17},{2,18},{3,19},{16,0},{17,1},{18,2},{19,3},{4,20},{5,... | collective-permute-start | bytes 294920 | tf_op jit(solution)/shard_map/ppermute | solution.py:95
  142.3 6.4 %collective-permute-start.11 = (bf16[384,128]{1,0:T(8,128)(2,1)S(1)}, bf16[384,128]{1,0:T(8,128)(2,1)S(1)}, u32[]{:S(2)}, u32[]{:S(2)}) collective-permute-start(bf16[384,128]{1,0:T(8,128)(2,1)S(1)} %get-tuple-element.10), channel_id=1, source_target_pairs={{0,17},{1,16},{2,19},{3,18},{16,1},{17,0},{18,3},{19,2},{4,21},{5,... | collective-permute-start | bytes 294920 | tf_op jit(solution)/shard_map/ppermute | solution.py:95
  142.9 8.0 %collective-permute-start.12 = (bf16[384,128]{1,0:T(8,128)(2,1)S(1)}, bf16[384,128]{1,0:T(8,128)(2,1)S(1)}, u32[]{:S(2)}, u32[]{:S(2)}) collective-permute-start(bf16[384,128]{1,0:T(8,128)(2,1)S(1)} %get-tuple-element.9), channel_id=1, source_target_pairs={{0,18},{1,19},{2,16},{3,17},{16,2},{17,3},{18,0},{19,1},{4,22},{5,... | collective-permute-start | bytes 294920 | tf_op jit(solution)/shard_map/ppermute | solution.py:95
  145.3 7.7 %collective-permute-start.13 = (bf16[384,128]{1,0:T(8,128)(2,1)S(1)}, bf16[384,128]{1,0:T(8,128)(2,1)S(1)}, u32[]{:S(2)}, u32[]{:S(2)}) collective-permute-start(bf16[384,128]{1,0:T(8,128)(2,1)S(1)} %get-tuple-element.8), channel_id=1, source_target_pairs={{0,19},{1,18},{2,17},{3,16},{16,3},{17,2},{18,1},{19,0},{4,23},{5,... | collective-permute-start | bytes 294920 | tf_op jit(solution)/shard_map/ppermute | solution.py:95
  145.8 7.9 %collective-permute-start.7 = (bf16[384,128]{1,0:T(8,128)(2,1)S(1)}, bf16[384,128]{1,0:T(8,128)(2,1)S(1)}, u32[]{:S(2)}, u32[]{:S(2)}) collective-permute-start(bf16[384,128]{1,0:T(8,128)(2,1)S(1)} %get-tuple-element.10), channel_id=1, source_target_pairs={{0,1},{1,0},{2,3},{3,2},{4,5},{5,4},{6,7},{7,6},{8,9},{9,8},{10,11... | collective-permute-start | bytes 294920 | tf_op jit(solution)/shard_map/ppermute | solution.py:97
  146.0 7.7 %collective-permute-start.8 = (bf16[384,128]{1,0:T(8,128)(2,1)S(1)}, bf16[384,128]{1,0:T(8,128)(2,1)S(1)}, u32[]{:S(2)}, u32[]{:S(2)}) collective-permute-start(bf16[384,128]{1,0:T(8,128)(2,1)S(1)} %get-tuple-element.9), channel_id=1, source_target_pairs={{0,2},{1,3},{2,0},{3,1},{4,6},{5,7},{6,4},{7,5},{8,10},{9,11},{10,... | collective-permute-start | bytes 294920 | tf_op jit(solution)/shard_map/ppermute | solution.py:97
  148.8 5.0 %collective-permute-start.9 = (bf16[384,128]{1,0:T(8,128)(2,1)S(1)}, bf16[384,128]{1,0:T(8,128)(2,1)S(1)}, u32[]{:S(2)}, u32[]{:S(2)}) collective-permute-start(bf16[384,128]{1,0:T(8,128)(2,1)S(1)} %get-tuple-element.8), channel_id=1, source_target_pairs={{0,3},{1,2},{2,1},{3,0},{4,7},{5,6},{6,5},{7,4},{8,11},{9,10},{10,... | collective-permute-start | bytes 294920 | tf_op jit(solution)/shard_map/ppermute | solution.py:97
  156.3 13.3 %collective-permute-start.14 = (f32[2,128,512]{2,1,0:T(8,128)S(1)}, f32[2,128,512]{2,1,0:T(8,128)S(1)}, u32[]{:S(2)}, u32[]{:S(2)}) collective-permute-start(f32[2,128,512]{2,1,0:T(8,128)S(1)} %slice_select_fusion), channel_id=1, source_target_pairs={{0,2},{1,3},{2,0},{3,1},{4,6},{5,7},{6,4},{7,5},{8,10},{9,11},{10,... | collective-permute-start | bytes 1572872 | tf_op jit(solution)/shard_map/ppermute | solution.py:79
  169.7 2.4 collective-permute-start.15
  172.2 13.5 %collective-permute-start.16 = (f32[128,512]{1,0:T(8,128)S(1)}, f32[128,512]{1,0:T(8,128)S(1)}, u32[]{:S(2)}, u32[]{:S(2)}) collective-permute-start(f32[128,512]{1,0:T(8,128)S(1)} %add_bitcast_fusion), channel_id=1, source_target_pairs={{0,4},{4,0},{8,12},{12,8},{16,20},{20,16},{24,28},{28,24},{32,36},... | collective-permute-start | bytes 786440 | tf_op jit(solution)/shard_map/ppermute | solution.py:65
  185.7 8.6 %collective-permute-start.17 = (f32[128,512]{1,0:T(8,128)S(1)}, f32[128,512]{1,0:T(8,128)S(1)}, u32[]{:S(2)}, u32[]{:S(2)}) collective-permute-start(f32[128,512]{1,0:T(8,128)S(1)} %add.107), channel_id=1, source_target_pairs={{0,8},{4,12},{8,0},{12,4},{16,24},{20,28},{24,16},{28,20},{32,40},... | collective-permute-start | bytes 786440 | tf_op jit(solution)/shard_map/ppermute | solution.py:65
  194.3 7.7 %collective-permute-start.18 = (f32[128,512]{1,0:T(8,128)S(1)}, f32[128,512]{1,0:T(8,128)S(1)}, u32[]{:S(2)}, u32[]{:S(2)}) collective-permute-start(f32[128,512]{1,0:T(8,128)S(1)} %add.108), channel_id=1, source_target_pairs={{0,16},{4,20},{8,24},{12,28},{16,0},{20,4},{24,8},{28,12},{32,48},... | collective-permute-start | bytes 786440 | tf_op jit(solution)/shard_map/ppermute | solution.py:65
  202.1 13.5 %collective-permute-start.19 = (f32[128,512]{1,0:T(8,128)S(1)}, f32[128,512]{1,0:T(8,128)S(1)}, u32[]{:S(2)}, u32[]{:S(2)}) collective-permute-start(f32[128,512]{1,0:T(8,128)S(1)} %add.109), channel_id=1, source_target_pairs={{0,32},{4,36},{8,40},{12,44},{16,48},{20,52},{24,56},{28,60},{32,0... | collective-permute-start | bytes 786440 | tf_op jit(solution)/shard_map/ppermute | solution.py:65
  215.6 14.9 %collective-permute-start.20 = (f32[128,512]{1,0:T(8,128)S(1)}, f32[128,512]{1,0:T(8,128)S(1)}, u32[]{:S(2)}, u32[]{:S(2)}) collective-permute-start(f32[128,512]{1,0:T(8,128)S(1)} %add.110), channel_id=1, source_target_pairs={{0,64},{4,68},{8,72},{12,76},{16,80},{20,84},{24,88},{28,92},{32,9... | collective-permute-start | bytes 786440 | tf_op jit(solution)/shard_map/ppermute | solution.py:65
Sparse Core Ops, SparseCore 0:
  22.4 92.4 all-gather.2
  155.7 103.1 all-gather.4

commit v11 on v10

--- a/solution.py
+++ b/solution.py
@@ -113,6 +113,12 @@
     return ((y * n_z + z) * n_xh + slot) * local_blocks + block
 
 
+def flat_positions(positions, local_blocks, n_z, n_xh, n_y):
+    owner, block = positions // local_blocks, positions % local_blocks
+    z, xh, y = owner // (n_xh * n_y), (owner // n_y) % n_xh, owner % n_y
+    return ((xh * n_y + y) * n_z + z) * local_blocks + block
+
+
 def local(sizes, node_features, weight, cotangent, adjacency_tiles, block_cols, block_perm):
     n_z, n_xh, n_y, n_xl, n_c = sizes
     n_blk, n_rep = n_z * n_xh * n_y, n_xl * n_c
@@ -121,9 +127,10 @@
     bs = adjacency_tiles.shape[2]
     w_split = weight.reshape(n_rep, feat_dev, f_all)
     positions = column_positions(block_cols, block_perm)
-    positions = hier_positions(positions, node_features.shape[0] // bs, n_z, n_xh, n_y)
-    gathered = hier_gather(node_features)
-    aggregate = block_product(adjacency_tiles, positions, gathered)
+    raw, lb = positions, node_features.shape[0] // bs
+    positions = hier_positions(raw, lb, n_z, n_xh, n_y)
+    gathered = lax.all_gather(node_features, ("xh", "y", "z"), axis=0, tiled=True)
+    aggregate = block_product(adjacency_tiles, flat_positions(raw, lb, n_z, n_xh, n_y), gathered)
     rows = aggregate.shape[0] // n_rep
     agg_rows = exchange(aggregate.reshape(n_rep, rows, feat_dev), n_rep)
     preact = jnp.einsum("irf,ifo->ro", agg_rows, w_split, preferred_element_type=jnp.float32)

time: 281 us -> 309 us (1.100)
  waiting for transfers between devices: 196 us -> 237 us
  starting transfers between devices: 29.5 us -> 18.4 us
  local copies, waits for them, and re-layouts: 5.32 us -> 2.22 us
    all_gather x1, waiting for transfers between devices: 91 us -> 134 us  [local(): lax.all_gather(node_features, ('xh', 'y', 'z'), axis=0, tiled=True)]
    ppermute x4 -> x0, starting transfers between devices: 6.7 us -> none  [hier_gather(): partner = [lax.ppermute(piece, 'xh', xor_pairs(2, 1)) for piece in pieces]]
    ppermute x4 -> x0, waiting for transfers between devices: 5.13 us -> none  [hier_gather(): partner = [lax.ppermute(piece, 'xh', xor_pairs(2, 1)) for piece in pieces]]
    ppermute x5, starting transfers between devices: 10.7 us -> 6.35 us  [butterfly_sum(): x = x + lax.ppermute(x, axis, xor_pairs(size, bit))]
    ppermute x5, waiting for transfers between devices: 47.4 us -> 51.2 us  [butterfly_sum(): x = x + lax.ppermute(x, axis, xor_pairs(size, bit))]
  transfers between devices with their start and end apart: 23 -> 19, of which waited for: 17 -> 14; matrix products, arithmetic and copies ran while one was open for 2% -> 1% of each run, Pallas kernels for 0% -> 0%
where the time goes in v11:
time: 309 us; the launch traced here: 308 us
  waiting for transfers between devices  237 us (77%)
  Pallas kernels  29.8 us (10%)
  starting transfers between devices  18.4 us (6%)
  between operations  14.3 us (5%)
  other arithmetic  3.74 us (1%)
    all_gather x1, waiting for transfers between devices, local(): lax.all_gather(node_features, ('xh', 'y', 'z'), axis=0, tiled=True)  134 us
    ppermute x5, waiting for transfers between devices, butterfly_sum(): x = x + lax.ppermute(x, axis, xor_pairs(size, bit))  51.2 us
    pallas_call x2, Pallas kernels, block_product(): pl.pallas_call(_product_kernel, grid_spec=pltpu.PrefetchScalarGridSpec(nu...  29.8 us
    all_gather x1, waiting for transfers between devices, local(): lax.all_gather(pair.reshape(-1, feat_dev), ('y', 'z'), axis=0, tiled=True)  27.4 us
    ppermute x2, waiting for transfers between devices, halving_scatter(): parts = keep + lax.ppermute(send, axis, xor_pairs(size, bit))  14 us
    ppermute x5, starting transfers between devices, butterfly_sum(): x = x + lax.ppermute(x, axis, xor_pairs(size, bit))  6.35 us
    ppermute x4, starting transfers between devices, exchange(): send = lax.ppermute(send, axis, xor_pairs(2 * size, size + s))  6.29 us
  transfers between devices with their start and end apart: 19, of which 14 were waited for; matrix products, arithmetic and copies ran while one was open for 1% of the time, Pallas kernels for 0%

profile of v11, /device:TPU:1, one launch (start us, length us, event | category | flops | bytes accessed | tf_op | source)
XLA Modules:
  0.0 308.4 jit_solution(2431138339485867486)
XLA Ops:
  7.2 0.0 copy-start
  7.2 0.0 all-gather.3.cloned.1.call-start
  7.2 0.7 all-gather.3.cloned.1.call-update
  7.9 0.0 all-gather.5.cloned.1.call-start
  8.0 1.1 select_reduce_fusion
  9.1 0.1 div.39
  9.2 0.1 rem.83
  9.3 0.1 ne.102
  9.5 133.7 %all-gather.3.cloned.1.call-done = bf16[49152,128]{1,0:T(8,128)(2,1)} async-done(((bf16[1536,128]{1,0:T(8,128)(2,1)}), bf16[49152,128]{1,0:T(8,128)(2,1)}) %all-gather.3.cloned.1.call-update) | async-done | bytes 12582928 | tf_op jit(solution)/shard_map/all_gather | solution.py:132
  143.2 14.5 %shard_map.85 = bf16[12,128,128]{2,1,0:T(8,128)(2,1)S(1)} custom-call(s32[672]{0:T(1024)S(1)} %get-tuple-element.16.pos_ref, bf16[12,56,128,128]{3,2,1,0:T(8,128)(2,1)} %a_ref.3, bf16[384,128,128]{2,1,0:T(8,128)(2,1)} %bitcast.47), custom_call_target="tpu_custom_call" | custom-call | flops 2818572288 | bytes 34996224 | tf_op jit(solution)/shard_map/pallas_call | solution.py:38
  157.8 1.5 collective-permute-start
  159.2 0.3 collective-permute-start.1
  159.5 1.4 collective-permute-start.2
  161.0 0.0 collective-permute-done
  161.0 2.5 collective-permute-done.1
  163.5 2.4 collective-permute-done.2
  165.9 0.1 pad_maximum_fusion.1
  165.9 0.6 gather_fusion
  166.6 0.0 copy-done
  166.6 1.4 multiply_convert_fusion
  168.0 0.4 convolution_convert_fusion
  168.4 0.1 dynamic-slice_bitcast_fusion.7
  168.5 0.7 collective-permute-start.6
  169.2 2.7 collective-permute-start.7
  171.8 0.9 collective-permute-start.8
  172.7 2.1 collective-permute-start.9
  174.8 0.1 collective-permute-start.3
  174.9 0.0 collective-permute-done.6
  174.9 0.0 collective-permute-start.4
  174.9 1.9 collective-permute-done.7
  176.8 0.7 collective-permute-start.5
  177.5 1.5 collective-permute-done.8
  179.0 2.1 collective-permute-done.9
  181.1 0.1 pad_maximum_fusion.3
  181.2 0.6 gather_fusion.2
  181.8 0.0 collective-permute-done.3
  181.8 0.0 collective-permute-done.4
  181.8 0.0 collective-permute-done.5
  181.9 0.1 pad_maximum_fusion.2
  182.0 0.6 gather_fusion.1
  182.6 0.1 broadcast_select_fusion.1
  182.7 1.0 pad_maximum_fusion
  183.8 0.0 all-gather.5.cloned.1.call-update
  183.8 0.6 fusion
  184.4 0.1 slice_select_fusion
  184.5 0.5 collective-permute-start.10
  185.0 12.8 %collective-permute-done.10 = f32[2,128,512]{2,1,0:T(8,128)S(1)} collective-permute-done((f32[2,128,512]{2,1,0:T(8,128)S(1)}, f32[2,128,512]{2,1,0:T(8,128)S(1)}, u32[]{:S(2)}, u32[]{:S(2)}) %collective-permute-start.10) | collective-permute-done | bytes 524320 | tf_op jit(solution)/shard_map/ppermute | solution.py:79
  197.8 0.1 select_add_fusion
  198.0 1.2 collective-permute-start.11
  199.2 1.2 collective-permute-done.11
  200.3 0.1 add_bitcast_fusion
  200.4 0.1 collective-permute-start.12
  200.5 12.9 %collective-permute-done.12 = f32[128,512]{1,0:T(8,128)S(1)} collective-permute-done((f32[128,512]{1,0:T(8,128)S(1)}, f32[128,512]{1,0:T(8,128)S(1)}, u32[]{:S(2)}, u32[]{:S(2)}) %collective-permute-start.12) | collective-permute-done | bytes 262176 | tf_op jit(solution)/shard_map/ppermute | solution.py:65
  213.4 2.0 collective-permute-start.13
  215.3 6.9 %collective-permute-done.13 = f32[128,512]{1,0:T(8,128)S(1)} collective-permute-done((f32[128,512]{1,0:T(8,128)S(1)}, f32[128,512]{1,0:T(8,128)S(1)}, u32[]{:S(2)}, u32[]{:S(2)}) %collective-permute-start.13) | collective-permute-done | bytes 262176 | tf_op jit(solution)/shard_map/ppermute | solution.py:65
  222.3 1.0 collective-permute-start.14
  223.2 7.0 %collective-permute-done.14 = f32[128,512]{1,0:T(8,128)S(1)} collective-permute-done((f32[128,512]{1,0:T(8,128)S(1)}, f32[128,512]{1,0:T(8,128)S(1)}, u32[]{:S(2)}, u32[]{:S(2)}) %collective-permute-start.14) | collective-permute-done | bytes 262176 | tf_op jit(solution)/shard_map/ppermute | solution.py:65
  230.3 0.9 collective-permute-start.15
  231.1 12.5 %collective-permute-done.15 = f32[128,512]{1,0:T(8,128)S(1)} collective-permute-done((f32[128,512]{1,0:T(8,128)S(1)}, f32[128,512]{1,0:T(8,128)S(1)}, u32[]{:S(2)}, u32[]{:S(2)}) %collective-permute-start.15) | collective-permute-done | bytes 262176 | tf_op jit(solution)/shard_map/ppermute | solution.py:65
  243.7 2.5 collective-permute-start.16
  246.1 12.0 %collective-permute-done.16 = f32[128,512]{1,0:T(8,128)S(1)} collective-permute-done((f32[128,512]{1,0:T(8,128)S(1)}, f32[128,512]{1,0:T(8,128)S(1)}, u32[]{:S(2)}, u32[]{:S(2)}) %collective-permute-start.16) | collective-permute-done | bytes 262176 | tf_op jit(solution)/shard_map/ppermute | solution.py:65
  258.1 0.7 add_multiply_fusion
  258.9 27.4 %all-gather.5.cloned.1.call-done = bf16[49152,128]{1,0:T(8,128)(2,1)} async-done(((bf16[3072,128]{1,0:T(8,128)(2,1)}), bf16[49152,128]{1,0:T(8,128)(2,1)}) %all-gather.5.cloned.1.call-update) | async-done | bytes 12582928 | tf_op jit(solution)/shard_map/all_gather | solution.py:145
  286.3 15.2 %shard_map.86 = bf16[12,128,128]{2,1,0:T(8,128)(2,1)} custom-call(s32[672]{0:T(1024)S(1)} %get-tuple-element.15.pos_ref, bf16[12,56,128,128]{3,2,1,0:T(8,128)(2,1)} %a_ref.3, bf16[384,128,128]{2,1,0:T(8,128)(2,1)} %bitcast.46), custom_call_target="tpu_custom_call" | custom-call | flops 2818572288 | bytes 34996224 | tf_op jit(solution)/shard_map/pallas_call | solution.py:38
  (14 shorter events, 0.3 us)
Async XLA Ops:
  7.2 159.4 %copy-start = (bf16[512,512]{1,0:T(8,128)(2,1)S(1)}, bf16[512,512]{1,0:T(8,128)(2,1)}, u32[]{:S(2)}) copy-start(bf16[512,512]{1,0:T(8,128)(2,1)} %param.9) | copy-start | bytes 1572868
  7.2 136.0 %all-gather.3.cloned.1.call-start = ((), (), s32[]{:S(2)}) async-start(), calls=%async_computation | async-start | bytes 12976128 | tf_op jit(solution)/shard_map/all_gather | solution.py:132
  7.9 278.4 %all-gather.5.cloned.1.call-start = ((), (), s32[]{:S(2)}) async-start(), calls=%async_computation.1 | async-start | bytes 13369344 | tf_op jit(solution)/shard_map/all_gather | solution.py:145
  143.2 23.4 %copy-start.1 = (bf16[384,512]{1,0:T(8,128)(2,1)S(1)}, bf16[384,512]{1,0:T(8,128)(2,1)}, u32[]{:S(2)}) copy-start(bf16[384,512]{1,0:T(8,128)(2,1)} %param.10) | copy-start | bytes 1179652
  157.8 3.2 %collective-permute-start = (bf16[384,128]{1,0:T(8,128)(2,1)S(1)}, bf16[384,128]{1,0:T(8,128)(2,1)S(1)}, u32[]{:S(2)}, u32[]{:S(2)}) collective-permute-start(bf16[384,128]{1,0:T(8,128)(2,1)S(1)} %get-tuple-element.14), channel_id=1, source_target_pairs={{0,1},{1,0},{2,3},{3,2},{4,5},{5,4},{6,7},{7,6},{8,9},{9,8},{10,11... | collective-permute-start | bytes 294920 | tf_op jit(solution)/shard_map/ppermute | solution.py:97
  159.2 4.3 %collective-permute-start.1 = (bf16[384,128]{1,0:T(8,128)(2,1)S(1)}, bf16[384,128]{1,0:T(8,128)(2,1)S(1)}, u32[]{:S(2)}, u32[]{:S(2)}) collective-permute-start(bf16[384,128]{1,0:T(8,128)(2,1)S(1)} %get-tuple-element.13), channel_id=1, source_target_pairs={{0,2},{1,3},{2,0},{3,1},{4,6},{5,7},{6,4},{7,5},{8,10},{9,11},{10,... | collective-permute-start | bytes 294920 | tf_op jit(solution)/shard_map/ppermute | solution.py:97
  159.5 6.3 %collective-permute-start.2 = (bf16[384,128]{1,0:T(8,128)(2,1)S(1)}, bf16[384,128]{1,0:T(8,128)(2,1)S(1)}, u32[]{:S(2)}, u32[]{:S(2)}) collective-permute-start(bf16[384,128]{1,0:T(8,128)(2,1)S(1)} %get-tuple-element.12), channel_id=1, source_target_pairs={{0,3},{1,2},{2,1},{3,0},{4,7},{5,6},{6,5},{7,4},{8,11},{9,10},{10,... | collective-permute-start | bytes 294920 | tf_op jit(solution)/shard_map/ppermute | solution.py:97
  168.5 6.4 %collective-permute-start.6 = (bf16[384,128]{1,0:T(8,128)(2,1)S(1)}, bf16[384,128]{1,0:T(8,128)(2,1)S(1)}, u32[]{:S(2)}, u32[]{:S(2)}) collective-permute-start(bf16[384,128]{1,0:T(8,128)(2,1)S(1)} %get-tuple-element.7), channel_id=1, source_target_pairs={{0,16},{1,17},{2,18},{3,19},{16,0},{17,1},{18,2},{19,3},{4,20},{5,... | collective-permute-start | bytes 294920 | tf_op jit(solution)/shard_map/ppermute | solution.py:95
  169.2 7.6 %collective-permute-start.7 = (bf16[384,128]{1,0:T(8,128)(2,1)S(1)}, bf16[384,128]{1,0:T(8,128)(2,1)S(1)}, u32[]{:S(2)}, u32[]{:S(2)}) collective-permute-start(bf16[384,128]{1,0:T(8,128)(2,1)S(1)} %get-tuple-element.10), channel_id=1, source_target_pairs={{0,17},{1,16},{2,19},{3,18},{16,1},{17,0},{18,3},{19,2},{4,21},{5,... | collective-permute-start | bytes 294920 | tf_op jit(solution)/shard_map/ppermute | solution.py:95
  171.8 7.2 %collective-permute-start.8 = (bf16[384,128]{1,0:T(8,128)(2,1)S(1)}, bf16[384,128]{1,0:T(8,128)(2,1)S(1)}, u32[]{:S(2)}, u32[]{:S(2)}) collective-permute-start(bf16[384,128]{1,0:T(8,128)(2,1)S(1)} %get-tuple-element.9), channel_id=1, source_target_pairs={{0,18},{1,19},{2,16},{3,17},{16,2},{17,3},{18,0},{19,1},{4,22},{5,... | collective-permute-start | bytes 294920 | tf_op jit(solution)/shard_map/ppermute | solution.py:95
  172.7 8.4 %collective-permute-start.9 = (bf16[384,128]{1,0:T(8,128)(2,1)S(1)}, bf16[384,128]{1,0:T(8,128)(2,1)S(1)}, u32[]{:S(2)}, u32[]{:S(2)}) collective-permute-start(bf16[384,128]{1,0:T(8,128)(2,1)S(1)} %get-tuple-element.8), channel_id=1, source_target_pairs={{0,19},{1,18},{2,17},{3,16},{16,3},{17,2},{18,1},{19,0},{4,23},{5,... | collective-permute-start | bytes 294920 | tf_op jit(solution)/shard_map/ppermute | solution.py:95
  174.8 7.1 %collective-permute-start.3 = (bf16[384,128]{1,0:T(8,128)(2,1)S(1)}, bf16[384,128]{1,0:T(8,128)(2,1)S(1)}, u32[]{:S(2)}, u32[]{:S(2)}) collective-permute-start(bf16[384,128]{1,0:T(8,128)(2,1)S(1)} %get-tuple-element.10), channel_id=1, source_target_pairs={{0,1},{1,0},{2,3},{3,2},{4,5},{5,4},{6,7},{7,6},{8,9},{9,8},{10,11... | collective-permute-start | bytes 294920 | tf_op jit(solution)/shard_map/ppermute | solution.py:97
  174.9 6.9 %collective-permute-start.4 = (bf16[384,128]{1,0:T(8,128)(2,1)S(1)}, bf16[384,128]{1,0:T(8,128)(2,1)S(1)}, u32[]{:S(2)}, u32[]{:S(2)}) collective-permute-start(bf16[384,128]{1,0:T(8,128)(2,1)S(1)} %get-tuple-element.9), channel_id=1, source_target_pairs={{0,2},{1,3},{2,0},{3,1},{4,6},{5,7},{6,4},{7,5},{8,10},{9,11},{10,... | collective-permute-start | bytes 294920 | tf_op jit(solution)/shard_map/ppermute | solution.py:97
  176.8 5.1 %collective-permute-start.5 = (bf16[384,128]{1,0:T(8,128)(2,1)S(1)}, bf16[384,128]{1,0:T(8,128)(2,1)S(1)}, u32[]{:S(2)}, u32[]{:S(2)}) collective-permute-start(bf16[384,128]{1,0:T(8,128)(2,1)S(1)} %get-tuple-element.8), channel_id=1, source_target_pairs={{0,3},{1,2},{2,1},{3,0},{4,7},{5,6},{6,5},{7,4},{8,11},{9,10},{10,... | collective-permute-start | bytes 294920 | tf_op jit(solution)/shard_map/ppermute | solution.py:97
  184.5 13.3 %collective-permute-start.10 = (f32[2,128,512]{2,1,0:T(8,128)S(1)}, f32[2,128,512]{2,1,0:T(8,128)S(1)}, u32[]{:S(2)}, u32[]{:S(2)}) collective-permute-start(f32[2,128,512]{2,1,0:T(8,128)S(1)} %slice_select_fusion), channel_id=1, source_target_pairs={{0,2},{1,3},{2,0},{3,1},{4,6},{5,7},{6,4},{7,5},{8,10},{9,11},{10,... | collective-permute-start | bytes 1572872 | tf_op jit(solution)/shard_map/ppermute | solution.py:79
  198.0 2.4 collective-permute-start.11
  200.4 13.0 %collective-permute-start.12 = (f32[128,512]{1,0:T(8,128)S(1)}, f32[128,512]{1,0:T(8,128)S(1)}, u32[]{:S(2)}, u32[]{:S(2)}) collective-permute-start(f32[128,512]{1,0:T(8,128)S(1)} %add_bitcast_fusion), channel_id=1, source_target_pairs={{0,4},{4,0},{8,12},{12,8},{16,20},{20,16},{24,28},{28,24},{32,36},... | collective-permute-start | bytes 786440 | tf_op jit(solution)/shard_map/ppermute | solution.py:65
  213.4 8.8 %collective-permute-start.13 = (f32[128,512]{1,0:T(8,128)S(1)}, f32[128,512]{1,0:T(8,128)S(1)}, u32[]{:S(2)}, u32[]{:S(2)}) collective-permute-start(f32[128,512]{1,0:T(8,128)S(1)} %add.134), channel_id=1, source_target_pairs={{0,8},{4,12},{8,0},{12,4},{16,24},{20,28},{24,16},{28,20},{32,40},... | collective-permute-start | bytes 786440 | tf_op jit(solution)/shard_map/ppermute | solution.py:65
  222.3 8.0 %collective-permute-start.14 = (f32[128,512]{1,0:T(8,128)S(1)}, f32[128,512]{1,0:T(8,128)S(1)}, u32[]{:S(2)}, u32[]{:S(2)}) collective-permute-start(f32[128,512]{1,0:T(8,128)S(1)} %add.135), channel_id=1, source_target_pairs={{0,16},{4,20},{8,24},{12,28},{16,0},{20,4},{24,8},{28,12},{32,48},... | collective-permute-start | bytes 786440 | tf_op jit(solution)/shard_map/ppermute | solution.py:65
  230.3 13.4 %collective-permute-start.15 = (f32[128,512]{1,0:T(8,128)S(1)}, f32[128,512]{1,0:T(8,128)S(1)}, u32[]{:S(2)}, u32[]{:S(2)}) collective-permute-start(f32[128,512]{1,0:T(8,128)S(1)} %add.136), channel_id=1, source_target_pairs={{0,32},{4,36},{8,40},{12,44},{16,48},{20,52},{24,56},{28,60},{32,0... | collective-permute-start | bytes 786440 | tf_op jit(solution)/shard_map/ppermute | solution.py:65
  243.7 14.4 %collective-permute-start.16 = (f32[128,512]{1,0:T(8,128)S(1)}, f32[128,512]{1,0:T(8,128)S(1)}, u32[]{:S(2)}, u32[]{:S(2)}) collective-permute-start(f32[128,512]{1,0:T(8,128)S(1)} %add.137), channel_id=1, source_target_pairs={{0,64},{4,68},{8,72},{12,76},{16,80},{20,84},{24,88},{28,92},{32,9... | collective-permute-start | bytes 786440 | tf_op jit(solution)/shard_map/ppermute | solution.py:65
Sparse Core Ops, SparseCore 0:
  11.0 132.1 all-gather.2
  183.9 102.3 all-gather.4

commit v12 on v10

--- a/solution.py
+++ b/solution.py
@@ -85,7 +85,7 @@
 REP = ("xl", "c")
 
 
-def exchange(parts, size, far=False):
+def exchange(parts, size, far=False, ordered=True):
     me = lax.axis_index(REP)
     axis = ("xh",) + REP if far else REP
     got = []
@@ -96,7 +96,8 @@
         elif s:
             send = lax.ppermute(send, axis, xor_pairs(size, s))
         got.append(send)
-    return jnp.take(jnp.stack(got), jnp.arange(size) ^ me, axis=0)
+    got = jnp.stack(got)
+    return jnp.take(got, jnp.arange(size) ^ me, axis=0) if ordered else got
 
 
 def hier_gather(x):
@@ -106,8 +107,11 @@
     return lax.all_gather(pair, ("y", "z"), axis=0, tiled=True)
 
 
-def hier_positions(positions, local_blocks, n_z, n_xh, n_y):
+def hier_positions(positions, local_blocks, n_z, n_xh, n_y, piece_blocks=None):
     owner, block = positions // local_blocks, positions % local_blocks
+    if piece_blocks:
+        piece = (block // piece_blocks) ^ lax.axis_index(REP)
+        block = piece * piece_blocks + block % piece_blocks
     z, xh, y = owner // (n_xh * n_y), (owner // n_y) % n_xh, owner % n_y
     slot = xh ^ lax.axis_index("xh")
     return ((y * n_z + z) * n_xh + slot) * local_blocks + block
@@ -121,12 +125,15 @@
     bs = adjacency_tiles.shape[2]
     w_split = weight.reshape(n_rep, feat_dev, f_all)
     positions = column_positions(block_cols, block_perm)
-    positions = hier_positions(positions, node_features.shape[0] // bs, n_z, n_xh, n_y)
+    raw, lb = positions, node_features.shape[0] // bs
+    positions = hier_positions(raw, lb, n_z, n_xh, n_y)
     gathered = hier_gather(node_features)
     aggregate = block_product(adjacency_tiles, positions, gathered)
     rows = aggregate.shape[0] // n_rep
-    agg_rows = exchange(aggregate.reshape(n_rep, rows, feat_dev), n_rep)
-    preact = jnp.einsum("irf,ifo->ro", agg_rows, w_split, preferred_element_type=jnp.float32)
+    flip = jnp.arange(n_rep) ^ lax.axis_index(REP)
+    agg_got = exchange(aggregate.reshape(n_rep, rows, feat_dev), n_rep, ordered=False)
+    w_got = jnp.take(w_split, flip, axis=0)
+    preact = jnp.einsum("irf,ifo->ro", agg_got, w_got, preferred_element_type=jnp.float32)
     gating = jax.nn.sigmoid(preact)
     activated = (preact * gating).astype(jnp.bfloat16)
     slopes = gating * (1.0 + preact * (1.0 - gating))
@@ -134,9 +141,13 @@
     grad_split = jnp.einsum(
         "rf,jof->jro", grad_pre, w_split, preferred_element_type=jnp.float32
     ).astype(jnp.bfloat16)
-    pair = jnp.concatenate([exchange(grad_split, n_rep), exchange(grad_split, n_rep, far=True)])
+    own = exchange(grad_split, n_rep, ordered=False)
+    far = exchange(grad_split, n_rep, far=True, ordered=False)
+    pair = jnp.concatenate([own, far])
     gathered_grad = lax.all_gather(pair.reshape(-1, feat_dev), ("y", "z"), axis=0, tiled=True)
-    feature_grad = block_product(adjacency_tiles, positions, gathered_grad)
+    grad_positions = hier_positions(raw, lb, n_z, n_xh, n_y, rows // bs)
+    feature_grad = block_product(adjacency_tiles, grad_positions, gathered_grad)
+    agg_rows = jnp.take(agg_got, flip, axis=0)
     weight_part = jnp.einsum("irf,ro->ifo", agg_rows, grad_pre, preferred_element_type=jnp.float32)
     weight_rows = halving_scatter(weight_part, REP, n_rep)
     node_total = node_features.shape[0] * n_blk

time: 281 us -> 281 us (level)
  starting transfers between devices: 29.5 us -> 33.1 us
  waiting for transfers between devices: 196 us -> 193 us
    ppermute x4, waiting for transfers between devices: 5.87 us -> 2.56 us  [exchange(): send = lax.ppermute(send, axis, xor_pairs(2 * size, size + s))]
where the time goes in v12:
time: 281 us
  waiting for transfers between devices  193 us (69%)
  starting transfers between devices  33.1 us (12%)
  Pallas kernels  29.7 us (11%)
  between operations  14.4 us (5%)
  local copies, waits for them, and re-layouts  5.65 us (2%)
    all_gather x1, waiting for transfers between devices, hier_gather(): return lax.all_gather(pair, ('y', 'z'), axis=0, tiled=True)  90.4 us
    ppermute x5, waiting for transfers between devices, butterfly_sum(): x = x + lax.ppermute(x, axis, xor_pairs(size, bit))  47.8 us
    pallas_call x2, Pallas kernels, block_product(): pl.pallas_call(_product_kernel, grid_spec=pltpu.PrefetchScalarGridSpec(nu...  29.7 us
    all_gather x1, waiting for transfers between devices, local(): lax.all_gather(pair.reshape(-1, feat_dev), ('y', 'z'), axis=0, tiled=True)  28.8 us
    ppermute x2, waiting for transfers between devices, halving_scatter(): parts = keep + lax.ppermute(send, axis, xor_pairs(size, bit))  11.3 us
    ppermute x5, starting transfers between devices, butterfly_sum(): x = x + lax.ppermute(x, axis, xor_pairs(size, bit))  10.5 us
    ppermute x6, waiting for transfers between devices, exchange(): send = lax.ppermute(send, axis, xor_pairs(size, s))  7.02 us
    ppermute x4, starting transfers between devices, exchange(): send = lax.ppermute(send, axis, xor_pairs(2 * size, size + s))  6.89 us
  transfers between devices with their start and end apart: 23, of which 17 were waited for; matrix products, arithmetic and copies ran while one was open for 2% of the time, Pallas kernels for 0%

profile of v12, /device:TPU:1, one launch (start us, length us, event | category | flops | bytes accessed | tf_op | source)
XLA Modules:
  0.0 280.9 jit_solution(14090079880797525501)
XLA Ops:
  7.2 0.0 copy-start
  7.2 0.0 all-gather.3.cloned.1.call-start
  7.2 1.1 fusion.31
  8.3 3.6 %collective-permute-start = (bf16[384,128]{1,0:T(8,128)(2,1)S(1)}, bf16[384,128]{1,0:T(8,128)(2,1)S(1)}, u32[]{:S(2)}, u32[]{:S(2)}) collective-permute-start(bf16[384,128]{1,0:T(8,128)(2,1)S(1)} %get-tuple-element.18), channel_id=1, source_target_pairs={{0,16},{16,0},{1,17},{17,1},{2,18},{18,2},{3,19},{19,3},{4,20},{20... | collective-permute-start | bytes 294920 | tf_op jit(solution)/shard_map/ppermute | solution.py:105
  12.0 0.1 collective-permute-start.1
  12.1 2.9 %collective-permute-start.2 = (bf16[384,128]{1,0:T(8,128)(2,1)S(1)}, bf16[384,128]{1,0:T(8,128)(2,1)S(1)}, u32[]{:S(2)}, u32[]{:S(2)}) collective-permute-start(bf16[384,128]{1,0:T(8,128)(2,1)S(1)} %get-tuple-element.16), channel_id=1, source_target_pairs={{0,16},{16,0},{1,17},{17,1},{2,18},{18,2},{3,19},{19,3},{4,20},{20... | collective-permute-start | bytes 294920 | tf_op jit(solution)/shard_map/ppermute | solution.py:105
  15.0 0.1 collective-permute-start.3
  15.0 1.0 constant_dynamic-update-slice_fusion.4
  16.1 0.0 collective-permute-done
  16.1 0.8 collective-permute-done.1
  17.0 2.0 collective-permute-done.2
  19.0 2.3 collective-permute-done.3
  21.3 0.9 copy-done.1
  22.2 0.0 all-gather.3.cloned.1.call-update
  22.2 0.0 all-gather.5.cloned.1.call-start
  22.3 1.1 select_reduce_fusion
  23.5 0.1 rem.91
  23.5 0.1 div.42
  23.6 0.1 ne.117
  23.8 0.6 gather_fusion
  24.4 90.4 %all-gather.3.cloned.1.call-done = bf16[49152,128]{1,0:T(8,128)(2,1)} async-done(((bf16[3072,128]{1,0:T(8,128)(2,1)}), bf16[49152,128]{1,0:T(8,128)(2,1)}) %all-gather.3.cloned.1.call-update) | async-done | bytes 12582928 | tf_op jit(solution)/shard_map/all_gather | solution.py:107
  114.8 14.5 %shard_map.85 = bf16[12,128,128]{2,1,0:T(8,128)(2,1)S(1)} custom-call(s32[672]{0:T(1024)S(1)} %fusion.26.pos_ref, bf16[12,56,128,128]{3,2,1,0:T(8,128)(2,1)} %a_ref.3, bf16[384,128,128]{2,1,0:T(8,128)(2,1)} %bitcast.55), custom_call_target="tpu_custom_call" | custom-call | flops 2818572288 | bytes 34996224 | tf_op jit(solution)/shard_map/pallas_call | solution.py:38
  129.4 0.9 collective-permute-start.4
  130.3 1.2 collective-permute-start.5
  131.5 0.5 collective-permute-start.6
  132.1 2.5 collective-permute-done.5
  134.6 2.4 collective-permute-done.6
  137.0 1.5 multiply_convert_fusion
  138.4 0.4 convolution_convert_fusion
  138.9 0.2 collective-permute-start.7
  139.1 3.0 %collective-permute-start.11 = (bf16[384,128]{1,0:T(8,128)(2,1)S(1)}, bf16[384,128]{1,0:T(8,128)(2,1)S(1)}, u32[]{:S(2)}, u32[]{:S(2)}) collective-permute-start(bf16[384,128]{1,0:T(8,128)(2,1)S(1)} %get-tuple-element.10), channel_id=1, source_target_pairs={{0,17},{1,16},{2,19},{3,18},{16,1},{17,0},{18,3},{19,2},{4,21},{5,... | collective-permute-start | bytes 294920 | tf_op jit(solution)/shard_map/ppermute | solution.py:95
  142.0 0.3 collective-permute-start.8
  142.3 0.6 collective-permute-start.12
  142.9 1.4 collective-permute-start.9
  144.4 1.6 collective-permute-start.13
  146.0 1.5 collective-permute-done.8
  147.5 1.8 collective-permute-start.10
  149.3 0.6 collective-permute-done.9
  149.9 2.6 collective-permute-done.10
  152.6 0.9 copy-done.2
  153.5 0.0 all-gather.5.cloned.1.call-update
  153.5 0.1 pad_maximum_fusion
  153.6 0.6 gather_fusion.1
  154.2 0.6 fusion.2
  154.8 0.1 slice_select_fusion
  154.9 1.3 collective-permute-start.14
  156.1 10.1 %collective-permute-done.14 = f32[2,128,512]{2,1,0:T(8,128)S(1)} collective-permute-done((f32[2,128,512]{2,1,0:T(8,128)S(1)}, f32[2,128,512]{2,1,0:T(8,128)S(1)}, u32[]{:S(2)}, u32[]{:S(2)}) %collective-permute-start.14) | collective-permute-done | bytes 524320 | tf_op jit(solution)/shard_map/ppermute | solution.py:79
  166.3 0.1 select_add_fusion
  166.5 3.1 %collective-permute-start.15 = (f32[1,128,512]{2,1,0:T(8,128)S(1)}, f32[1,128,512]{2,1,0:T(8,128)S(1)}, u32[]{:S(2)}, u32[]{:S(2)}) collective-permute-start(f32[1,128,512]{2,1,0:T(8,128)S(1)} %slice_select_fusion.1), channel_id=1, source_target_pairs={{0,1},{1,0},{2,3},{3,2},{4,5},{5,4},{6,7},{7,6},{8,9},{9,8},{10,11... | collective-permute-start | bytes 786440 | tf_op jit(solution)/shard_map/ppermute | solution.py:79
  169.6 1.2 collective-permute-done.15
  170.7 0.1 add_bitcast_fusion
  170.8 1.3 collective-permute-start.16
  172.1 12.3 %collective-permute-done.16 = f32[128,512]{1,0:T(8,128)S(1)} collective-permute-done((f32[128,512]{1,0:T(8,128)S(1)}, f32[128,512]{1,0:T(8,128)S(1)}, u32[]{:S(2)}, u32[]{:S(2)}) %collective-permute-start.16) | collective-permute-done | bytes 262176 | tf_op jit(solution)/shard_map/ppermute | solution.py:65
  184.5 2.8 %collective-permute-start.17 = (f32[128,512]{1,0:T(8,128)S(1)}, f32[128,512]{1,0:T(8,128)S(1)}, u32[]{:S(2)}, u32[]{:S(2)}) collective-permute-start(f32[128,512]{1,0:T(8,128)S(1)} %add.159), channel_id=1, source_target_pairs={{0,8},{4,12},{8,0},{12,4},{16,24},{20,28},{24,16},{28,20},{32,40},... | collective-permute-start | bytes 786440 | tf_op jit(solution)/shard_map/ppermute | solution.py:65
  187.3 5.4 %collective-permute-done.17 = f32[128,512]{1,0:T(8,128)S(1)} collective-permute-done((f32[128,512]{1,0:T(8,128)S(1)}, f32[128,512]{1,0:T(8,128)S(1)}, u32[]{:S(2)}, u32[]{:S(2)}) %collective-permute-start.17) | collective-permute-done | bytes 262176 | tf_op jit(solution)/shard_map/ppermute | solution.py:65
  192.7 1.0 collective-permute-start.18
  193.7 6.4 %collective-permute-done.18 = f32[128,512]{1,0:T(8,128)S(1)} collective-permute-done((f32[128,512]{1,0:T(8,128)S(1)}, f32[128,512]{1,0:T(8,128)S(1)}, u32[]{:S(2)}, u32[]{:S(2)}) %collective-permute-start.18) | collective-permute-done | bytes 262176 | tf_op jit(solution)/shard_map/ppermute | solution.py:65
  200.1 2.4 collective-permute-start.19
  202.5 11.9 %collective-permute-done.19 = f32[128,512]{1,0:T(8,128)S(1)} collective-permute-done((f32[128,512]{1,0:T(8,128)S(1)}, f32[128,512]{1,0:T(8,128)S(1)}, u32[]{:S(2)}, u32[]{:S(2)}) %collective-permute-start.19) | collective-permute-done | bytes 262176 | tf_op jit(solution)/shard_map/ppermute | solution.py:65
  214.4 3.0 %collective-permute-start.20 = (f32[128,512]{1,0:T(8,128)S(1)}, f32[128,512]{1,0:T(8,128)S(1)}, u32[]{:S(2)}, u32[]{:S(2)}) collective-permute-start(f32[128,512]{1,0:T(8,128)S(1)} %add.162), channel_id=1, source_target_pairs={{0,64},{4,68},{8,72},{12,76},{16,80},{20,84},{24,88},{28,92},{32,9... | collective-permute-start | bytes 786440 | tf_op jit(solution)/shard_map/ppermute | solution.py:65
  217.4 11.8 %collective-permute-done.20 = f32[128,512]{1,0:T(8,128)S(1)} collective-permute-done((f32[128,512]{1,0:T(8,128)S(1)}, f32[128,512]{1,0:T(8,128)S(1)}, u32[]{:S(2)}, u32[]{:S(2)}) %collective-permute-start.20) | collective-permute-done | bytes 262176 | tf_op jit(solution)/shard_map/ppermute | solution.py:65
  229.2 0.7 add_multiply_fusion
  230.0 28.8 %all-gather.5.cloned.1.call-done = bf16[49152,128]{1,0:T(8,128)(2,1)} async-done(((bf16[3072,128]{1,0:T(8,128)(2,1)}), bf16[49152,128]{1,0:T(8,128)(2,1)}) %all-gather.5.cloned.1.call-update) | async-done | bytes 12582928 | tf_op jit(solution)/shard_map/all_gather | solution.py:147
  258.8 15.2 %shard_map.86 = bf16[12,128,128]{2,1,0:T(8,128)(2,1)} custom-call(s32[672]{0:T(1024)S(1)} %get-tuple-element.3.pos_ref, bf16[12,56,128,128]{3,2,1,0:T(8,128)(2,1)} %a_ref.3, bf16[384,128,128]{2,1,0:T(8,128)(2,1)} %bitcast.54), custom_call_target="tpu_custom_call" | custom-call | flops 2818572288 | bytes 34996224 | tf_op jit(solution)/shard_map/pallas_call | solution.py:38
  (36 shorter events, 0.5 us)
Async XLA Ops:
  7.2 16.6 %copy-start = (bf16[512,512]{1,0:T(8,128)(2,1)S(1)}, bf16[512,512]{1,0:T(8,128)(2,1)}, u32[]{:S(2)}) copy-start(bf16[512,512]{1,0:T(8,128)(2,1)} %param.7) | copy-start | bytes 1572868
  7.2 107.7 %all-gather.3.cloned.1.call-start = ((), (), s32[]{:S(2)}) async-start(), calls=%async_computation | async-start | bytes 13369344 | tf_op jit(solution)/shard_map/all_gather | solution.py:107
  8.3 7.7 %collective-permute-start = (bf16[384,128]{1,0:T(8,128)(2,1)S(1)}, bf16[384,128]{1,0:T(8,128)(2,1)S(1)}, u32[]{:S(2)}, u32[]{:S(2)}) collective-permute-start(bf16[384,128]{1,0:T(8,128)(2,1)S(1)} %get-tuple-element.18), channel_id=1, source_target_pairs={{0,16},{16,0},{1,17},{17,1},{2,18},{18,2},{3,19},{19,3},{4,20},{20... | collective-permute-start | bytes 294920 | tf_op jit(solution)/shard_map/ppermute | solution.py:105
  12.0 5.0 %collective-permute-start.1 = (bf16[384,128]{1,0:T(8,128)(2,1)S(1)}, bf16[384,128]{1,0:T(8,128)(2,1)S(1)}, u32[]{:S(2)}, u32[]{:S(2)}) collective-permute-start(bf16[384,128]{1,0:T(8,128)(2,1)S(1)} %get-tuple-element.17), channel_id=1, source_target_pairs={{0,16},{16,0},{1,17},{17,1},{2,18},{18,2},{3,19},{19,3},{4,20},{20... | collective-permute-start | bytes 294920 | tf_op jit(solution)/shard_map/ppermute | solution.py:105
  12.1 6.9 %collective-permute-start.2 = (bf16[384,128]{1,0:T(8,128)(2,1)S(1)}, bf16[384,128]{1,0:T(8,128)(2,1)S(1)}, u32[]{:S(2)}, u32[]{:S(2)}) collective-permute-start(bf16[384,128]{1,0:T(8,128)(2,1)S(1)} %get-tuple-element.16), channel_id=1, source_target_pairs={{0,16},{16,0},{1,17},{17,1},{2,18},{18,2},{3,19},{19,3},{4,20},{20... | collective-permute-start | bytes 294920 | tf_op jit(solution)/shard_map/ppermute | solution.py:105
  15.0 6.3 %collective-permute-start.3 = (bf16[384,128]{1,0:T(8,128)(2,1)S(1)}, bf16[384,128]{1,0:T(8,128)(2,1)S(1)}, u32[]{:S(2)}, u32[]{:S(2)}) collective-permute-start(bf16[384,128]{1,0:T(8,128)(2,1)S(1)} %get-tuple-element.15), channel_id=1, source_target_pairs={{0,16},{16,0},{1,17},{17,1},{2,18},{18,2},{3,19},{19,3},{4,20},{20... | collective-permute-start | bytes 294920 | tf_op jit(solution)/shard_map/ppermute | solution.py:105
  21.3 0.9 copy-start.1
  22.2 236.6 %all-gather.5.cloned.1.call-start = ((), (), s32[]{:S(2)}) async-start(), calls=%async_computation.1 | async-start | bytes 13369344 | tf_op jit(solution)/shard_map/all_gather | solution.py:147
  114.8 22.1 %copy-start.3 = (bf16[384,512]{1,0:T(8,128)(2,1)S(1)}, bf16[384,512]{1,0:T(8,128)(2,1)}, u32[]{:S(2)}) copy-start(bf16[384,512]{1,0:T(8,128)(2,1)} %param.8) | copy-start | bytes 1179652
  129.4 2.7 collective-permute-start.4
  130.3 4.3 %collective-permute-start.5 = (bf16[384,128]{1,0:T(8,128)(2,1)S(1)}, bf16[384,128]{1,0:T(8,128)(2,1)S(1)}, u32[]{:S(2)}, u32[]{:S(2)}) collective-permute-start(bf16[384,128]{1,0:T(8,128)(2,1)S(1)} %get-tuple-element.13), channel_id=1, source_target_pairs={{0,2},{1,3},{2,0},{3,1},{4,6},{5,7},{6,4},{7,5},{8,10},{9,11},{10,... | collective-permute-start | bytes 294920 | tf_op jit(solution)/shard_map/ppermute | solution.py:97
  131.5 5.4 %collective-permute-start.6 = (bf16[384,128]{1,0:T(8,128)(2,1)S(1)}, bf16[384,128]{1,0:T(8,128)(2,1)S(1)}, u32[]{:S(2)}, u32[]{:S(2)}) collective-permute-start(bf16[384,128]{1,0:T(8,128)(2,1)S(1)} %get-tuple-element.12), channel_id=1, source_target_pairs={{0,3},{1,2},{2,1},{3,0},{4,7},{5,6},{6,5},{7,4},{8,11},{9,10},{10,... | collective-permute-start | bytes 294920 | tf_op jit(solution)/shard_map/ppermute | solution.py:97
  138.9 5.5 %collective-permute-start.7 = (bf16[384,128]{1,0:T(8,128)(2,1)S(1)}, bf16[384,128]{1,0:T(8,128)(2,1)S(1)}, u32[]{:S(2)}, u32[]{:S(2)}) collective-permute-start(bf16[384,128]{1,0:T(8,128)(2,1)S(1)} %get-tuple-element.10), channel_id=1, source_target_pairs={{0,1},{1,0},{2,3},{3,2},{4,5},{5,4},{6,7},{7,6},{8,9},{9,8},{10,11... | collective-permute-start | bytes 294920 | tf_op jit(solution)/shard_map/ppermute | solution.py:97
  139.1 13.4 %collective-permute-start.11 = (bf16[384,128]{1,0:T(8,128)(2,1)S(1)}, bf16[384,128]{1,0:T(8,128)(2,1)S(1)}, u32[]{:S(2)}, u32[]{:S(2)}) collective-permute-start(bf16[384,128]{1,0:T(8,128)(2,1)S(1)} %get-tuple-element.10), channel_id=1, source_target_pairs={{0,17},{1,16},{2,19},{3,18},{16,1},{17,0},{18,3},{19,2},{4,21},{5,... | collective-permute-start | bytes 294920 | tf_op jit(solution)/shard_map/ppermute | solution.py:95
  142.0 5.4 %collective-permute-start.8 = (bf16[384,128]{1,0:T(8,128)(2,1)S(1)}, bf16[384,128]{1,0:T(8,128)(2,1)S(1)}, u32[]{:S(2)}, u32[]{:S(2)}) collective-permute-start(bf16[384,128]{1,0:T(8,128)(2,1)S(1)} %get-tuple-element.9), channel_id=1, source_target_pairs={{0,2},{1,3},{2,0},{3,1},{4,6},{5,7},{6,4},{7,5},{8,10},{9,11},{10,... | collective-permute-start | bytes 294920 | tf_op jit(solution)/shard_map/ppermute | solution.py:97
  142.3 10.2 %collective-permute-start.12 = (bf16[384,128]{1,0:T(8,128)(2,1)S(1)}, bf16[384,128]{1,0:T(8,128)(2,1)S(1)}, u32[]{:S(2)}, u32[]{:S(2)}) collective-permute-start(bf16[384,128]{1,0:T(8,128)(2,1)S(1)} %get-tuple-element.9), channel_id=1, source_target_pairs={{0,18},{1,19},{2,16},{3,17},{16,2},{17,3},{18,0},{19,1},{4,22},{5,... | collective-permute-start | bytes 294920 | tf_op jit(solution)/shard_map/ppermute | solution.py:95
  142.9 7.0 %collective-permute-start.9 = (bf16[384,128]{1,0:T(8,128)(2,1)S(1)}, bf16[384,128]{1,0:T(8,128)(2,1)S(1)}, u32[]{:S(2)}, u32[]{:S(2)}) collective-permute-start(bf16[384,128]{1,0:T(8,128)(2,1)S(1)} %get-tuple-element.8), channel_id=1, source_target_pairs={{0,3},{1,2},{2,1},{3,0},{4,7},{5,6},{6,5},{7,4},{8,11},{9,10},{10,... | collective-permute-start | bytes 294920 | tf_op jit(solution)/shard_map/ppermute | solution.py:97
  144.4 8.2 %collective-permute-start.13 = (bf16[384,128]{1,0:T(8,128)(2,1)S(1)}, bf16[384,128]{1,0:T(8,128)(2,1)S(1)}, u32[]{:S(2)}, u32[]{:S(2)}) collective-permute-start(bf16[384,128]{1,0:T(8,128)(2,1)S(1)} %get-tuple-element.8), channel_id=1, source_target_pairs={{0,19},{1,18},{2,17},{3,16},{16,3},{17,2},{18,1},{19,0},{4,23},{5,... | collective-permute-start | bytes 294920 | tf_op jit(solution)/shard_map/ppermute | solution.py:95
  147.5 5.0 %collective-permute-start.10 = (bf16[384,128]{1,0:T(8,128)(2,1)S(1)}, bf16[384,128]{1,0:T(8,128)(2,1)S(1)}, u32[]{:S(2)}, u32[]{:S(2)}) collective-permute-start(bf16[384,128]{1,0:T(8,128)(2,1)S(1)} %get-tuple-element.7), channel_id=1, source_target_pairs={{0,16},{1,17},{2,18},{3,19},{16,0},{17,1},{18,2},{19,3},{4,20},{5,... | collective-permute-start | bytes 294920 | tf_op jit(solution)/shard_map/ppermute | solution.py:95
  152.6 0.9 copy-start.2
  154.9 11.4 %collective-permute-start.14 = (f32[2,128,512]{2,1,0:T(8,128)S(1)}, f32[2,128,512]{2,1,0:T(8,128)S(1)}, u32[]{:S(2)}, u32[]{:S(2)}) collective-permute-start(f32[2,128,512]{2,1,0:T(8,128)S(1)} %slice_select_fusion), channel_id=1, source_target_pairs={{0,2},{1,3},{2,0},{3,1},{4,6},{5,7},{6,4},{7,5},{8,10},{9,11},{10,... | collective-permute-start | bytes 1572872 | tf_op jit(solution)/shard_map/ppermute | solution.py:79
  166.5 4.3 %collective-permute-start.15 = (f32[1,128,512]{2,1,0:T(8,128)S(1)}, f32[1,128,512]{2,1,0:T(8,128)S(1)}, u32[]{:S(2)}, u32[]{:S(2)}) collective-permute-start(f32[1,128,512]{2,1,0:T(8,128)S(1)} %slice_select_fusion.1), channel_id=1, source_target_pairs={{0,1},{1,0},{2,3},{3,2},{4,5},{5,4},{6,7},{7,6},{8,9},{9,8},{10,11... | collective-permute-start | bytes 786440 | tf_op jit(solution)/shard_map/ppermute | solution.py:79
  170.8 13.6 %collective-permute-start.16 = (f32[128,512]{1,0:T(8,128)S(1)}, f32[128,512]{1,0:T(8,128)S(1)}, u32[]{:S(2)}, u32[]{:S(2)}) collective-permute-start(f32[128,512]{1,0:T(8,128)S(1)} %add_bitcast_fusion), channel_id=1, source_target_pairs={{0,4},{4,0},{8,12},{12,8},{16,20},{20,16},{24,28},{28,24},{32,36},... | collective-permute-start | bytes 786440 | tf_op jit(solution)/shard_map/ppermute | solution.py:65
  184.5 8.2 %collective-permute-start.17 = (f32[128,512]{1,0:T(8,128)S(1)}, f32[128,512]{1,0:T(8,128)S(1)}, u32[]{:S(2)}, u32[]{:S(2)}) collective-permute-start(f32[128,512]{1,0:T(8,128)S(1)} %add.159), channel_id=1, source_target_pairs={{0,8},{4,12},{8,0},{12,4},{16,24},{20,28},{24,16},{28,20},{32,40},... | collective-permute-start | bytes 786440 | tf_op jit(solution)/shard_map/ppermute | solution.py:65
  192.7 7.4 %collective-permute-start.18 = (f32[128,512]{1,0:T(8,128)S(1)}, f32[128,512]{1,0:T(8,128)S(1)}, u32[]{:S(2)}, u32[]{:S(2)}) collective-permute-start(f32[128,512]{1,0:T(8,128)S(1)} %add.160), channel_id=1, source_target_pairs={{0,16},{4,20},{8,24},{12,28},{16,0},{20,4},{24,8},{28,12},{32,48},... | collective-permute-start | bytes 786440 | tf_op jit(solution)/shard_map/ppermute | solution.py:65
  200.1 14.3 %collective-permute-start.19 = (f32[128,512]{1,0:T(8,128)S(1)}, f32[128,512]{1,0:T(8,128)S(1)}, u32[]{:S(2)}, u32[]{:S(2)}) collective-permute-start(f32[128,512]{1,0:T(8,128)S(1)} %add.161), channel_id=1, source_target_pairs={{0,32},{4,36},{8,40},{12,44},{16,48},{20,52},{24,56},{28,60},{32,0... | collective-permute-start | bytes 786440 | tf_op jit(solution)/shard_map/ppermute | solution.py:65
  214.4 14.8 %collective-permute-start.20 = (f32[128,512]{1,0:T(8,128)S(1)}, f32[128,512]{1,0:T(8,128)S(1)}, u32[]{:S(2)}, u32[]{:S(2)}) collective-permute-start(f32[128,512]{1,0:T(8,128)S(1)} %add.162), channel_id=1, source_target_pairs={{0,64},{4,68},{8,72},{12,76},{16,80},{20,84},{24,88},{28,92},{32,9... | collective-permute-start | bytes 786440 | tf_op jit(solution)/shard_map/ppermute | solution.py:65
Sparse Core Ops, SparseCore 0:
  22.4 92.4 all-gather.2
  153.6 105.1 all-gather.4

commit v13 on v12

--- a/solution.py
+++ b/solution.py
@@ -81,6 +81,16 @@
     return parts[0]
 
 
+def doubling_gather(x, axis, size):
+    me = lax.axis_index(axis)
+    bit = 1
+    while bit < size:
+        got = lax.ppermute(x, axis, xor_pairs(size, bit))
+        x = jnp.where((me & bit) != 0, jnp.concatenate([got, x]), jnp.concatenate([x, got]))
+        bit *= 2
+    return x
+
+
 BLK = ("z", "xh", "y")
 REP = ("xl", "c")
 
@@ -151,7 +161,9 @@
     weight_part = jnp.einsum("irf,ro->ifo", agg_rows, grad_pre, preferred_element_type=jnp.float32)
     weight_rows = halving_scatter(weight_part, REP, n_rep)
     node_total = node_features.shape[0] * n_blk
-    weight_grad = butterfly_sum(weight_rows, BLK, n_blk) * (1.0 / math.sqrt(node_total))
+    quarter = halving_scatter(weight_rows.reshape(n_y, -1, f_all), "y", n_y)
+    quarter = butterfly_sum(quarter, ("z", "xh"), n_z * n_xh)
+    weight_grad = doubling_gather(quarter, "y", n_y) * (1.0 / math.sqrt(node_total))
     return (activated, feature_grad, weight_grad)
 
 

time: 281 us -> 272 us (0.968)
  waiting for transfers between devices: 193 us -> 179 us
  starting transfers between devices: 33.1 us -> 38 us
    ppermute x5 -> x3, waiting for transfers between devices: 47.8 us -> 6.81 us  [butterfly_sum(): x = x + lax.ppermute(x, axis, xor_pairs(size, bit))]
    ppermute x0 -> x2, waiting for transfers between devices: none -> 9.96 us  [doubling_gather(): got = lax.ppermute(x, axis, xor_pairs(size, bit))]
    ppermute x2 -> x4, waiting for transfers between devices: 11.3 us -> 20 us  [halving_scatter(): parts = keep + lax.ppermute(send, axis, xor_pairs(size, bit))]
    all_gather x1, waiting for transfers between devices: 28.8 us -> 37.2 us  [local(): lax.all_gather(pair.reshape(-1, feat_dev), ('y', 'z'), axis=0, tiled=True)]
    ppermute x0 -> x2, starting transfers between devices: none -> 4.23 us  [doubling_gather(): got = lax.ppermute(x, axis, xor_pairs(size, bit))]
    ppermute x2 -> x4, starting transfers between devices: 4.36 us -> 8.58 us  [halving_scatter(): parts = keep + lax.ppermute(send, axis, xor_pairs(size, bit))]
    ppermute x5 -> x3, starting transfers between devices: 10.5 us -> 6.93 us  [butterfly_sum(): x = x + lax.ppermute(x, axis, xor_pairs(size, bit))]
  transfers between devices with their start and end apart: 23 -> 25, of which waited for: 17 -> 19; matrix products, arithmetic and copies ran while one was open for 2% -> 2% of each run, Pallas kernels for 0% -> 0%
where the time goes in v13:
time: 272 us
  waiting for transfers between devices  179 us (66%)
  starting transfers between devices  38 us (14%)
  Pallas kernels  29.7 us (11%)
  between operations  14.4 us (5%)
  local copies, waits for them, and re-layouts  5.66 us (2%)
    all_gather x1, waiting for transfers between devices, hier_gather(): return lax.all_gather(pair, ('y', 'z'), axis=0, tiled=True)  90.4 us
    all_gather x1, waiting for transfers between devices, local(): lax.all_gather(pair.reshape(-1, feat_dev), ('y', 'z'), axis=0, tiled=True)  37.2 us
    pallas_call x2, Pallas kernels, block_product(): pl.pallas_call(_product_kernel, grid_spec=pltpu.PrefetchScalarGridSpec(nu...  29.7 us
    ppermute x4, waiting for transfers between devices, halving_scatter(): parts = keep + lax.ppermute(send, axis, xor_pairs(size, bit))  20 us
    ppermute x2, waiting for transfers between devices, doubling_gather(): got = lax.ppermute(x, axis, xor_pairs(size, bit))  9.96 us
    ppermute x4, starting transfers between devices, halving_scatter(): parts = keep + lax.ppermute(send, axis, xor_pairs(size, bit))  8.58 us
    ppermute x6, waiting for transfers between devices, exchange(): send = lax.ppermute(send, axis, xor_pairs(size, s))  7 us
    ppermute x3, starting transfers between devices, butterfly_sum(): x = x + lax.ppermute(x, axis, xor_pairs(size, bit))  6.93 us
  transfers between devices with their start and end apart: 25, of which 19 were waited for; matrix products, arithmetic and copies ran while one was open for 2% of the time, Pallas kernels for 0%

profile of v13, /device:TPU:1, one launch (start us, length us, event | category | flops | bytes accessed | tf_op | source)
XLA Modules:
  0.0 271.8 jit_solution(1116576123854746447)
XLA Ops:
  7.2 0.0 all-gather.3.cloned.1.call-start
  7.2 1.1 fusion.32
  8.3 3.6 %collective-permute-start = (bf16[384,128]{1,0:T(8,128)(2,1)S(1)}, bf16[384,128]{1,0:T(8,128)(2,1)S(1)}, u32[]{:S(2)}, u32[]{:S(2)}) collective-permute-start(bf16[384,128]{1,0:T(8,128)(2,1)S(1)} %get-tuple-element.18), channel_id=1, source_target_pairs={{0,16},{16,0},{1,17},{17,1},{2,18},{18,2},{3,19},{19,3},{4,20},{20... | collective-permute-start | bytes 294920 | tf_op jit(solution)/shard_map/ppermute | solution.py:115
  12.0 0.1 collective-permute-start.1
  12.1 2.9 %collective-permute-start.2 = (bf16[384,128]{1,0:T(8,128)(2,1)S(1)}, bf16[384,128]{1,0:T(8,128)(2,1)S(1)}, u32[]{:S(2)}, u32[]{:S(2)}) collective-permute-start(bf16[384,128]{1,0:T(8,128)(2,1)S(1)} %get-tuple-element.16), channel_id=1, source_target_pairs={{0,16},{16,0},{1,17},{17,1},{2,18},{18,2},{3,19},{19,3},{4,20},{20... | collective-permute-start | bytes 294920 | tf_op jit(solution)/shard_map/ppermute | solution.py:115
  15.0 0.1 collective-permute-start.3
  15.0 1.0 constant_dynamic-update-slice_fusion.4
  16.1 0.8 collective-permute-done.1
  17.0 2.0 collective-permute-done.2
  19.0 2.3 collective-permute-done.3
  21.3 0.9 copy-done.1
  22.2 0.0 all-gather.5.cloned.1.call-start
  22.3 1.1 select_reduce_fusion
  23.5 0.1 rem.91
  23.5 0.1 div.42
  23.6 0.1 ne.125
  23.8 0.6 gather_fusion
  24.4 90.4 %all-gather.3.cloned.1.call-done = bf16[49152,128]{1,0:T(8,128)(2,1)} async-done(((bf16[3072,128]{1,0:T(8,128)(2,1)}), bf16[49152,128]{1,0:T(8,128)(2,1)}) %all-gather.3.cloned.1.call-update) | async-done | bytes 12582928 | tf_op jit(solution)/shard_map/all_gather | solution.py:117
  114.9 14.5 %shard_map.85 = bf16[12,128,128]{2,1,0:T(8,128)(2,1)S(1)} custom-call(s32[672]{0:T(1024)S(1)} %fusion.27.pos_ref, bf16[12,56,128,128]{3,2,1,0:T(8,128)(2,1)} %a_ref.3, bf16[384,128,128]{2,1,0:T(8,128)(2,1)} %bitcast.57), custom_call_target="tpu_custom_call" | custom-call | flops 2818572288 | bytes 34996224 | tf_op jit(solution)/shard_map/pallas_call | solution.py:38
  129.4 0.9 collective-permute-start.4
  130.3 1.2 collective-permute-start.5
  131.5 0.5 collective-permute-start.6
  132.1 2.5 collective-permute-done.5
  134.6 2.4 collective-permute-done.6
  137.0 1.5 multiply_convert_fusion
  138.4 0.4 convolution_convert_fusion
  138.9 0.2 collective-permute-start.7
  139.1 3.0 %collective-permute-start.11 = (bf16[384,128]{1,0:T(8,128)(2,1)S(1)}, bf16[384,128]{1,0:T(8,128)(2,1)S(1)}, u32[]{:S(2)}, u32[]{:S(2)}) collective-permute-start(bf16[384,128]{1,0:T(8,128)(2,1)S(1)} %get-tuple-element.10), channel_id=1, source_target_pairs={{0,17},{1,16},{2,19},{3,18},{16,1},{17,0},{18,3},{19,2},{4,21},{5,... | collective-permute-start | bytes 294920 | tf_op jit(solution)/shard_map/ppermute | solution.py:105
  142.0 0.3 collective-permute-start.8
  142.3 0.6 collective-permute-start.12
  142.9 1.4 collective-permute-start.9
  144.4 1.6 collective-permute-start.13
  146.0 1.5 collective-permute-done.8
  147.5 1.8 collective-permute-start.10
  149.3 0.6 collective-permute-done.9
  149.9 2.6 collective-permute-done.10
  152.6 0.9 copy-done.2
  153.5 0.1 pad_maximum_fusion
  153.6 0.6 gather_fusion.1
  154.2 0.6 fusion.2
  154.8 0.1 slice_select_fusion
  154.9 1.2 collective-permute-start.14
  156.1 10.2 %collective-permute-done.14 = f32[2,128,512]{2,1,0:T(8,128)S(1)} collective-permute-done((f32[2,128,512]{2,1,0:T(8,128)S(1)}, f32[2,128,512]{2,1,0:T(8,128)S(1)}, u32[]{:S(2)}, u32[]{:S(2)}) %collective-permute-start.14) | collective-permute-done | bytes 524320 | tf_op jit(solution)/shard_map/ppermute | solution.py:79
  166.3 0.1 select_add_fusion
  166.5 3.1 %collective-permute-start.15 = (f32[1,128,512]{2,1,0:T(8,128)S(1)}, f32[1,128,512]{2,1,0:T(8,128)S(1)}, u32[]{:S(2)}, u32[]{:S(2)}) collective-permute-start(f32[1,128,512]{2,1,0:T(8,128)S(1)} %slice_select_fusion.1), channel_id=1, source_target_pairs={{0,1},{1,0},{2,3},{3,2},{4,5},{5,4},{6,7},{7,6},{8,9},{9,8},{10,11... | collective-permute-start | bytes 786440 | tf_op jit(solution)/shard_map/ppermute | solution.py:79
  169.6 1.2 collective-permute-done.15
  170.8 0.1 select_add_fusion.1
  170.8 2.8 %collective-permute-start.16 = (f32[2,32,512]{2,1,0:T(8,128)S(1)}, f32[2,32,512]{2,1,0:T(8,128)S(1)}, u32[]{:S(2)}, u32[]{:S(2)}) collective-permute-start(f32[2,32,512]{2,1,0:T(8,128)S(1)} %bitcast.61), channel_id=1, source_target_pairs={{0,8},{4,12},{8,0},{12,4},{1,9},{5,13},{9,1},{13,5},{2,10},{6,14},... | collective-permute-start | bytes 393224 | tf_op jit(solution)/shard_map/ppermute | solution.py:79
  173.6 6.6 %collective-permute-done.16 = f32[2,32,512]{2,1,0:T(8,128)S(1)} collective-permute-done((f32[2,32,512]{2,1,0:T(8,128)S(1)}, f32[2,32,512]{2,1,0:T(8,128)S(1)}, u32[]{:S(2)}, u32[]{:S(2)}) %collective-permute-start.16) | collective-permute-done | bytes 131104 | tf_op jit(solution)/shard_map/ppermute | solution.py:79
  180.2 1.4 collective-permute-start.17
  181.7 2.2 collective-permute-done.17
  183.9 2.7 collective-permute-start.18
  186.5 2.0 collective-permute-done.18
  188.6 1.3 collective-permute-start.19
  189.9 1.9 collective-permute-done.19
  191.8 2.9 %collective-permute-start.20 = (f32[32,512]{1,0:T(8,128)S(1)}, f32[32,512]{1,0:T(8,128)S(1)}, u32[]{:S(2)}, u32[]{:S(2)}) collective-permute-start(f32[32,512]{1,0:T(8,128)S(1)} %add.162), channel_id=1, source_target_pairs={{0,64},{16,80},{32,96},{48,112},{64,0},{80,16},{96,32},{112,48},{1... | collective-permute-start | bytes 196616 | tf_op jit(solution)/shard_map/ppermute | solution.py:65
  194.7 2.9 %collective-permute-done.20 = f32[32,512]{1,0:T(8,128)S(1)} collective-permute-done((f32[32,512]{1,0:T(8,128)S(1)}, f32[32,512]{1,0:T(8,128)S(1)}, u32[]{:S(2)}, u32[]{:S(2)}) %collective-permute-start.20) | collective-permute-done | bytes 65568 | tf_op jit(solution)/shard_map/ppermute | solution.py:65
  197.6 1.9 collective-permute-start.21
  199.6 3.6 %collective-permute-done.21 = f32[32,512]{1,0:T(8,128)S(1)} collective-permute-done((f32[32,512]{1,0:T(8,128)S(1)}, f32[32,512]{1,0:T(8,128)S(1)}, u32[]{:S(2)}, u32[]{:S(2)}) %collective-permute-start.21) | collective-permute-done | bytes 65568 | tf_op jit(solution)/shard_map/ppermute | solution.py:88
  203.2 2.3 collective-permute-start.22
  205.5 6.4 %collective-permute-done.22 = f32[64,512]{1,0:T(8,128)S(1)} collective-permute-done((f32[64,512]{1,0:T(8,128)S(1)}, f32[64,512]{1,0:T(8,128)S(1)}, u32[]{:S(2)}, u32[]{:S(2)}) %collective-permute-start.22) | collective-permute-done | bytes 131104 | tf_op jit(solution)/shard_map/ppermute | solution.py:88
  211.9 0.7 fusion.7
  212.6 37.2 %all-gather.5.cloned.1.call-done = bf16[49152,128]{1,0:T(8,128)(2,1)} async-done(((bf16[3072,128]{1,0:T(8,128)(2,1)}), bf16[49152,128]{1,0:T(8,128)(2,1)}) %all-gather.5.cloned.1.call-update) | async-done | bytes 12582928 | tf_op jit(solution)/shard_map/all_gather | solution.py:157
  249.7 15.2 %shard_map.86 = bf16[12,128,128]{2,1,0:T(8,128)(2,1)} custom-call(s32[672]{0:T(1024)S(1)} %get-tuple-element.3.pos_ref, bf16[12,56,128,128]{3,2,1,0:T(8,128)(2,1)} %a_ref.3, bf16[384,128,128]{2,1,0:T(8,128)(2,1)} %bitcast.56), custom_call_target="tpu_custom_call" | custom-call | flops 2818572288 | bytes 34996224 | tf_op jit(solution)/shard_map/pallas_call | solution.py:38
  (44 shorter events, 0.5 us)
Async XLA Ops:
  7.2 16.6 %copy-start = (bf16[512,512]{1,0:T(8,128)(2,1)S(1)}, bf16[512,512]{1,0:T(8,128)(2,1)}, u32[]{:S(2)}) copy-start(bf16[512,512]{1,0:T(8,128)(2,1)} %param.7) | copy-start | bytes 1572868
  7.2 107.7 %all-gather.3.cloned.1.call-start = ((), (), s32[]{:S(2)}) async-start(), calls=%async_computation | async-start | bytes 13369344 | tf_op jit(solution)/shard_map/all_gather | solution.py:117
  8.3 7.7 %collective-permute-start = (bf16[384,128]{1,0:T(8,128)(2,1)S(1)}, bf16[384,128]{1,0:T(8,128)(2,1)S(1)}, u32[]{:S(2)}, u32[]{:S(2)}) collective-permute-start(bf16[384,128]{1,0:T(8,128)(2,1)S(1)} %get-tuple-element.18), channel_id=1, source_target_pairs={{0,16},{16,0},{1,17},{17,1},{2,18},{18,2},{3,19},{19,3},{4,20},{20... | collective-permute-start | bytes 294920 | tf_op jit(solution)/shard_map/ppermute | solution.py:115
  12.0 5.0 %collective-permute-start.1 = (bf16[384,128]{1,0:T(8,128)(2,1)S(1)}, bf16[384,128]{1,0:T(8,128)(2,1)S(1)}, u32[]{:S(2)}, u32[]{:S(2)}) collective-permute-start(bf16[384,128]{1,0:T(8,128)(2,1)S(1)} %get-tuple-element.17), channel_id=1, source_target_pairs={{0,16},{16,0},{1,17},{17,1},{2,18},{18,2},{3,19},{19,3},{4,20},{20... | collective-permute-start | bytes 294920 | tf_op jit(solution)/shard_map/ppermute | solution.py:115
  12.1 6.9 %collective-permute-start.2 = (bf16[384,128]{1,0:T(8,128)(2,1)S(1)}, bf16[384,128]{1,0:T(8,128)(2,1)S(1)}, u32[]{:S(2)}, u32[]{:S(2)}) collective-permute-start(bf16[384,128]{1,0:T(8,128)(2,1)S(1)} %get-tuple-element.16), channel_id=1, source_target_pairs={{0,16},{16,0},{1,17},{17,1},{2,18},{18,2},{3,19},{19,3},{4,20},{20... | collective-permute-start | bytes 294920 | tf_op jit(solution)/shard_map/ppermute | solution.py:115
  15.0 6.3 %collective-permute-start.3 = (bf16[384,128]{1,0:T(8,128)(2,1)S(1)}, bf16[384,128]{1,0:T(8,128)(2,1)S(1)}, u32[]{:S(2)}, u32[]{:S(2)}) collective-permute-start(bf16[384,128]{1,0:T(8,128)(2,1)S(1)} %get-tuple-element.15), channel_id=1, source_target_pairs={{0,16},{16,0},{1,17},{17,1},{2,18},{18,2},{3,19},{19,3},{4,20},{20... | collective-permute-start | bytes 294920 | tf_op jit(solution)/shard_map/ppermute | solution.py:115
  21.3 0.9 copy-start.1
  22.2 227.5 %all-gather.5.cloned.1.call-start = ((), (), s32[]{:S(2)}) async-start(), calls=%async_computation.1 | async-start | bytes 13369344 | tf_op jit(solution)/shard_map/all_gather | solution.py:157
  114.8 22.1 %copy-start.3 = (bf16[384,512]{1,0:T(8,128)(2,1)S(1)}, bf16[384,512]{1,0:T(8,128)(2,1)}, u32[]{:S(2)}) copy-start(bf16[384,512]{1,0:T(8,128)(2,1)} %param.8) | copy-start | bytes 1179652
  129.4 2.7 collective-permute-start.4
  130.3 4.3 %collective-permute-start.5 = (bf16[384,128]{1,0:T(8,128)(2,1)S(1)}, bf16[384,128]{1,0:T(8,128)(2,1)S(1)}, u32[]{:S(2)}, u32[]{:S(2)}) collective-permute-start(bf16[384,128]{1,0:T(8,128)(2,1)S(1)} %get-tuple-element.13), channel_id=1, source_target_pairs={{0,2},{1,3},{2,0},{3,1},{4,6},{5,7},{6,4},{7,5},{8,10},{9,11},{10,... | collective-permute-start | bytes 294920 | tf_op jit(solution)/shard_map/ppermute | solution.py:107
  131.5 5.4 %collective-permute-start.6 = (bf16[384,128]{1,0:T(8,128)(2,1)S(1)}, bf16[384,128]{1,0:T(8,128)(2,1)S(1)}, u32[]{:S(2)}, u32[]{:S(2)}) collective-permute-start(bf16[384,128]{1,0:T(8,128)(2,1)S(1)} %get-tuple-element.12), channel_id=1, source_target_pairs={{0,3},{1,2},{2,1},{3,0},{4,7},{5,6},{6,5},{7,4},{8,11},{9,10},{10,... | collective-permute-start | bytes 294920 | tf_op jit(solution)/shard_map/ppermute | solution.py:107
  138.9 5.5 %collective-permute-start.7 = (bf16[384,128]{1,0:T(8,128)(2,1)S(1)}, bf16[384,128]{1,0:T(8,128)(2,1)S(1)}, u32[]{:S(2)}, u32[]{:S(2)}) collective-permute-start(bf16[384,128]{1,0:T(8,128)(2,1)S(1)} %get-tuple-element.10), channel_id=1, source_target_pairs={{0,1},{1,0},{2,3},{3,2},{4,5},{5,4},{6,7},{7,6},{8,9},{9,8},{10,11... | collective-permute-start | bytes 294920 | tf_op jit(solution)/shard_map/ppermute | solution.py:107
  139.1 13.4 %collective-permute-start.11 = (bf16[384,128]{1,0:T(8,128)(2,1)S(1)}, bf16[384,128]{1,0:T(8,128)(2,1)S(1)}, u32[]{:S(2)}, u32[]{:S(2)}) collective-permute-start(bf16[384,128]{1,0:T(8,128)(2,1)S(1)} %get-tuple-element.10), channel_id=1, source_target_pairs={{0,17},{1,16},{2,19},{3,18},{16,1},{17,0},{18,3},{19,2},{4,21},{5,... | collective-permute-start | bytes 294920 | tf_op jit(solution)/shard_map/ppermute | solution.py:105
  142.0 5.4 %collective-permute-start.8 = (bf16[384,128]{1,0:T(8,128)(2,1)S(1)}, bf16[384,128]{1,0:T(8,128)(2,1)S(1)}, u32[]{:S(2)}, u32[]{:S(2)}) collective-permute-start(bf16[384,128]{1,0:T(8,128)(2,1)S(1)} %get-tuple-element.9), channel_id=1, source_target_pairs={{0,2},{1,3},{2,0},{3,1},{4,6},{5,7},{6,4},{7,5},{8,10},{9,11},{10,... | collective-permute-start | bytes 294920 | tf_op jit(solution)/shard_map/ppermute | solution.py:107
  142.3 10.2 %collective-permute-start.12 = (bf16[384,128]{1,0:T(8,128)(2,1)S(1)}, bf16[384,128]{1,0:T(8,128)(2,1)S(1)}, u32[]{:S(2)}, u32[]{:S(2)}) collective-permute-start(bf16[384,128]{1,0:T(8,128)(2,1)S(1)} %get-tuple-element.9), channel_id=1, source_target_pairs={{0,18},{1,19},{2,16},{3,17},{16,2},{17,3},{18,0},{19,1},{4,22},{5,... | collective-permute-start | bytes 294920 | tf_op jit(solution)/shard_map/ppermute | solution.py:105
  142.9 6.9 %collective-permute-start.9 = (bf16[384,128]{1,0:T(8,128)(2,1)S(1)}, bf16[384,128]{1,0:T(8,128)(2,1)S(1)}, u32[]{:S(2)}, u32[]{:S(2)}) collective-permute-start(bf16[384,128]{1,0:T(8,128)(2,1)S(1)} %get-tuple-element.8), channel_id=1, source_target_pairs={{0,3},{1,2},{2,1},{3,0},{4,7},{5,6},{6,5},{7,4},{8,11},{9,10},{10,... | collective-permute-start | bytes 294920 | tf_op jit(solution)/shard_map/ppermute | solution.py:107
  144.4 8.2 %collective-permute-start.13 = (bf16[384,128]{1,0:T(8,128)(2,1)S(1)}, bf16[384,128]{1,0:T(8,128)(2,1)S(1)}, u32[]{:S(2)}, u32[]{:S(2)}) collective-permute-start(bf16[384,128]{1,0:T(8,128)(2,1)S(1)} %get-tuple-element.8), channel_id=1, source_target_pairs={{0,19},{1,18},{2,17},{3,16},{16,3},{17,2},{18,1},{19,0},{4,23},{5,... | collective-permute-start | bytes 294920 | tf_op jit(solution)/shard_map/ppermute | solution.py:105
  147.5 5.0 %collective-permute-start.10 = (bf16[384,128]{1,0:T(8,128)(2,1)S(1)}, bf16[384,128]{1,0:T(8,128)(2,1)S(1)}, u32[]{:S(2)}, u32[]{:S(2)}) collective-permute-start(bf16[384,128]{1,0:T(8,128)(2,1)S(1)} %get-tuple-element.7), channel_id=1, source_target_pairs={{0,16},{1,17},{2,18},{3,19},{16,0},{17,1},{18,2},{19,3},{4,20},{5,... | collective-permute-start | bytes 294920 | tf_op jit(solution)/shard_map/ppermute | solution.py:105
  152.6 0.9 copy-start.2
  154.9 11.4 %collective-permute-start.14 = (f32[2,128,512]{2,1,0:T(8,128)S(1)}, f32[2,128,512]{2,1,0:T(8,128)S(1)}, u32[]{:S(2)}, u32[]{:S(2)}) collective-permute-start(f32[2,128,512]{2,1,0:T(8,128)S(1)} %slice_select_fusion), channel_id=1, source_target_pairs={{0,2},{1,3},{2,0},{3,1},{4,6},{5,7},{6,4},{7,5},{8,10},{9,11},{10,... | collective-permute-start | bytes 1572872 | tf_op jit(solution)/shard_map/ppermute | solution.py:79
  166.5 4.3 %collective-permute-start.15 = (f32[1,128,512]{2,1,0:T(8,128)S(1)}, f32[1,128,512]{2,1,0:T(8,128)S(1)}, u32[]{:S(2)}, u32[]{:S(2)}) collective-permute-start(f32[1,128,512]{2,1,0:T(8,128)S(1)} %slice_select_fusion.1), channel_id=1, source_target_pairs={{0,1},{1,0},{2,3},{3,2},{4,5},{5,4},{6,7},{7,6},{8,9},{9,8},{10,11... | collective-permute-start | bytes 786440 | tf_op jit(solution)/shard_map/ppermute | solution.py:79
  170.8 9.4 %collective-permute-start.16 = (f32[2,32,512]{2,1,0:T(8,128)S(1)}, f32[2,32,512]{2,1,0:T(8,128)S(1)}, u32[]{:S(2)}, u32[]{:S(2)}) collective-permute-start(f32[2,32,512]{2,1,0:T(8,128)S(1)} %bitcast.61), channel_id=1, source_target_pairs={{0,8},{4,12},{8,0},{12,4},{1,9},{5,13},{9,1},{13,5},{2,10},{6,14},... | collective-permute-start | bytes 393224 | tf_op jit(solution)/shard_map/ppermute | solution.py:79
  180.2 3.6 %collective-permute-start.17 = (f32[1,32,512]{2,1,0:T(8,128)S(1)}, f32[1,32,512]{2,1,0:T(8,128)S(1)}, u32[]{:S(2)}, u32[]{:S(2)}) collective-permute-start(f32[1,32,512]{2,1,0:T(8,128)S(1)} %slice_select_fusion.4), channel_id=1, source_target_pairs={{0,4},{4,0},{8,12},{12,8},{1,5},{5,1},{9,13},{13,9},{2,6},{6,2},{1... | collective-permute-start | bytes 196616 | tf_op jit(solution)/shard_map/ppermute | solution.py:79
  183.9 4.7 %collective-permute-start.18 = (f32[32,512]{1,0:T(8,128)S(1)}, f32[32,512]{1,0:T(8,128)S(1)}, u32[]{:S(2)}, u32[]{:S(2)}) collective-permute-start(f32[32,512]{1,0:T(8,128)S(1)} %add_bitcast_fusion), channel_id=1, source_target_pairs={{0,16},{16,0},{32,48},{48,32},{64,80},{80,64},{96,112},{112,96},{1... | collective-permute-start | bytes 196616 | tf_op jit(solution)/shard_map/ppermute | solution.py:65
  188.6 3.2 %collective-permute-start.19 = (f32[32,512]{1,0:T(8,128)S(1)}, f32[32,512]{1,0:T(8,128)S(1)}, u32[]{:S(2)}, u32[]{:S(2)}) collective-permute-start(f32[32,512]{1,0:T(8,128)S(1)} %add.161), channel_id=1, source_target_pairs={{0,32},{16,48},{32,0},{48,16},{64,96},{80,112},{96,64},{112,80},{1... | collective-permute-start | bytes 196616 | tf_op jit(solution)/shard_map/ppermute | solution.py:65
  191.8 5.9 %collective-permute-start.20 = (f32[32,512]{1,0:T(8,128)S(1)}, f32[32,512]{1,0:T(8,128)S(1)}, u32[]{:S(2)}, u32[]{:S(2)}) collective-permute-start(f32[32,512]{1,0:T(8,128)S(1)} %add.162), channel_id=1, source_target_pairs={{0,64},{16,80},{32,96},{48,112},{64,0},{80,16},{96,32},{112,48},{1... | collective-permute-start | bytes 196616 | tf_op jit(solution)/shard_map/ppermute | solution.py:65
  197.6 5.5 %collective-permute-start.21 = (f32[32,512]{1,0:T(8,128)S(1)}, f32[32,512]{1,0:T(8,128)S(1)}, u32[]{:S(2)}, u32[]{:S(2)}) collective-permute-start(f32[32,512]{1,0:T(8,128)S(1)} %add.163), channel_id=1, source_target_pairs={{0,4},{4,0},{8,12},{12,8},{1,5},{5,1},{9,13},{13,9},{2,6},{6,2},{1... | collective-permute-start | bytes 196616 | tf_op jit(solution)/shard_map/ppermute | solution.py:88
  203.2 8.7 %collective-permute-start.22 = (f32[64,512]{1,0:T(8,128)S(1)}, f32[64,512]{1,0:T(8,128)S(1)}, u32[]{:S(2)}, u32[]{:S(2)}) collective-permute-start(f32[64,512]{1,0:T(8,128)S(1)} %maximum_select_fusion.1), channel_id=1, source_target_pairs={{0,8},{4,12},{8,0},{12,4},{1,9},{5,13},{9,1},{13,5},{2,10},{6,14},... | collective-permute-start | bytes 393224 | tf_op jit(solution)/shard_map/ppermute | solution.py:88
Sparse Core Ops, SparseCore 0:
  22.4 92.4 all-gather.2
  153.6 96.0 all-gather.4

commit v14 on v13

--- a/solution.py
+++ b/solution.py
@@ -111,9 +111,8 @@
 
 
 def hier_gather(x):
-    pieces = jnp.split(x, 4, axis=0)
-    partner = [lax.ppermute(piece, "xh", xor_pairs(2, 1)) for piece in pieces]
-    pair = jnp.concatenate([x] + partner, axis=0)
+    partner = lax.ppermute(x, "xh", xor_pairs(2, 1))
+    pair = jnp.concatenate([x, partner], axis=0)
     return lax.all_gather(pair, ("y", "z"), axis=0, tiled=True)
 
 

time: 272 us -> 272 us (level)
  waiting for transfers between devices: 179 us -> 184 us
  starting transfers between devices: 38 us -> 34.9 us
  local copies, waits for them, and re-layouts: 5.66 us -> 2.56 us
    ppermute x4 -> x1, waiting for transfers between devices: 5.13 us -> 8.64 us  [hier_gather(): partner = lax.ppermute(x, 'xh', xor_pairs(2, 1))]
    ppermute x4 -> x1, starting transfers between devices: 6.7 us -> 3.64 us  [hier_gather(): partner = lax.ppermute(x, 'xh', xor_pairs(2, 1))]
  transfers between devices with their start and end apart: 25 -> 22, of which waited for: 19 -> 17; matrix products, arithmetic and copies ran while one was open for 2% -> 2% of each run, Pallas kernels for 0% -> 0%
where the time goes in v14:
time: 272 us
  waiting for transfers between devices  184 us (68%)
  starting transfers between devices  34.9 us (13%)
  Pallas kernels  29.7 us (11%)
  between operations  14.4 us (5%)
  other arithmetic  4.38 us (2%)
    all_gather x1, waiting for transfers between devices, hier_gather(): return lax.all_gather(pair, ('y', 'z'), axis=0, tiled=True)  91.3 us
    all_gather x1, waiting for transfers between devices, local(): lax.all_gather(pair.reshape(-1, feat_dev), ('y', 'z'), axis=0, tiled=True)  37.1 us
    pallas_call x2, Pallas kernels, block_product(): pl.pallas_call(_product_kernel, grid_spec=pltpu.PrefetchScalarGridSpec(nu...  29.7 us
    ppermute x4, waiting for transfers between devices, halving_scatter(): parts = keep + lax.ppermute(send, axis, xor_pairs(size, bit))  20 us
    ppermute x2, waiting for transfers between devices, doubling_gather(): got = lax.ppermute(x, axis, xor_pairs(size, bit))  10 us
    ppermute x1, waiting for transfers between devices, hier_gather(): partner = lax.ppermute(x, 'xh', xor_pairs(2, 1))  8.64 us
    ppermute x4, starting transfers between devices, halving_scatter(): parts = keep + lax.ppermute(send, axis, xor_pairs(size, bit))  8.59 us
    ppermute x6, waiting for transfers between devices, exchange(): send = lax.ppermute(send, axis, xor_pairs(size, s))  7.02 us
  transfers between devices with their start and end apart: 22, of which 17 were waited for; matrix products, arithmetic and copies ran while one was open for 2% of the time, Pallas kernels for 0%

profile of v14, /device:TPU:1, one launch (start us, length us, event | category | flops | bytes accessed | tf_op | source)
XLA Modules:
  0.0 271.9 jit_solution(5185818815415445551)
XLA Ops:
  7.2 0.0 copy-start
  7.2 0.0 all-gather.3.cloned.1.call-start
  7.2 3.6 %collective-permute-start = (bf16[1536,128]{1,0:T(8,128)(2,1)}, bf16[1536,128]{1,0:T(8,128)(2,1)S(1)}, u32[]{:S(2)}, u32[]{:S(2)}) collective-permute-start(bf16[1536,128]{1,0:T(8,128)(2,1)} %param.6), channel_id=1, source_target_pairs={{0,16},{16,0},{1,17},{17,1},{2,18},{18,2},{3,19},{19,3},{4,20},{20... | collective-permute-start | bytes 1179656 | tf_op jit(solution)/shard_map/ppermute | solution.py:114
  10.9 8.6 %collective-permute-done = bf16[1536,128]{1,0:T(8,128)(2,1)S(1)} collective-permute-done((bf16[1536,128]{1,0:T(8,128)(2,1)}, bf16[1536,128]{1,0:T(8,128)(2,1)S(1)}, u32[]{:S(2)}, u32[]{:S(2)}) %collective-permute-start) | collective-permute-done | bytes 393248 | tf_op jit(solution)/shard_map/ppermute | solution.py:114
  19.5 2.0 pad_maximum_fusion
  21.5 0.0 all-gather.3.cloned.1.call-update
  21.5 0.0 all-gather.5.cloned.1.call-start
  21.6 1.1 select_reduce_fusion
  22.7 0.1 rem.91
  22.8 0.1 div.42
  22.9 0.1 ne.125
  23.1 0.6 gather_fusion
  23.7 91.3 %all-gather.3.cloned.1.call-done = bf16[49152,128]{1,0:T(8,128)(2,1)} async-done(((bf16[3072,128]{1,0:T(8,128)(2,1)}), bf16[49152,128]{1,0:T(8,128)(2,1)}) %all-gather.3.cloned.1.call-update) | async-done | bytes 12582928 | tf_op jit(solution)/shard_map/all_gather | solution.py:116
  115.0 14.5 %shard_map.85 = bf16[12,128,128]{2,1,0:T(8,128)(2,1)S(1)} custom-call(s32[672]{0:T(1024)S(1)} %fusion.27.pos_ref, bf16[12,56,128,128]{3,2,1,0:T(8,128)(2,1)} %a_ref.3, bf16[384,128,128]{2,1,0:T(8,128)(2,1)} %bitcast.57), custom_call_target="tpu_custom_call" | custom-call | flops 2818572288 | bytes 34996224 | tf_op jit(solution)/shard_map/pallas_call | solution.py:38
  129.5 0.9 collective-permute-start.1
  130.5 1.2 collective-permute-start.2
  131.6 0.5 collective-permute-start.3
  132.2 0.0 collective-permute-done.1
  132.2 2.5 collective-permute-done.2
  134.7 2.4 collective-permute-done.3
  137.1 1.5 multiply_convert_fusion
  138.5 0.4 convolution_convert_fusion
  139.0 0.2 collective-permute-start.4
  139.2 3.0 %collective-permute-start.8 = (bf16[384,128]{1,0:T(8,128)(2,1)S(1)}, bf16[384,128]{1,0:T(8,128)(2,1)S(1)}, u32[]{:S(2)}, u32[]{:S(2)}) collective-permute-start(bf16[384,128]{1,0:T(8,128)(2,1)S(1)} %get-tuple-element.10), channel_id=1, source_target_pairs={{0,17},{1,16},{2,19},{3,18},{16,1},{17,0},{18,3},{19,2},{4,21},{5,... | collective-permute-start | bytes 294920 | tf_op jit(solution)/shard_map/ppermute | solution.py:105
  142.2 0.3 collective-permute-start.5
  142.5 0.6 collective-permute-start.9
  143.1 1.4 collective-permute-start.6
  144.5 0.0 collective-permute-done.4
  144.5 1.6 collective-permute-start.10
  146.1 1.5 collective-permute-done.5
  147.6 1.8 collective-permute-start.7
  149.4 0.6 collective-permute-done.6
  150.0 2.6 collective-permute-done.7
  152.6 0.0 collective-permute-done.8
  152.7 0.0 collective-permute-done.10
  152.7 0.9 copy-done.1
  153.6 0.0 all-gather.5.cloned.1.call-update
  153.7 0.1 pad_maximum_fusion.1
  153.7 0.6 gather_fusion.1
  154.3 0.6 fusion.2
  154.9 0.1 slice_select_fusion
  155.0 1.3 collective-permute-start.11
  156.3 10.1 %collective-permute-done.11 = f32[2,128,512]{2,1,0:T(8,128)S(1)} collective-permute-done((f32[2,128,512]{2,1,0:T(8,128)S(1)}, f32[2,128,512]{2,1,0:T(8,128)S(1)}, u32[]{:S(2)}, u32[]{:S(2)}) %collective-permute-start.11) | collective-permute-done | bytes 524320 | tf_op jit(solution)/shard_map/ppermute | solution.py:79
  166.4 0.1 select_add_fusion
  166.6 3.1 %collective-permute-start.12 = (f32[1,128,512]{2,1,0:T(8,128)S(1)}, f32[1,128,512]{2,1,0:T(8,128)S(1)}, u32[]{:S(2)}, u32[]{:S(2)}) collective-permute-start(f32[1,128,512]{2,1,0:T(8,128)S(1)} %slice_select_fusion.1), channel_id=1, source_target_pairs={{0,1},{1,0},{2,3},{3,2},{4,5},{5,4},{6,7},{7,6},{8,9},{9,8},{10,11... | collective-permute-start | bytes 786440 | tf_op jit(solution)/shard_map/ppermute | solution.py:79
  169.7 1.2 collective-permute-done.12
  170.9 0.1 select_add_fusion.1
  171.0 2.8 %collective-permute-start.13 = (f32[2,32,512]{2,1,0:T(8,128)S(1)}, f32[2,32,512]{2,1,0:T(8,128)S(1)}, u32[]{:S(2)}, u32[]{:S(2)}) collective-permute-start(f32[2,32,512]{2,1,0:T(8,128)S(1)} %bitcast.61), channel_id=1, source_target_pairs={{0,8},{4,12},{8,0},{12,4},{1,9},{5,13},{9,1},{13,5},{2,10},{6,14},... | collective-permute-start | bytes 393224 | tf_op jit(solution)/shard_map/ppermute | solution.py:79
  173.8 6.5 %collective-permute-done.13 = f32[2,32,512]{2,1,0:T(8,128)S(1)} collective-permute-done((f32[2,32,512]{2,1,0:T(8,128)S(1)}, f32[2,32,512]{2,1,0:T(8,128)S(1)}, u32[]{:S(2)}, u32[]{:S(2)}) %collective-permute-start.13) | collective-permute-done | bytes 131104 | tf_op jit(solution)/shard_map/ppermute | solution.py:79
  180.4 1.4 collective-permute-start.14
  181.8 2.2 collective-permute-done.14
  184.0 2.6 collective-permute-start.15
  186.6 2.0 collective-permute-done.15
  188.7 1.3 collective-permute-start.16
  190.0 1.9 collective-permute-done.16
  191.9 2.9 %collective-permute-start.17 = (f32[32,512]{1,0:T(8,128)S(1)}, f32[32,512]{1,0:T(8,128)S(1)}, u32[]{:S(2)}, u32[]{:S(2)}) collective-permute-start(f32[32,512]{1,0:T(8,128)S(1)} %add.162), channel_id=1, source_target_pairs={{0,64},{16,80},{32,96},{48,112},{64,0},{80,16},{96,32},{112,48},{1... | collective-permute-start | bytes 196616 | tf_op jit(solution)/shard_map/ppermute | solution.py:65
  194.8 2.9 %collective-permute-done.17 = f32[32,512]{1,0:T(8,128)S(1)} collective-permute-done((f32[32,512]{1,0:T(8,128)S(1)}, f32[32,512]{1,0:T(8,128)S(1)}, u32[]{:S(2)}, u32[]{:S(2)}) %collective-permute-start.17) | collective-permute-done | bytes 65568 | tf_op jit(solution)/shard_map/ppermute | solution.py:65
  197.8 2.0 collective-permute-start.18
  199.7 3.6 %collective-permute-done.18 = f32[32,512]{1,0:T(8,128)S(1)} collective-permute-done((f32[32,512]{1,0:T(8,128)S(1)}, f32[32,512]{1,0:T(8,128)S(1)}, u32[]{:S(2)}, u32[]{:S(2)}) %collective-permute-start.18) | collective-permute-done | bytes 65568 | tf_op jit(solution)/shard_map/ppermute | solution.py:88
  203.3 2.2 collective-permute-start.19
  205.6 6.5 %collective-permute-done.19 = f32[64,512]{1,0:T(8,128)S(1)} collective-permute-done((f32[64,512]{1,0:T(8,128)S(1)}, f32[64,512]{1,0:T(8,128)S(1)}, u32[]{:S(2)}, u32[]{:S(2)}) %collective-permute-start.19) | collective-permute-done | bytes 131104 | tf_op jit(solution)/shard_map/ppermute | solution.py:88
  212.0 0.7 fusion.7
  212.7 37.1 %all-gather.5.cloned.1.call-done = bf16[49152,128]{1,0:T(8,128)(2,1)} async-done(((bf16[3072,128]{1,0:T(8,128)(2,1)}), bf16[49152,128]{1,0:T(8,128)(2,1)}) %all-gather.5.cloned.1.call-update) | async-done | bytes 12582928 | tf_op jit(solution)/shard_map/all_gather | solution.py:156
  249.9 15.2 %shard_map.86 = bf16[12,128,128]{2,1,0:T(8,128)(2,1)} custom-call(s32[672]{0:T(1024)S(1)} %get-tuple-element.3.pos_ref, bf16[12,56,128,128]{3,2,1,0:T(8,128)(2,1)} %a_ref.3, bf16[384,128,128]{2,1,0:T(8,128)(2,1)} %bitcast.56), custom_call_target="tpu_custom_call" | custom-call | flops 2818572288 | bytes 34996224 | tf_op jit(solution)/shard_map/pallas_call | solution.py:38
  (31 shorter events, 0.4 us)
Async XLA Ops:
  7.2 15.9 %copy-start = (bf16[512,512]{1,0:T(8,128)(2,1)S(1)}, bf16[512,512]{1,0:T(8,128)(2,1)}, u32[]{:S(2)}) copy-start(bf16[512,512]{1,0:T(8,128)(2,1)} %param.7) | copy-start | bytes 1572868
  7.2 107.8 %all-gather.3.cloned.1.call-start = ((), (), s32[]{:S(2)}) async-start(), calls=%async_computation | async-start | bytes 13369344 | tf_op jit(solution)/shard_map/all_gather | solution.py:116
  7.2 12.3 %collective-permute-start = (bf16[1536,128]{1,0:T(8,128)(2,1)}, bf16[1536,128]{1,0:T(8,128)(2,1)S(1)}, u32[]{:S(2)}, u32[]{:S(2)}) collective-permute-start(bf16[1536,128]{1,0:T(8,128)(2,1)} %param.6), channel_id=1, source_target_pairs={{0,16},{16,0},{1,17},{17,1},{2,18},{18,2},{3,19},{19,3},{4,20},{20... | collective-permute-start | bytes 1179656 | tf_op jit(solution)/shard_map/ppermute | solution.py:114
  21.5 228.4 %all-gather.5.cloned.1.call-start = ((), (), s32[]{:S(2)}) async-start(), calls=%async_computation.1 | async-start | bytes 13369344 | tf_op jit(solution)/shard_map/all_gather | solution.py:156
  115.0 22.1 %copy-start.2 = (bf16[384,512]{1,0:T(8,128)(2,1)S(1)}, bf16[384,512]{1,0:T(8,128)(2,1)}, u32[]{:S(2)}) copy-start(bf16[384,512]{1,0:T(8,128)(2,1)} %param.8) | copy-start | bytes 1179652
  129.5 2.7 collective-permute-start.1
  130.5 4.3 %collective-permute-start.2 = (bf16[384,128]{1,0:T(8,128)(2,1)S(1)}, bf16[384,128]{1,0:T(8,128)(2,1)S(1)}, u32[]{:S(2)}, u32[]{:S(2)}) collective-permute-start(bf16[384,128]{1,0:T(8,128)(2,1)S(1)} %get-tuple-element.13), channel_id=1, source_target_pairs={{0,2},{1,3},{2,0},{3,1},{4,6},{5,7},{6,4},{7,5},{8,10},{9,11},{10,... | collective-permute-start | bytes 294920 | tf_op jit(solution)/shard_map/ppermute | solution.py:107
  131.6 5.4 %collective-permute-start.3 = (bf16[384,128]{1,0:T(8,128)(2,1)S(1)}, bf16[384,128]{1,0:T(8,128)(2,1)S(1)}, u32[]{:S(2)}, u32[]{:S(2)}) collective-permute-start(bf16[384,128]{1,0:T(8,128)(2,1)S(1)} %get-tuple-element.12), channel_id=1, source_target_pairs={{0,3},{1,2},{2,1},{3,0},{4,7},{5,6},{6,5},{7,4},{8,11},{9,10},{10,... | collective-permute-start | bytes 294920 | tf_op jit(solution)/shard_map/ppermute | solution.py:107
  139.0 5.5 %collective-permute-start.4 = (bf16[384,128]{1,0:T(8,128)(2,1)S(1)}, bf16[384,128]{1,0:T(8,128)(2,1)S(1)}, u32[]{:S(2)}, u32[]{:S(2)}) collective-permute-start(bf16[384,128]{1,0:T(8,128)(2,1)S(1)} %get-tuple-element.10), channel_id=1, source_target_pairs={{0,1},{1,0},{2,3},{3,2},{4,5},{5,4},{6,7},{7,6},{8,9},{9,8},{10,11... | collective-permute-start | bytes 294920 | tf_op jit(solution)/shard_map/ppermute | solution.py:107
  139.2 13.4 %collective-permute-start.8 = (bf16[384,128]{1,0:T(8,128)(2,1)S(1)}, bf16[384,128]{1,0:T(8,128)(2,1)S(1)}, u32[]{:S(2)}, u32[]{:S(2)}) collective-permute-start(bf16[384,128]{1,0:T(8,128)(2,1)S(1)} %get-tuple-element.10), channel_id=1, source_target_pairs={{0,17},{1,16},{2,19},{3,18},{16,1},{17,0},{18,3},{19,2},{4,21},{5,... | collective-permute-start | bytes 294920 | tf_op jit(solution)/shard_map/ppermute | solution.py:105
  142.2 5.4 %collective-permute-start.5 = (bf16[384,128]{1,0:T(8,128)(2,1)S(1)}, bf16[384,128]{1,0:T(8,128)(2,1)S(1)}, u32[]{:S(2)}, u32[]{:S(2)}) collective-permute-start(bf16[384,128]{1,0:T(8,128)(2,1)S(1)} %get-tuple-element.9), channel_id=1, source_target_pairs={{0,2},{1,3},{2,0},{3,1},{4,6},{5,7},{6,4},{7,5},{8,10},{9,11},{10,... | collective-permute-start | bytes 294920 | tf_op jit(solution)/shard_map/ppermute | solution.py:107
  142.5 10.2 %collective-permute-start.9 = (bf16[384,128]{1,0:T(8,128)(2,1)S(1)}, bf16[384,128]{1,0:T(8,128)(2,1)S(1)}, u32[]{:S(2)}, u32[]{:S(2)}) collective-permute-start(bf16[384,128]{1,0:T(8,128)(2,1)S(1)} %get-tuple-element.9), channel_id=1, source_target_pairs={{0,18},{1,19},{2,16},{3,17},{16,2},{17,3},{18,0},{19,1},{4,22},{5,... | collective-permute-start | bytes 294920 | tf_op jit(solution)/shard_map/ppermute | solution.py:105
  143.1 7.0 %collective-permute-start.6 = (bf16[384,128]{1,0:T(8,128)(2,1)S(1)}, bf16[384,128]{1,0:T(8,128)(2,1)S(1)}, u32[]{:S(2)}, u32[]{:S(2)}) collective-permute-start(bf16[384,128]{1,0:T(8,128)(2,1)S(1)} %get-tuple-element.8), channel_id=1, source_target_pairs={{0,3},{1,2},{2,1},{3,0},{4,7},{5,6},{6,5},{7,4},{8,11},{9,10},{10,... | collective-permute-start | bytes 294920 | tf_op jit(solution)/shard_map/ppermute | solution.py:107
  144.5 8.2 %collective-permute-start.10 = (bf16[384,128]{1,0:T(8,128)(2,1)S(1)}, bf16[384,128]{1,0:T(8,128)(2,1)S(1)}, u32[]{:S(2)}, u32[]{:S(2)}) collective-permute-start(bf16[384,128]{1,0:T(8,128)(2,1)S(1)} %get-tuple-element.8), channel_id=1, source_target_pairs={{0,19},{1,18},{2,17},{3,16},{16,3},{17,2},{18,1},{19,0},{4,23},{5,... | collective-permute-start | bytes 294920 | tf_op jit(solution)/shard_map/ppermute | solution.py:105
  147.6 5.0 %collective-permute-start.7 = (bf16[384,128]{1,0:T(8,128)(2,1)S(1)}, bf16[384,128]{1,0:T(8,128)(2,1)S(1)}, u32[]{:S(2)}, u32[]{:S(2)}) collective-permute-start(bf16[384,128]{1,0:T(8,128)(2,1)S(1)} %get-tuple-element.7), channel_id=1, source_target_pairs={{0,16},{1,17},{2,18},{3,19},{16,0},{17,1},{18,2},{19,3},{4,20},{5,... | collective-permute-start | bytes 294920 | tf_op jit(solution)/shard_map/ppermute | solution.py:105
  152.7 0.9 copy-start.1
  155.0 11.4 %collective-permute-start.11 = (f32[2,128,512]{2,1,0:T(8,128)S(1)}, f32[2,128,512]{2,1,0:T(8,128)S(1)}, u32[]{:S(2)}, u32[]{:S(2)}) collective-permute-start(f32[2,128,512]{2,1,0:T(8,128)S(1)} %slice_select_fusion), channel_id=1, source_target_pairs={{0,2},{1,3},{2,0},{3,1},{4,6},{5,7},{6,4},{7,5},{8,10},{9,11},{10,... | collective-permute-start | bytes 1572872 | tf_op jit(solution)/shard_map/ppermute | solution.py:79
  166.6 4.3 %collective-permute-start.12 = (f32[1,128,512]{2,1,0:T(8,128)S(1)}, f32[1,128,512]{2,1,0:T(8,128)S(1)}, u32[]{:S(2)}, u32[]{:S(2)}) collective-permute-start(f32[1,128,512]{2,1,0:T(8,128)S(1)} %slice_select_fusion.1), channel_id=1, source_target_pairs={{0,1},{1,0},{2,3},{3,2},{4,5},{5,4},{6,7},{7,6},{8,9},{9,8},{10,11... | collective-permute-start | bytes 786440 | tf_op jit(solution)/shard_map/ppermute | solution.py:79
  171.0 9.4 %collective-permute-start.13 = (f32[2,32,512]{2,1,0:T(8,128)S(1)}, f32[2,32,512]{2,1,0:T(8,128)S(1)}, u32[]{:S(2)}, u32[]{:S(2)}) collective-permute-start(f32[2,32,512]{2,1,0:T(8,128)S(1)} %bitcast.61), channel_id=1, source_target_pairs={{0,8},{4,12},{8,0},{12,4},{1,9},{5,13},{9,1},{13,5},{2,10},{6,14},... | collective-permute-start | bytes 393224 | tf_op jit(solution)/shard_map/ppermute | solution.py:79
  180.4 3.6 %collective-permute-start.14 = (f32[1,32,512]{2,1,0:T(8,128)S(1)}, f32[1,32,512]{2,1,0:T(8,128)S(1)}, u32[]{:S(2)}, u32[]{:S(2)}) collective-permute-start(f32[1,32,512]{2,1,0:T(8,128)S(1)} %slice_select_fusion.4), channel_id=1, source_target_pairs={{0,4},{4,0},{8,12},{12,8},{1,5},{5,1},{9,13},{13,9},{2,6},{6,2},{1... | collective-permute-start | bytes 196616 | tf_op jit(solution)/shard_map/ppermute | solution.py:79
  184.0 4.7 %collective-permute-start.15 = (f32[32,512]{1,0:T(8,128)S(1)}, f32[32,512]{1,0:T(8,128)S(1)}, u32[]{:S(2)}, u32[]{:S(2)}) collective-permute-start(f32[32,512]{1,0:T(8,128)S(1)} %add_bitcast_fusion), channel_id=1, source_target_pairs={{0,16},{16,0},{32,48},{48,32},{64,80},{80,64},{96,112},{112,96},{1... | collective-permute-start | bytes 196616 | tf_op jit(solution)/shard_map/ppermute | solution.py:65
  188.7 3.2 %collective-permute-start.16 = (f32[32,512]{1,0:T(8,128)S(1)}, f32[32,512]{1,0:T(8,128)S(1)}, u32[]{:S(2)}, u32[]{:S(2)}) collective-permute-start(f32[32,512]{1,0:T(8,128)S(1)} %add.161), channel_id=1, source_target_pairs={{0,32},{16,48},{32,0},{48,16},{64,96},{80,112},{96,64},{112,80},{1... | collective-permute-start | bytes 196616 | tf_op jit(solution)/shard_map/ppermute | solution.py:65
  191.9 5.9 %collective-permute-start.17 = (f32[32,512]{1,0:T(8,128)S(1)}, f32[32,512]{1,0:T(8,128)S(1)}, u32[]{:S(2)}, u32[]{:S(2)}) collective-permute-start(f32[32,512]{1,0:T(8,128)S(1)} %add.162), channel_id=1, source_target_pairs={{0,64},{16,80},{32,96},{48,112},{64,0},{80,16},{96,32},{112,48},{1... | collective-permute-start | bytes 196616 | tf_op jit(solution)/shard_map/ppermute | solution.py:65
  197.8 5.6 %collective-permute-start.18 = (f32[32,512]{1,0:T(8,128)S(1)}, f32[32,512]{1,0:T(8,128)S(1)}, u32[]{:S(2)}, u32[]{:S(2)}) collective-permute-start(f32[32,512]{1,0:T(8,128)S(1)} %add.163), channel_id=1, source_target_pairs={{0,4},{4,0},{8,12},{12,8},{1,5},{5,1},{9,13},{13,9},{2,6},{6,2},{1... | collective-permute-start | bytes 196616 | tf_op jit(solution)/shard_map/ppermute | solution.py:88
  203.3 8.7 %collective-permute-start.19 = (f32[64,512]{1,0:T(8,128)S(1)}, f32[64,512]{1,0:T(8,128)S(1)}, u32[]{:S(2)}, u32[]{:S(2)}) collective-permute-start(f32[64,512]{1,0:T(8,128)S(1)} %maximum_select_fusion.1), channel_id=1, source_target_pairs={{0,8},{4,12},{8,0},{12,4},{1,9},{5,13},{9,1},{13,5},{2,10},{6,14},... | collective-permute-start | bytes 393224 | tf_op jit(solution)/shard_map/ppermute | solution.py:88
Sparse Core Ops, SparseCore 0:
  21.6 93.3 all-gather.2
  153.8 96.0 all-gather.4

commit v15 on v14

--- a/solution.py
+++ b/solution.py
@@ -28,7 +28,7 @@
 def block_product(adjacency_tiles, positions, gathered):
     rows, tiles, bs, _ = adjacency_tiles.shape
     width = gathered.shape[1]
-    group = 4 if rows % 4 == 0 else 1
+    group = 6 if rows % 6 == 0 else 1
     blocks = gathered.reshape(-1, bs, width)
     cost = pl.CostEstimate(
         flops=2 * rows * tiles * bs * bs * width,

time: 272 us -> 272 us (level)
  no operation moved by 1% of the time
where the time goes in v15:
time: 272 us
  waiting for transfers between devices  183 us (67%)
  starting transfers between devices  35.1 us (13%)
  Pallas kernels  29.6 us (11%)
  between operations  14.4 us (5%)
  other arithmetic  4.38 us (2%)
    all_gather x1, waiting for transfers between devices, hier_gather(): return lax.all_gather(pair, ('y', 'z'), axis=0, tiled=True)  91.3 us
    all_gather x1, waiting for transfers between devices, local(): lax.all_gather(pair.reshape(-1, feat_dev), ('y', 'z'), axis=0, tiled=True)  36.9 us
    pallas_call x2, Pallas kernels, block_product(): pl.pallas_call(_product_kernel, grid_spec=pltpu.PrefetchScalarGridSpec(nu...  29.6 us
    ppermute x4, waiting for transfers between devices, halving_scatter(): parts = keep + lax.ppermute(send, axis, xor_pairs(size, bit))  20 us
    ppermute x2, waiting for transfers between devices, doubling_gather(): got = lax.ppermute(x, axis, xor_pairs(size, bit))  10.1 us
    ppermute x1, waiting for transfers between devices, hier_gather(): partner = lax.ppermute(x, 'xh', xor_pairs(2, 1))  8.64 us
    ppermute x4, starting transfers between devices, halving_scatter(): parts = keep + lax.ppermute(send, axis, xor_pairs(size, bit))  8.62 us
    ppermute x6, waiting for transfers between devices, exchange(): send = lax.ppermute(send, axis, xor_pairs(size, s))  7.01 us
  transfers between devices with their start and end apart: 22, of which 17 were waited for; matrix products, arithmetic and copies ran while one was open for 2% of the time, Pallas kernels for 0%

profile of v15, /device:TPU:1, one launch (start us, length us, event | category | flops | bytes accessed | tf_op | source)
XLA Modules:
  0.0 271.8 jit_solution(5327744361194389835)
XLA Ops:
  7.2 0.0 copy-start
  7.2 0.0 all-gather.3.cloned.1.call-start
  7.2 3.6 %collective-permute-start = (bf16[1536,128]{1,0:T(8,128)(2,1)}, bf16[1536,128]{1,0:T(8,128)(2,1)S(1)}, u32[]{:S(2)}, u32[]{:S(2)}) collective-permute-start(bf16[1536,128]{1,0:T(8,128)(2,1)} %param.6), channel_id=1, source_target_pairs={{0,16},{16,0},{1,17},{17,1},{2,18},{18,2},{3,19},{19,3},{4,20},{20... | collective-permute-start | bytes 1179656 | tf_op jit(solution)/shard_map/ppermute | solution.py:114
  10.9 8.6 %collective-permute-done = bf16[1536,128]{1,0:T(8,128)(2,1)S(1)} collective-permute-done((bf16[1536,128]{1,0:T(8,128)(2,1)}, bf16[1536,128]{1,0:T(8,128)(2,1)S(1)}, u32[]{:S(2)}, u32[]{:S(2)}) %collective-permute-start) | collective-permute-done | bytes 393248 | tf_op jit(solution)/shard_map/ppermute | solution.py:114
  19.5 2.0 pad_maximum_fusion
  21.5 0.0 all-gather.3.cloned.1.call-update
  21.5 0.0 all-gather.5.cloned.1.call-start
  21.6 1.1 select_reduce_fusion
  22.7 0.1 rem.91
  22.8 0.1 div.42
  22.9 0.1 ne.125
  23.1 0.6 gather_fusion
  23.7 91.3 %all-gather.3.cloned.1.call-done = bf16[49152,128]{1,0:T(8,128)(2,1)} async-done(((bf16[3072,128]{1,0:T(8,128)(2,1)}), bf16[49152,128]{1,0:T(8,128)(2,1)}) %all-gather.3.cloned.1.call-update) | async-done | bytes 12582928 | tf_op jit(solution)/shard_map/all_gather | solution.py:116
  115.0 14.5 %shard_map.85 = bf16[12,128,128]{2,1,0:T(8,128)(2,1)S(1)} custom-call(s32[672]{0:T(1024)S(1)} %fusion.27.pos_ref, bf16[12,56,128,128]{3,2,1,0:T(8,128)(2,1)} %a_ref.3, bf16[384,128,128]{2,1,0:T(8,128)(2,1)} %bitcast.57), custom_call_target="tpu_custom_call" | custom-call | flops 2818572288 | bytes 34996224 | tf_op jit(solution)/shard_map/pallas_call | solution.py:38
  129.5 0.9 collective-permute-start.1
  130.4 1.2 collective-permute-start.2
  131.6 0.5 collective-permute-start.3
  132.2 0.0 collective-permute-done.1
  132.2 2.5 collective-permute-done.2
  134.7 2.4 collective-permute-done.3
  137.1 1.5 multiply_convert_fusion
  138.5 0.4 convolution_convert_fusion
  139.0 0.2 collective-permute-start.4
  139.2 3.0 %collective-permute-start.8 = (bf16[384,128]{1,0:T(8,128)(2,1)S(1)}, bf16[384,128]{1,0:T(8,128)(2,1)S(1)}, u32[]{:S(2)}, u32[]{:S(2)}) collective-permute-start(bf16[384,128]{1,0:T(8,128)(2,1)S(1)} %get-tuple-element.10), channel_id=1, source_target_pairs={{0,17},{1,16},{2,19},{3,18},{16,1},{17,0},{18,3},{19,2},{4,21},{5,... | collective-permute-start | bytes 294920 | tf_op jit(solution)/shard_map/ppermute | solution.py:105
  142.1 0.3 collective-permute-start.5
  142.4 0.6 collective-permute-start.9
  143.0 1.4 collective-permute-start.6
  144.5 0.0 collective-permute-done.4
  144.5 1.6 collective-permute-start.10
  146.1 1.5 collective-permute-done.5
  147.6 1.8 collective-permute-start.7
  149.4 0.6 collective-permute-done.6
  150.0 2.6 collective-permute-done.7
  152.6 0.0 collective-permute-done.8
  152.6 0.0 collective-permute-done.10
  152.7 0.9 copy-done.1
  153.6 0.0 all-gather.5.cloned.1.call-update
  153.6 0.1 pad_maximum_fusion.1
  153.7 0.6 gather_fusion.1
  154.3 0.6 fusion.2
  154.9 0.1 slice_select_fusion
  155.0 1.2 collective-permute-start.11
  156.2 10.1 %collective-permute-done.11 = f32[2,128,512]{2,1,0:T(8,128)S(1)} collective-permute-done((f32[2,128,512]{2,1,0:T(8,128)S(1)}, f32[2,128,512]{2,1,0:T(8,128)S(1)}, u32[]{:S(2)}, u32[]{:S(2)}) %collective-permute-start.11) | collective-permute-done | bytes 524320 | tf_op jit(solution)/shard_map/ppermute | solution.py:79
  166.4 0.1 select_add_fusion
  166.6 3.1 %collective-permute-start.12 = (f32[1,128,512]{2,1,0:T(8,128)S(1)}, f32[1,128,512]{2,1,0:T(8,128)S(1)}, u32[]{:S(2)}, u32[]{:S(2)}) collective-permute-start(f32[1,128,512]{2,1,0:T(8,128)S(1)} %slice_select_fusion.1), channel_id=1, source_target_pairs={{0,1},{1,0},{2,3},{3,2},{4,5},{5,4},{6,7},{7,6},{8,9},{9,8},{10,11... | collective-permute-start | bytes 786440 | tf_op jit(solution)/shard_map/ppermute | solution.py:79
  169.7 1.2 collective-permute-done.12
  170.8 0.1 select_add_fusion.1
  170.9 2.8 %collective-permute-start.13 = (f32[2,32,512]{2,1,0:T(8,128)S(1)}, f32[2,32,512]{2,1,0:T(8,128)S(1)}, u32[]{:S(2)}, u32[]{:S(2)}) collective-permute-start(f32[2,32,512]{2,1,0:T(8,128)S(1)} %bitcast.61), channel_id=1, source_target_pairs={{0,8},{4,12},{8,0},{12,4},{1,9},{5,13},{9,1},{13,5},{2,10},{6,14},... | collective-permute-start | bytes 393224 | tf_op jit(solution)/shard_map/ppermute | solution.py:79
  173.7 6.6 %collective-permute-done.13 = f32[2,32,512]{2,1,0:T(8,128)S(1)} collective-permute-done((f32[2,32,512]{2,1,0:T(8,128)S(1)}, f32[2,32,512]{2,1,0:T(8,128)S(1)}, u32[]{:S(2)}, u32[]{:S(2)}) %collective-permute-start.13) | collective-permute-done | bytes 131104 | tf_op jit(solution)/shard_map/ppermute | solution.py:79
  180.3 1.4 collective-permute-start.14
  181.8 2.2 collective-permute-done.14
  184.0 2.6 collective-permute-start.15
  186.6 2.0 collective-permute-done.15
  188.7 1.3 collective-permute-start.16
  190.0 1.9 collective-permute-done.16
  191.9 2.9 %collective-permute-start.17 = (f32[32,512]{1,0:T(8,128)S(1)}, f32[32,512]{1,0:T(8,128)S(1)}, u32[]{:S(2)}, u32[]{:S(2)}) collective-permute-start(f32[32,512]{1,0:T(8,128)S(1)} %add.162), channel_id=1, source_target_pairs={{0,64},{16,80},{32,96},{48,112},{64,0},{80,16},{96,32},{112,48},{1... | collective-permute-start | bytes 196616 | tf_op jit(solution)/shard_map/ppermute | solution.py:65
  194.8 2.9 %collective-permute-done.17 = f32[32,512]{1,0:T(8,128)S(1)} collective-permute-done((f32[32,512]{1,0:T(8,128)S(1)}, f32[32,512]{1,0:T(8,128)S(1)}, u32[]{:S(2)}, u32[]{:S(2)}) %collective-permute-start.17) | collective-permute-done | bytes 65568 | tf_op jit(solution)/shard_map/ppermute | solution.py:65
  197.8 1.9 collective-permute-start.18
  199.7 3.6 %collective-permute-done.18 = f32[32,512]{1,0:T(8,128)S(1)} collective-permute-done((f32[32,512]{1,0:T(8,128)S(1)}, f32[32,512]{1,0:T(8,128)S(1)}, u32[]{:S(2)}, u32[]{:S(2)}) %collective-permute-start.18) | collective-permute-done | bytes 65568 | tf_op jit(solution)/shard_map/ppermute | solution.py:88
  203.3 2.4 collective-permute-start.19
  205.7 6.5 %collective-permute-done.19 = f32[64,512]{1,0:T(8,128)S(1)} collective-permute-done((f32[64,512]{1,0:T(8,128)S(1)}, f32[64,512]{1,0:T(8,128)S(1)}, u32[]{:S(2)}, u32[]{:S(2)}) %collective-permute-start.19) | collective-permute-done | bytes 131104 | tf_op jit(solution)/shard_map/ppermute | solution.py:88
  212.2 0.7 fusion.7
  212.9 36.9 %all-gather.5.cloned.1.call-done = bf16[49152,128]{1,0:T(8,128)(2,1)} async-done(((bf16[3072,128]{1,0:T(8,128)(2,1)}), bf16[49152,128]{1,0:T(8,128)(2,1)}) %all-gather.5.cloned.1.call-update) | async-done | bytes 12582928 | tf_op jit(solution)/shard_map/all_gather | solution.py:156
  249.8 15.1 %shard_map.86 = bf16[12,128,128]{2,1,0:T(8,128)(2,1)} custom-call(s32[672]{0:T(1024)S(1)} %get-tuple-element.3.pos_ref, bf16[12,56,128,128]{3,2,1,0:T(8,128)(2,1)} %a_ref.3, bf16[384,128,128]{2,1,0:T(8,128)(2,1)} %bitcast.56), custom_call_target="tpu_custom_call" | custom-call | flops 2818572288 | bytes 34996224 | tf_op jit(solution)/shard_map/pallas_call | solution.py:38
  (31 shorter events, 0.4 us)
Async XLA Ops:
  7.2 15.9 %copy-start = (bf16[512,512]{1,0:T(8,128)(2,1)S(1)}, bf16[512,512]{1,0:T(8,128)(2,1)}, u32[]{:S(2)}) copy-start(bf16[512,512]{1,0:T(8,128)(2,1)} %param.7) | copy-start | bytes 1572868
  7.2 107.8 %all-gather.3.cloned.1.call-start = ((), (), s32[]{:S(2)}) async-start(), calls=%async_computation | async-start | bytes 13369344 | tf_op jit(solution)/shard_map/all_gather | solution.py:116
  7.2 12.3 %collective-permute-start = (bf16[1536,128]{1,0:T(8,128)(2,1)}, bf16[1536,128]{1,0:T(8,128)(2,1)S(1)}, u32[]{:S(2)}, u32[]{:S(2)}) collective-permute-start(bf16[1536,128]{1,0:T(8,128)(2,1)} %param.6), channel_id=1, source_target_pairs={{0,16},{16,0},{1,17},{17,1},{2,18},{18,2},{3,19},{19,3},{4,20},{20... | collective-permute-start | bytes 1179656 | tf_op jit(solution)/shard_map/ppermute | solution.py:114
  21.5 228.3 %all-gather.5.cloned.1.call-start = ((), (), s32[]{:S(2)}) async-start(), calls=%async_computation.1 | async-start | bytes 13369344 | tf_op jit(solution)/shard_map/all_gather | solution.py:156
  115.0 22.1 %copy-start.2 = (bf16[384,512]{1,0:T(8,128)(2,1)S(1)}, bf16[384,512]{1,0:T(8,128)(2,1)}, u32[]{:S(2)}) copy-start(bf16[384,512]{1,0:T(8,128)(2,1)} %param.8) | copy-start | bytes 1179652
  129.5 2.7 collective-permute-start.1
  130.4 4.3 %collective-permute-start.2 = (bf16[384,128]{1,0:T(8,128)(2,1)S(1)}, bf16[384,128]{1,0:T(8,128)(2,1)S(1)}, u32[]{:S(2)}, u32[]{:S(2)}) collective-permute-start(bf16[384,128]{1,0:T(8,128)(2,1)S(1)} %get-tuple-element.13), channel_id=1, source_target_pairs={{0,2},{1,3},{2,0},{3,1},{4,6},{5,7},{6,4},{7,5},{8,10},{9,11},{10,... | collective-permute-start | bytes 294920 | tf_op jit(solution)/shard_map/ppermute | solution.py:107
  131.6 5.4 %collective-permute-start.3 = (bf16[384,128]{1,0:T(8,128)(2,1)S(1)}, bf16[384,128]{1,0:T(8,128)(2,1)S(1)}, u32[]{:S(2)}, u32[]{:S(2)}) collective-permute-start(bf16[384,128]{1,0:T(8,128)(2,1)S(1)} %get-tuple-element.12), channel_id=1, source_target_pairs={{0,3},{1,2},{2,1},{3,0},{4,7},{5,6},{6,5},{7,4},{8,11},{9,10},{10,... | collective-permute-start | bytes 294920 | tf_op jit(solution)/shard_map/ppermute | solution.py:107
  139.0 5.5 %collective-permute-start.4 = (bf16[384,128]{1,0:T(8,128)(2,1)S(1)}, bf16[384,128]{1,0:T(8,128)(2,1)S(1)}, u32[]{:S(2)}, u32[]{:S(2)}) collective-permute-start(bf16[384,128]{1,0:T(8,128)(2,1)S(1)} %get-tuple-element.10), channel_id=1, source_target_pairs={{0,1},{1,0},{2,3},{3,2},{4,5},{5,4},{6,7},{7,6},{8,9},{9,8},{10,11... | collective-permute-start | bytes 294920 | tf_op jit(solution)/shard_map/ppermute | solution.py:107
  139.2 13.4 %collective-permute-start.8 = (bf16[384,128]{1,0:T(8,128)(2,1)S(1)}, bf16[384,128]{1,0:T(8,128)(2,1)S(1)}, u32[]{:S(2)}, u32[]{:S(2)}) collective-permute-start(bf16[384,128]{1,0:T(8,128)(2,1)S(1)} %get-tuple-element.10), channel_id=1, source_target_pairs={{0,17},{1,16},{2,19},{3,18},{16,1},{17,0},{18,3},{19,2},{4,21},{5,... | collective-permute-start | bytes 294920 | tf_op jit(solution)/shard_map/ppermute | solution.py:105
  142.1 5.4 %collective-permute-start.5 = (bf16[384,128]{1,0:T(8,128)(2,1)S(1)}, bf16[384,128]{1,0:T(8,128)(2,1)S(1)}, u32[]{:S(2)}, u32[]{:S(2)}) collective-permute-start(bf16[384,128]{1,0:T(8,128)(2,1)S(1)} %get-tuple-element.9), channel_id=1, source_target_pairs={{0,2},{1,3},{2,0},{3,1},{4,6},{5,7},{6,4},{7,5},{8,10},{9,11},{10,... | collective-permute-start | bytes 294920 | tf_op jit(solution)/shard_map/ppermute | solution.py:107
  142.4 10.2 %collective-permute-start.9 = (bf16[384,128]{1,0:T(8,128)(2,1)S(1)}, bf16[384,128]{1,0:T(8,128)(2,1)S(1)}, u32[]{:S(2)}, u32[]{:S(2)}) collective-permute-start(bf16[384,128]{1,0:T(8,128)(2,1)S(1)} %get-tuple-element.9), channel_id=1, source_target_pairs={{0,18},{1,19},{2,16},{3,17},{16,2},{17,3},{18,0},{19,1},{4,22},{5,... | collective-permute-start | bytes 294920 | tf_op jit(solution)/shard_map/ppermute | solution.py:105
  143.0 6.9 %collective-permute-start.6 = (bf16[384,128]{1,0:T(8,128)(2,1)S(1)}, bf16[384,128]{1,0:T(8,128)(2,1)S(1)}, u32[]{:S(2)}, u32[]{:S(2)}) collective-permute-start(bf16[384,128]{1,0:T(8,128)(2,1)S(1)} %get-tuple-element.8), channel_id=1, source_target_pairs={{0,3},{1,2},{2,1},{3,0},{4,7},{5,6},{6,5},{7,4},{8,11},{9,10},{10,... | collective-permute-start | bytes 294920 | tf_op jit(solution)/shard_map/ppermute | solution.py:107
  144.5 8.2 %collective-permute-start.10 = (bf16[384,128]{1,0:T(8,128)(2,1)S(1)}, bf16[384,128]{1,0:T(8,128)(2,1)S(1)}, u32[]{:S(2)}, u32[]{:S(2)}) collective-permute-start(bf16[384,128]{1,0:T(8,128)(2,1)S(1)} %get-tuple-element.8), channel_id=1, source_target_pairs={{0,19},{1,18},{2,17},{3,16},{16,3},{17,2},{18,1},{19,0},{4,23},{5,... | collective-permute-start | bytes 294920 | tf_op jit(solution)/shard_map/ppermute | solution.py:105
  147.6 5.0 %collective-permute-start.7 = (bf16[384,128]{1,0:T(8,128)(2,1)S(1)}, bf16[384,128]{1,0:T(8,128)(2,1)S(1)}, u32[]{:S(2)}, u32[]{:S(2)}) collective-permute-start(bf16[384,128]{1,0:T(8,128)(2,1)S(1)} %get-tuple-element.7), channel_id=1, source_target_pairs={{0,16},{1,17},{2,18},{3,19},{16,0},{17,1},{18,2},{19,3},{4,20},{5,... | collective-permute-start | bytes 294920 | tf_op jit(solution)/shard_map/ppermute | solution.py:105
  152.7 0.9 copy-start.1
  155.0 11.4 %collective-permute-start.11 = (f32[2,128,512]{2,1,0:T(8,128)S(1)}, f32[2,128,512]{2,1,0:T(8,128)S(1)}, u32[]{:S(2)}, u32[]{:S(2)}) collective-permute-start(f32[2,128,512]{2,1,0:T(8,128)S(1)} %slice_select_fusion), channel_id=1, source_target_pairs={{0,2},{1,3},{2,0},{3,1},{4,6},{5,7},{6,4},{7,5},{8,10},{9,11},{10,... | collective-permute-start | bytes 1572872 | tf_op jit(solution)/shard_map/ppermute | solution.py:79
  166.6 4.3 %collective-permute-start.12 = (f32[1,128,512]{2,1,0:T(8,128)S(1)}, f32[1,128,512]{2,1,0:T(8,128)S(1)}, u32[]{:S(2)}, u32[]{:S(2)}) collective-permute-start(f32[1,128,512]{2,1,0:T(8,128)S(1)} %slice_select_fusion.1), channel_id=1, source_target_pairs={{0,1},{1,0},{2,3},{3,2},{4,5},{5,4},{6,7},{7,6},{8,9},{9,8},{10,11... | collective-permute-start | bytes 786440 | tf_op jit(solution)/shard_map/ppermute | solution.py:79
  170.9 9.4 %collective-permute-start.13 = (f32[2,32,512]{2,1,0:T(8,128)S(1)}, f32[2,32,512]{2,1,0:T(8,128)S(1)}, u32[]{:S(2)}, u32[]{:S(2)}) collective-permute-start(f32[2,32,512]{2,1,0:T(8,128)S(1)} %bitcast.61), channel_id=1, source_target_pairs={{0,8},{4,12},{8,0},{12,4},{1,9},{5,13},{9,1},{13,5},{2,10},{6,14},... | collective-permute-start | bytes 393224 | tf_op jit(solution)/shard_map/ppermute | solution.py:79
  180.3 3.6 %collective-permute-start.14 = (f32[1,32,512]{2,1,0:T(8,128)S(1)}, f32[1,32,512]{2,1,0:T(8,128)S(1)}, u32[]{:S(2)}, u32[]{:S(2)}) collective-permute-start(f32[1,32,512]{2,1,0:T(8,128)S(1)} %slice_select_fusion.4), channel_id=1, source_target_pairs={{0,4},{4,0},{8,12},{12,8},{1,5},{5,1},{9,13},{13,9},{2,6},{6,2},{1... | collective-permute-start | bytes 196616 | tf_op jit(solution)/shard_map/ppermute | solution.py:79
  184.0 4.7 %collective-permute-start.15 = (f32[32,512]{1,0:T(8,128)S(1)}, f32[32,512]{1,0:T(8,128)S(1)}, u32[]{:S(2)}, u32[]{:S(2)}) collective-permute-start(f32[32,512]{1,0:T(8,128)S(1)} %add_bitcast_fusion), channel_id=1, source_target_pairs={{0,16},{16,0},{32,48},{48,32},{64,80},{80,64},{96,112},{112,96},{1... | collective-permute-start | bytes 196616 | tf_op jit(solution)/shard_map/ppermute | solution.py:65
  188.7 3.2 %collective-permute-start.16 = (f32[32,512]{1,0:T(8,128)S(1)}, f32[32,512]{1,0:T(8,128)S(1)}, u32[]{:S(2)}, u32[]{:S(2)}) collective-permute-start(f32[32,512]{1,0:T(8,128)S(1)} %add.161), channel_id=1, source_target_pairs={{0,32},{16,48},{32,0},{48,16},{64,96},{80,112},{96,64},{112,80},{1... | collective-permute-start | bytes 196616 | tf_op jit(solution)/shard_map/ppermute | solution.py:65
  191.9 5.9 %collective-permute-start.17 = (f32[32,512]{1,0:T(8,128)S(1)}, f32[32,512]{1,0:T(8,128)S(1)}, u32[]{:S(2)}, u32[]{:S(2)}) collective-permute-start(f32[32,512]{1,0:T(8,128)S(1)} %add.162), channel_id=1, source_target_pairs={{0,64},{16,80},{32,96},{48,112},{64,0},{80,16},{96,32},{112,48},{1... | collective-permute-start | bytes 196616 | tf_op jit(solution)/shard_map/ppermute | solution.py:65
  197.8 5.5 %collective-permute-start.18 = (f32[32,512]{1,0:T(8,128)S(1)}, f32[32,512]{1,0:T(8,128)S(1)}, u32[]{:S(2)}, u32[]{:S(2)}) collective-permute-start(f32[32,512]{1,0:T(8,128)S(1)} %add.163), channel_id=1, source_target_pairs={{0,4},{4,0},{8,12},{12,8},{1,5},{5,1},{9,13},{13,9},{2,6},{6,2},{1... | collective-permute-start | bytes 196616 | tf_op jit(solution)/shard_map/ppermute | solution.py:88
  203.3 8.9 %collective-permute-start.19 = (f32[64,512]{1,0:T(8,128)S(1)}, f32[64,512]{1,0:T(8,128)S(1)}, u32[]{:S(2)}, u32[]{:S(2)}) collective-permute-start(f32[64,512]{1,0:T(8,128)S(1)} %maximum_select_fusion.1), channel_id=1, source_target_pairs={{0,8},{4,12},{8,0},{12,4},{1,9},{5,13},{9,1},{13,5},{2,10},{6,14},... | collective-permute-start | bytes 393224 | tf_op jit(solution)/shard_map/ppermute | solution.py:88
Sparse Core Ops, SparseCore 0:
  21.6 93.3 all-gather.2
  153.7 96.0 all-gather.4
